TPU v7x, 128 devices: a whole 4x4x4 slice. The times are simulated.
128 devices in a mesh: ctx: 8 (over x, y_hi), head: 16 (over y_lo, z, core).
Axes of the slice: x: 4, y: 4 (y_hi: 2, y_lo: 2; y = y_hi * 2 + y_lo), z: 4, core: 2. Of those that a mesh axis runs over, the one named last changes fastest.
Arguments:
- hidden_in: bfloat16 [8192, 5376], P(('ctx', 'head')), may hold values from -6 to 6
- pre_gain: float32 [5376], replicated, may hold values from 0.1 to 1.9
- w_query: bfloat16 [5376, 4096], P('ctx', 'head'), may hold values from -0.054554473 to 0.054554473, as said below
- w_key: bfloat16 [5376, 2048], P('ctx', 'head'), may hold values from -0.054554473 to 0.054554473, as said below
- value_weight: bfloat16 [5376, 2048], P('ctx', 'head'), may hold values from -0.078125 to 0.078125
- query_gain: float32 [128], replicated, may hold values from 0.6 to 7, as said below
- key_norm_gain: float32 [128], replicated, may hold values from 0.6 to 7, as said below
- w_output: bfloat16 [4096, 5376], P(('head', 'ctx')), may hold values from -0.09375 to 0.09375
- post_gain: float32 [5376], replicated, may hold values from 0.1 to 1.9
Outputs:
- layer_out: bfloat16 [8192, 5376], P(('ctx', 'head'))
Inputs may be any that keep to these rules, and one draw needn't show every extreme that they name: `w_query`: entries are normal draws clipped to 4 standard deviations, scaled by 5376 ** -0.5. `w_key`: entries are normal draws clipped to 4 standard deviations, scaled by 5376 ** -0.5. `query_gain`: positive gains. `key_norm_gain`: positive gains.
All inputs are finite; a program needn't handle non-finite values.
Results may differ from a plain program's by a relative error of at most 0.015.
The roundings to bfloat16 on the way count: a program that leaves them out, or rounds other values in their place, can miss the bound.
Values may be sent and summed in bfloat16 or wider, within the bound.
No kernel may reach another device: no remote copies, remote signals or barrier semaphores. Data moves between devices by JAX's collectives and lax.ppermute only.
A program may use at most 64 MiB of HBM per device.

v0:
```python
import jax
import jax.numpy as jnp
from jax import lax
from jax.sharding import PartitionSpec as P

HEAD_SIZE = 128
WINDOW_SPAN = 1024


norm_eps = 1e-06
query_scale = 168.0 ** (-0.5)
rope_base = 10000.0
mask_value = -1e30


def passed_along(shard, axis, by):
    count = lax.axis_size(axis)
    pairs = [(i, i + by) for i in range(count) if 0 <= i + by < count]
    return lax.ppermute(shard, axis, pairs)


def root_mean_scale(values, scaling):
    mean_sq = jnp.mean(values * values, axis=-1, keepdims=True)
    return values * lax.rsqrt(mean_sq + norm_eps) * scaling


def apply_rotary(values, token_places):
    full_width = values.shape[-1]
    half_width = full_width // 2
    frequency = rope_base ** (-jnp.arange(half_width, dtype=jnp.float32) * 2.0 / full_width)
    angles = token_places.astype(jnp.float32)[:, None] * frequency[None, :]
    cosine = jnp.cos(angles)[:, None, :]
    sine_part = jnp.sin(angles)[:, None, :]
    lower_half = values[..., :half_width]
    upper_half = values[..., half_width:]
    return jnp.concatenate(
        [
            lower_half * cosine - upper_half * sine_part,
            upper_half * cosine + lower_half * sine_part,
        ],
        axis=-1,
    )


def body(
    hidden_in,
    pre_gain,
    w_query,
    w_key,
    value_weight,
    query_gain,
    key_norm_gain,
    w_output,
    post_gain,
):
    own_rows = hidden_in.astype(jnp.float32)
    raw_rows = lax.all_gather(hidden_in, "head", axis=0, tiled=True)
    normed = root_mean_scale(raw_rows.astype(jnp.float32), pre_gain).astype(jnp.bfloat16)
    tok_count = normed.shape[0]

    def add_rows(weight_piece):
        return jnp.dot(normed, weight_piece, preferred_element_type=jnp.float32)

    query_raw = add_rows(lax.all_gather(w_query, "ctx", axis=0, tiled=True))
    key_unnormed = add_rows(lax.all_gather(w_key, "ctx", axis=0, tiled=True))
    value_unnormed = add_rows(lax.all_gather(value_weight, "ctx", axis=0, tiled=True))
    local_heads = w_query.shape[1] // HEAD_SIZE
    local_groups = w_key.shape[1] // HEAD_SIZE
    heads_per_group = local_heads // local_groups
    ctx_index = lax.axis_index("ctx")
    token_places = ctx_index * tok_count + jnp.arange(tok_count, dtype=jnp.int32)
    query_matrix = (
        apply_rotary(
            root_mean_scale(query_raw.reshape(tok_count, local_heads, HEAD_SIZE), query_gain),
            token_places,
        )
        * query_scale
    ).astype(jnp.bfloat16)
    projected_keys = apply_rotary(
        root_mean_scale(key_unnormed.reshape(tok_count, local_groups, HEAD_SIZE), key_norm_gain),
        token_places,
    ).astype(jnp.bfloat16)
    projected_values = value_unnormed.astype(jnp.bfloat16)
    key_value = jnp.stack(
        [projected_keys.reshape(tok_count, local_groups * HEAD_SIZE), projected_values]
    )
    pieces = [passed_along(key_value, "ctx", 1)]
    extended = jnp.concatenate(pieces + [key_value], axis=1)
    band_keys = extended[0].reshape(-1, local_groups, HEAD_SIZE)
    band_values = extended[1].reshape(-1, local_groups, HEAD_SIZE)
    block_rows = min(512, tok_count)
    grouped_queries = query_matrix.reshape(tok_count, local_groups, heads_per_group, HEAD_SIZE)
    outputs = []
    for block_index in range(tok_count // block_rows):
        first_row = block_index * block_rows
        query_block = grouped_queries[first_row : first_row + block_rows]
        key_block = band_keys[first_row : first_row + block_rows + WINDOW_SPAN]
        value_block = band_values[first_row : first_row + block_rows + WINDOW_SPAN]
        scores = jnp.einsum(
            "qjgd,kjd->jgqk", query_block, key_block, preferred_element_type=jnp.float32
        )
        query_spots = token_places[first_row : first_row + block_rows]
        key_spots = (
            ctx_index * tok_count
            - WINDOW_SPAN
            + first_row
            + jnp.arange(block_rows + WINDOW_SPAN, dtype=jnp.int32)
        )
        allowed = (
            (key_spots[None, :] <= query_spots[:, None])
            & (key_spots[None, :] > query_spots[:, None] - WINDOW_SPAN)
            & (key_spots[None, :] >= 0)
        )
        scores = jnp.where(allowed, scores, mask_value)
        row_max = jnp.max(scores, axis=-1, keepdims=True)
        weights = jnp.exp(scores - row_max)
        row_sum = jnp.sum(weights, axis=-1, keepdims=True)
        probabilities = (weights / row_sum).astype(jnp.bfloat16)
        mixed = jnp.einsum(
            "jgqk,kjd->qjgd", probabilities, value_block, preferred_element_type=jnp.float32
        )
        outputs.append(mixed.astype(jnp.bfloat16).reshape(block_rows, local_heads * HEAD_SIZE))
    attended = jnp.concatenate(outputs, axis=0)
    out_weight = lax.all_gather(w_output, "ctx", axis=0, tiled=True)
    partial_value = jnp.dot(attended, out_weight, preferred_element_type=jnp.float32).astype(
        jnp.bfloat16
    )
    summed = lax.psum_scatter(
        lax.optimization_barrier(partial_value).astype(jnp.float32).astype(jnp.bfloat16),
        "head",
        scatter_dimension=0,
        tiled=True,
    ).astype(jnp.float32)
    result = own_rows + root_mean_scale(summed, post_gain)
    return result.astype(jnp.bfloat16)


def solution(mesh):
    return jax.shard_map(
        body,
        mesh=mesh,
        in_specs=(
            P(("ctx", "head"), None),
            P(),
            P("ctx", "head"),
            P("ctx", "head"),
            P("ctx", "head"),
            P(),
            P(),
            P(("head", "ctx"), None),
            P(),
        ),
        out_specs=P(("ctx", "head"), None),
        check_vma=False,
    )
```

profile of v0, /device:TPU:0, one launch (start us, length us, event | category | flops | bytes accessed | tf_op | source)
XLA Modules:
  0.0 400.9 jit_solution(7037838070945432475)
XLA Ops:
  6.5 0.0 all-gather.6.cloned.1.call-start
  6.5 0.7 all-gather.6.cloned.1.call-update
  7.3 0.0 all-gather.8.cloned.1.call-start
  7.3 0.7 all-gather.8.cloned.1.call-update
  8.0 0.0 all-gather.10.cloned.1.call-start
  8.1 0.7 all-gather.10.cloned.1.call-update
  8.7 0.0 all-gather.12.cloned.1.call-start
  8.8 0.5 all-gather.12.cloned.1.call-update
  9.3 0.0 all-gather.14.cloned.1.call-start
  9.4 0.5 all-gather.14.cloned.1.call-update
  9.9 0.0 reduce-scatter.2.cloned.1.call-start
  10.1 3.0 multiply_cosine_fusion
  13.1 0.0 copy-start.6
  13.1 1.8 and_and_fusion.1
  15.0 1.9 and_and_fusion
  16.8 59.2 %all-gather.6.cloned.1.call-done = bf16[1024,5376]{1,0:T(8,128)(2,1)} async-done(((bf16[64,5376]{1,0:T(8,128)(2,1)}), bf16[1024,5376]{1,0:T(8,128)(2,1)}) %all-gather.6.cloned.1.call-update) | async-done | bytes 11010064 | tf_op jit(solution)/shard_map/all_gather | solution.py:57
  76.0 0.0 copy-start
  76.0 6.5 %fusion = f32[1024]{0:T(1024)S(1)} fusion(bf16[1024,5376]{1,0:T(8,128)(2,1)} %all-gather.6.cloned.1.call-done), kind=kLoop, calls=%fused_computation.2 | loop fusion | flops 16514048 | bytes 11014144 | tf_op jit(solution)/shard_map/reduce_sum | solution.py:23
  82.5 0.0 copy-done.6
  82.5 0.8 copy-done
  83.3 6.0 %fusion.2 = bf16[1024,5376]{1,0:T(8,128)(2,1)} fusion(bf16[1024,5376]{1,0:T(8,128)(2,1)S(1)} %copy-done, f32[5376]{0:T(1024)S(1)} %copy-done.6, f32[1024]{0:T(1024)S(1)} %add_rsqrt_fusion.2), kind=kLoop, calls=%fused_computation.4 | loop fusion | flops 22020096 | bytes 22045696 | tf_op jit(solution)/shard_map/convert_element_type | solution.py:58
  89.2 0.0 copy-start.8
  89.2 39.5 %all-gather.8.cloned.1.call-done = bf16[5376,128]{1,0:T(8,128)(2,1)} async-done(((bf16[672,128]{1,0:T(8,128)(2,1)}), bf16[5376,128]{1,0:T(8,128)(2,1)}) %all-gather.8.cloned.1.call-update) | async-done | bytes 1376272 | tf_op jit(solution)/shard_map/all_gather | solution.py:65
  128.7 8.2 %multiply_reduce_fusion.1 = (f32[1024]{0:T(1024)S(1)}, f32[1024,128]{0,1:T(8,128)S(1)}) fusion(bf16[1024,5376]{1,0:T(8,128)(2,1)} %fusion.2, bf16[5376,128]{1,0:T(8,128)(2,1)} %all-gather.8.cloned.1.call-done), kind=kOutput, calls=%fused_computation.46 | convolution fusion | flops 1409547264 | bytes 12914688 | tf_op jit(solution)/shard_map/dot_general | solution.py:62
  137.0 0.0 copy-done.8
  137.0 0.1 multiply_bitcast_fusion
  137.1 1.2 fusion.39
  138.2 41.1 %all-gather.10.cloned.1.call-done = bf16[5376,128]{1,0:T(8,128)(2,1)} async-done(((bf16[672,128]{1,0:T(8,128)(2,1)}), bf16[5376,128]{1,0:T(8,128)(2,1)}) %all-gather.10.cloned.1.call-update) | async-done | bytes 1376272 | tf_op jit(solution)/shard_map/all_gather | solution.py:66
  179.3 8.2 %fusion.21 = bf16[1,1024,128]{1,2,0:T(8,128)(2,1)S(1)} fusion(bf16[1024,5376]{1,0:T(8,128)(2,1)} %fusion.2, bf16[5376,128]{1,0:T(8,128)(2,1)} %all-gather.10.cloned.1.call-done), kind=kOutput, calls=%fused_computation.31 | convolution fusion | flops 1409417216 | bytes 12648448 | tf_op jit(solution)/shard_map/dot_general | solution.py:62
  187.6 0.0 copy-start.9
  187.6 0.0 copy-start.4
  187.6 0.0 copy-start.5
  187.6 3.4 collective-permute-start
  191.0 52.1 %all-gather.12.cloned.1.call-done = bf16[5376,256]{1,0:T(8,128)(2,1)} async-done(((bf16[672,256]{1,0:T(8,128)(2,1)}), bf16[5376,256]{1,0:T(8,128)(2,1)}) %all-gather.12.cloned.1.call-update) | async-done | bytes 2752528 | tf_op jit(solution)/shard_map/all_gather | solution.py:64
  243.1 9.0 %multiply_reduce_fusion = (f32[1024,2]{0,1:T(2,128)S(1)}, f32[1024,256]{0,1:T(8,128)}) fusion(bf16[1024,5376]{1,0:T(8,128)(2,1)} %fusion.2, bf16[5376,256]{1,0:T(8,128)(2,1)} %all-gather.12.cloned.1.call-done), kind=kOutput, calls=%fused_computation.38 | convolution fusion | flops 2819094528 | bytes 14819328 | tf_op jit(solution)/shard_map/dot_general | solution.py:62
  252.1 1.6 copy.11
  253.7 0.0 copy-start.1
  253.7 0.0 copy-done.9
  253.7 0.3 multiply_multiply_fusion
  254.1 0.0 copy-done.4
  254.1 0.0 copy-done.5
  254.1 0.5 multiply_subtract_fusion
  254.6 0.0 copy-start.2
  254.6 0.3 fusion.22
  255.0 0.0 collective-permute-done
  255.0 1.1 maximum_maximum_fusion
  256.1 0.0 copy-done.1
  256.1 1.3 fusion.3
  257.4 0.0 copy-done.2
  257.4 1.3 fusion.4
  258.7 1.2 fusion.5
  260.0 1.2 fusion.6
  261.2 2.0 fusion.15
  263.2 2.2 fusion.18
  265.4 38.4 %all-gather.14.cloned.1.call-done = bf16[256,5376]{1,0:T(8,128)(2,1)} async-done(((bf16[32,5376]{1,0:T(8,128)(2,1)}), bf16[256,5376]{1,0:T(8,128)(2,1)}) %all-gather.14.cloned.1.call-update) | async-done | bytes 2752528 | tf_op jit(solution)/shard_map/all_gather | solution.py:124
  303.9 7.6 %convolution_convert_fusion = bf16[1024,5376]{1,0:T(8,128)(2,1)} fusion(bf16[256,5376]{1,0:T(8,128)(2,1)} %all-gather.14.cloned.1.call-done, bf16[512,256]{0,1:T(8,128)(2,1)S(1)} %bitcast.95, bf16[512,256]{0,1:T(8,128)(2,1)S(1)} %bitcast.94), kind=kOutput, calls=%fused_computation.5 | convolution fusion | flops 2825125888 | bytes 14286848 | tf_op jit(solution)/shard_map/dot_general | solution.py:125
  311.5 0.0 copy-start.3
  311.5 0.0 copy-start.7
  311.5 0.0 reduce-scatter.2.cloned.1.call-update
  311.5 78.9 %reduce-scatter.2.cloned.1.call-done = bf16[64,5376]{1,0:T(8,128)(2,1)} async-done(((bf16[1024,5376]{1,0:T(8,128)(2,1)}), bf16[64,5376]{1,0:T(8,128)(2,1)}) %reduce-scatter.2.cloned.1.call-update) | async-done | bytes 688144 | tf_op jit(solution)/shard_map/reduce_scatter | solution.py:128
  390.4 1.3 fusion.11
  391.8 0.0 copy-done.3
  391.8 0.0 copy-done.7
  391.8 2.3 fusion.14
  (12 shorter events, 0.1 us)
Async XLA Ops:
  6.5 69.5 %all-gather.6.cloned.1.call-start = ((), (), s32[]{:S(2)}) async-start(), calls=%async_computation.1 | async-start | bytes 11698176 | tf_op jit(solution)/shard_map/all_gather | solution.py:57
  7.3 121.5 %all-gather.8.cloned.1.call-start = ((), (), s32[]{:S(2)}) async-start(), calls=%async_computation.2 | async-start | bytes 1548288 | tf_op jit(solution)/shard_map/all_gather | solution.py:65
  8.0 171.3 %all-gather.10.cloned.1.call-start = ((), (), s32[]{:S(2)}) async-start(), calls=%async_computation.3 | async-start | bytes 1548288 | tf_op jit(solution)/shard_map/all_gather | solution.py:66
  8.7 234.4 %all-gather.12.cloned.1.call-start = ((), (), s32[]{:S(2)}) async-start(), calls=%async_computation.4 | async-start | bytes 3096576 | tf_op jit(solution)/shard_map/all_gather | solution.py:64
  9.3 294.5 %all-gather.14.cloned.1.call-start = ((), (), s32[]{:S(2)}) async-start(), calls=%async_computation.5 | async-start | bytes 3096576 | tf_op jit(solution)/shard_map/all_gather | solution.py:124
  9.9 380.5 %reduce-scatter.2.cloned.1.call-start = ((), (), s32[]{:S(2)}) async-start(), calls=%async_computation.6 | async-start | bytes 11698176 | tf_op jit(solution)/shard_map/reduce_scatter | solution.py:128
  13.1 69.4 %copy-start.6 = (f32[5376]{0:T(1024)S(1)}, f32[5376]{0:T(1024)}, u32[]{:S(2)}) copy-start(f32[5376]{0:T(1024)} %param.10) | copy-start | bytes 64516
  76.0 7.3 %copy-start = (bf16[1024,5376]{1,0:T(8,128)(2,1)S(1)}, bf16[1024,5376]{1,0:T(8,128)(2,1)}, u32[]{:S(2)}) copy-start(bf16[1024,5376]{1,0:T(8,128)(2,1)} %all-gather.6.cloned.1.call-done) | copy-start | bytes 33030148
  89.2 47.7 %copy-start.8 = (f32[128]{0:T(128)S(1)}, f32[128]{0:T(128)}, u32[]{:S(2)}) copy-start(f32[128]{0:T(128)} %param.15) | copy-start | bytes 1540
  187.6 66.1 %copy-start.9 = (f32[128]{0:T(128)S(1)}, f32[128]{0:T(128)}, u32[]{:S(2)}) copy-start(f32[128]{0:T(128)} %param.14) | copy-start | bytes 1540
  187.6 66.5 %copy-start.4 = (f32[1024,64]{1,0:T(8,128)S(1)}, f32[1024,64]{1,0:T(8,128)}, u32[]{:S(2)}) copy-start(f32[1024,64]{1,0:T(8,128)} %get-tuple-element.9) | copy-start | bytes 786436
  187.6 66.5 %copy-start.5 = (f32[1024,64]{1,0:T(8,128)S(1)}, f32[1024,64]{1,0:T(8,128)}, u32[]{:S(2)}) copy-start(f32[1024,64]{1,0:T(8,128)} %get-tuple-element.10) | copy-start | bytes 786436
  187.6 67.4 %collective-permute-start = (bf16[2,1024,128]{1,2,0:T(8,128)(2,1)S(1)}, bf16[2,1024,128]{1,2,0:T(8,128)(2,1)}, u32[]{:S(2)}, u32[]{:S(2)}) collective-permute-start(bf16[2,1024,128]{1,2,0:T(8,128)(2,1)S(1)} %pad_maximum_fusion), channel_id=1, source_target_pairs={{0,16},{16,32},{32,48},{48,64},{64,80},{80,96},{96,112},{1,17},{17... | collective-permute-start | bytes 1572872 | tf_op jit(solution)/shard_map/ppermute | solution.py:19
  253.7 2.4 copy-start.1
  254.6 2.8 copy-start.2
  311.5 80.3 %copy-start.3 = (bf16[64,5376]{1,0:T(8,128)(2,1)S(1)}, bf16[64,5376]{1,0:T(8,128)(2,1)}, u32[]{:S(2)}) copy-start(bf16[64,5376]{1,0:T(8,128)(2,1)} %param.9) | copy-start | bytes 2064388
  311.5 80.3 %copy-start.7 = (f32[5376]{0:T(1024)S(1)}, f32[5376]{0:T(1024)}, u32[]{:S(2)}) copy-start(f32[5376]{0:T(1024)} %param.17) | copy-start | bytes 64516
Sparse Core Ops, SparseCore 0:
  9.0 66.9 all-gather.5
  78.3 50.3 all-gather.7
  131.0 48.2 all-gather.9
  181.5 61.6 all-gather.11
  245.3 58.5 all-gather.13
  311.7 78.7 reduce-scatter.1
where the time goes:
time: 401 us
  waiting for transfers between devices  312 us (78%)
  matrix products  39.9 us (10%)
  other arithmetic  28.9 us (7%)
  between operations  13.8 us (3%)
    reduce_scatter x1, waiting for transfers between devices, body(): lax.psum_scatter(lax.optimization_barrier(partial_value).astype(jnp.float...  78.9 us
    all_gather x1, waiting for transfers between devices, body(): raw_rows = lax.all_gather(hidden_in, 'head', axis=0, tiled=True)  59.2 us
    all_gather x1, waiting for transfers between devices, body(): query_raw = add_rows(lax.all_gather(w_query, 'ctx', axis=0, tiled=True))  52.1 us
    all_gather x1, waiting for transfers between devices, body(): lax.all_gather(value_weight, 'ctx', axis=0, tiled=True)  41.1 us
    all_gather x1, waiting for transfers between devices, body(): key_unnormed = add_rows(lax.all_gather(w_key, 'ctx', axis=0, tiled=True))  39.5 us
    all_gather x1, waiting for transfers between devices, body(): out_weight = lax.all_gather(w_output, 'ctx', axis=0, tiled=True)  38.4 us
    dot_general x3, matrix products, add_rows(): return jnp.dot(normed, weight_piece, preferred_element_type=jnp.float32)  25.4 us
  transfers between devices with their start and end apart: 7, of which 6 were waited for; matrix products, arithmetic and copies ran while one was open for 15% of the time, Pallas kernels for 0%

commit v1 on v0

--- a/solution.py
+++ b/solution.py
@@ -1,7 +1,7 @@
 import jax
 import jax.numpy as jnp
 from jax import lax
-from jax.sharding import PartitionSpec as P
+from jax.sharding import Mesh, PartitionSpec as P
 
 HEAD_SIZE = 128
 WINDOW_SPAN = 1024
@@ -17,6 +17,23 @@
     count = lax.axis_size(axis)
     pairs = [(i, i + by) for i in range(count) if 0 <= i + by < count]
     return lax.ppermute(shard, axis, pairs)
+
+
+def rotated(shard, axis, by):
+    count = lax.axis_size(axis)
+    pairs = [(i, (i + by) % count) for i in range(count)]
+    return lax.ppermute(shard, axis, pairs)
+
+
+def gathered_by_permutes(shard, axis):
+    count = lax.axis_size(axis)
+    me = lax.axis_index(axis)
+    stacked = jnp.zeros((count,) + shard.shape, shard.dtype)
+    stacked = lax.dynamic_update_index_in_dim(stacked, shard, me, 0)
+    for by in range(1, count):
+        piece = rotated(shard, axis, by)
+        stacked = lax.dynamic_update_index_in_dim(stacked, piece, (me - by) % count, 0)
+    return stacked.reshape((count * shard.shape[0],) + shard.shape[1:])
 
 
 def root_mean_scale(values, scaling):
@@ -42,6 +59,15 @@
     )
 
 
+def interleave(mine, other, core, chips, rows):
+    first = jnp.where(core == 0, mine, other)
+    second = jnp.where(core == 0, other, mine)
+    width = mine.shape[-1]
+    return jnp.stack(
+        [first.reshape(chips, rows, width), second.reshape(chips, rows, width)], axis=1
+    ).reshape(chips * 2 * rows, width)
+
+
 def body(
     hidden_in,
     pre_gain,
@@ -53,19 +79,31 @@
     w_output,
     post_gain,
 ):
+    core = lax.axis_index("core")
+    chips = lax.axis_size("hc")
+    rows = hidden_in.shape[0]
     own_rows = hidden_in.astype(jnp.float32)
-    raw_rows = lax.all_gather(hidden_in, "head", axis=0, tiled=True)
-    normed = root_mean_scale(raw_rows.astype(jnp.float32), pre_gain).astype(jnp.bfloat16)
-    tok_count = normed.shape[0]
-
-    def add_rows(weight_piece):
-        return jnp.dot(normed, weight_piece, preferred_element_type=jnp.float32)
-
-    query_raw = add_rows(lax.all_gather(w_query, "ctx", axis=0, tiled=True))
-    key_unnormed = add_rows(lax.all_gather(w_key, "ctx", axis=0, tiled=True))
-    value_unnormed = add_rows(lax.all_gather(value_weight, "ctx", axis=0, tiled=True))
-    local_heads = w_query.shape[1] // HEAD_SIZE
-    local_groups = w_key.shape[1] // HEAD_SIZE
+
+    q_cols = w_query.shape[1]
+    k_cols = w_key.shape[1]
+    w_in = gathered_by_permutes(jnp.concatenate([w_query, w_key, value_weight], axis=1), "ctx")
+    out_weight = gathered_by_permutes(w_output, "ctx")
+
+    mine_rows = lax.all_gather(hidden_in, "hc", axis=0, tiled=True)
+    other_rows = rotated(mine_rows, "core", 1)
+
+    def project(raw):
+        normed = root_mean_scale(raw.astype(jnp.float32), pre_gain).astype(jnp.bfloat16)
+        return jnp.dot(normed, w_in, preferred_element_type=jnp.float32)
+
+    projected = interleave(project(mine_rows), project(other_rows), core, chips, rows)
+    tok_count = projected.shape[0]
+    query_raw = projected[:, :q_cols]
+    key_unnormed = projected[:, q_cols : q_cols + k_cols]
+    value_unnormed = projected[:, q_cols + k_cols :]
+
+    local_heads = q_cols // HEAD_SIZE
+    local_groups = k_cols // HEAD_SIZE
     heads_per_group = local_heads // local_groups
     ctx_index = lax.axis_index("ctx")
     token_places = ctx_index * tok_count + jnp.arange(tok_count, dtype=jnp.int32)
@@ -121,35 +159,47 @@
         )
         outputs.append(mixed.astype(jnp.bfloat16).reshape(block_rows, local_heads * HEAD_SIZE))
     attended = jnp.concatenate(outputs, axis=0)
-    out_weight = lax.all_gather(w_output, "ctx", axis=0, tiled=True)
-    partial_value = jnp.dot(attended, out_weight, preferred_element_type=jnp.float32).astype(
-        jnp.bfloat16
-    )
+
+    by_core = attended.reshape(chips, 2, rows, attended.shape[-1])
+    attended_other = lax.dynamic_index_in_dim(by_core, 1 - core, 1, keepdims=False)
+    attended_mine = lax.dynamic_index_in_dim(by_core, core, 1, keepdims=False)
+
+    def out_project(part):
+        part = part.reshape(chips * rows, part.shape[-1])
+        return jnp.dot(part, out_weight, preferred_element_type=jnp.float32).astype(jnp.bfloat16)
+
+    sent = rotated(out_project(attended_other), "core", 1)
+    pair_sum = (
+        out_project(attended_mine).astype(jnp.float32) + sent.astype(jnp.float32)
+    ).astype(jnp.bfloat16)
     summed = lax.psum_scatter(
-        lax.optimization_barrier(partial_value).astype(jnp.float32).astype(jnp.bfloat16),
-        "head",
-        scatter_dimension=0,
-        tiled=True,
+        pair_sum, "hc", scatter_dimension=0, tiled=True
     ).astype(jnp.float32)
     result = own_rows + root_mean_scale(summed, post_gain)
     return result.astype(jnp.bfloat16)
 
 
 def solution(mesh):
+    ctx_size, head_size = mesh.devices.shape
+    view = Mesh(
+        mesh.devices.reshape(ctx_size, head_size // 2, 2), ("ctx", "hc", "core")
+    )
+    rows_spec = P(("ctx", "hc", "core"), None)
+    cols_spec = P("ctx", ("hc", "core"))
     return jax.shard_map(
         body,
-        mesh=mesh,
+        mesh=view,
         in_specs=(
-            P(("ctx", "head"), None),
-            P(),
-            P("ctx", "head"),
-            P("ctx", "head"),
-            P("ctx", "head"),
-            P(),
-            P(),
-            P(("head", "ctx"), None),
+            rows_spec,
+            P(),
+            cols_spec,
+            cols_spec,
+            cols_spec,
+            P(),
+            P(),
+            P(("hc", "core", "ctx"), None),
             P(),
         ),
-        out_specs=P(("ctx", "head"), None),
+        out_specs=rows_spec,
         check_vma=False,
     )

time: 401 us -> 345 us (0.86)
  waiting for transfers between devices: 312 us -> 207 us
  starting transfers between devices: 3.56 us -> 40.1 us
  local copies, waits for them, and re-layouts: 2.37 us -> 31.2 us
  matrix products: 39.9 us -> 19.2 us
    all_gather x5 -> x1, waiting for transfers between devices: 230 us -> 10.3 us  [body(): mine_rows = lax.all_gather(hidden_in, 'hc', axis=0, tiled=True)]
    ppermute x0 -> x16, waiting for transfers between devices: none -> 130 us  [rotated(): return lax.ppermute(shard, axis, pairs)]
    ppermute x0 -> x16, starting transfers between devices: none -> 33.4 us  [rotated(): return lax.ppermute(shard, axis, pairs)]
    dot_general x4, matrix products: 33.1 us -> 9.32 us  [the longest x2 6.1 us: project(): return jnp.dot(normed, w_in, preferred_element_type=jnp.float32)]
    dynamic_update_slice x0 -> x16, local copies, waits for them, and re-layouts: none -> 15.9 us  [the longest x14 13.8 us: gathered_by_permutes(): lax.dynamic_update_index_in_dim(stacked, piece, (me - by) % count, 0)]
    reduce_scatter x1, waiting for transfers between devices: 78.9 us -> 66.3 us  [body(): lax.psum_scatter(pair_sum, 'hc', scatter_dimension=0, tiled=True)]
  transfers between devices with their start and end apart: 7 -> 19, of which waited for: 6 -> 11; matrix products, arithmetic and copies ran while one was open for 15% -> 12% of each run, Pallas kernels for 0% -> 0%
where the time goes in v1:
time: 345 us; the launch traced here: 343 us
  waiting for transfers between devices  207 us (60%)
  starting transfers between devices  40.1 us (12%)
  other arithmetic  32.2 us (9%)
  local copies, waits for them, and re-layouts  31.2 us (9%)
  matrix products  19.2 us (6%)
  between operations  13.9 us (4%)
    ppermute x16, waiting for transfers between devices, rotated(): return lax.ppermute(shard, axis, pairs)  130 us
    reduce_scatter x1, waiting for transfers between devices, body(): lax.psum_scatter(pair_sum, 'hc', scatter_dimension=0, tiled=True)  66.3 us
    ppermute x16, starting transfers between devices, rotated(): return lax.ppermute(shard, axis, pairs)  33.4 us
    dynamic_update_slice x14, local copies, waits for them, and re-layouts, gathered_by_permutes(): lax.dynamic_update_index_in_dim(stacked, piece, (me - by) % count, 0)  13.8 us
    all_gather x1, waiting for transfers between devices, body(): mine_rows = lax.all_gather(hidden_in, 'hc', axis=0, tiled=True)  10.3 us
  transfers between devices with their start and end apart: 19, of which 11 were waited for; matrix products, arithmetic and copies ran while one was open for 12% of the time, Pallas kernels for 0%

profile of v1, /device:TPU:0, one launch (start us, length us, event | category | flops | bytes accessed | tf_op | source)
XLA Modules:
  0.0 343.3 jit_solution(14646667927642795432)
XLA Ops:
  7.3 1.7 constant_dynamic-update-slice_fusion.2
  9.0 1.6 constant_dynamic-update-slice_fusion.1
  10.6 1.6 constant_dynamic-update-slice_fusion
  12.2 3.3 collective-permute-start
  15.5 1.5 collective-permute-start.1
  17.0 1.9 collective-permute-start.2
  18.9 3.8 %collective-permute-start.9 = (bf16[32,5376]{1,0:T(8,128)(2,1)}, bf16[32,5376]{1,0:T(8,128)(2,1)}, u32[]{:S(2)}, u32[]{:S(2)}) collective-permute-start(bf16[32,5376]{1,0:T(8,128)(2,1)} %param.16), channel_id=1, source_target_pairs={{0,16},{16,32},{32,48},{48,64},{64,80},{80,96},{96,112},{112,0},{1... | collective-permute-start | bytes 1032200 | tf_op jit(solution)/shard_map/ppermute | solution.py:25
  22.8 1.9 and_and_fusion.1
  24.7 1.1 and_and_fusion
  26.0 1.0 bitcast_dynamic-update-slice_fusion.15
  27.0 3.1 multiply_cosine_fusion
  30.6 1.2 bitcast_dynamic-update-slice_fusion.7
  31.7 40.0 %collective-permute-done.9 = bf16[32,5376]{1,0:T(8,128)(2,1)} collective-permute-done((bf16[32,5376]{1,0:T(8,128)(2,1)}, bf16[32,5376]{1,0:T(8,128)(2,1)}, u32[]{:S(2)}, u32[]{:S(2)}) %collective-permute-start.9) | collective-permute-done | bytes 344096 | tf_op jit(solution)/shard_map/ppermute | solution.py:25
  71.7 4.8 %collective-permute-start.11 = (bf16[32,5376]{1,0:T(8,128)(2,1)}, bf16[32,5376]{1,0:T(8,128)(2,1)S(1)}, u32[]{:S(2)}, u32[]{:S(2)}) collective-permute-start(bf16[32,5376]{1,0:T(8,128)(2,1)} %param.16), channel_id=1, source_target_pairs={{0,48},{16,64},{32,80},{48,96},{64,112},{80,0},{96,16},{112,32},{1... | collective-permute-start | bytes 1032200 | tf_op jit(solution)/shard_map/ppermute | solution.py:25
  76.5 1.0 bitcast_dynamic-update-slice_fusion.14
  77.5 2.9 collective-permute-start.12
  80.4 1.0 bitcast_dynamic-update-slice_fusion.13
  81.4 19.6 %collective-permute-done.11 = bf16[32,5376]{1,0:T(8,128)(2,1)S(1)} collective-permute-done((bf16[32,5376]{1,0:T(8,128)(2,1)}, bf16[32,5376]{1,0:T(8,128)(2,1)S(1)}, u32[]{:S(2)}, u32[]{:S(2)}) %collective-permute-start.11) | collective-permute-done | bytes 344096 | tf_op jit(solution)/shard_map/ppermute | solution.py:25
  101.4 12.5 %collective-permute-done.13 = bf16[32,5376]{1,0:T(8,128)(2,1)} collective-permute-done((bf16[32,5376]{1,0:T(8,128)(2,1)}, bf16[32,5376]{1,0:T(8,128)(2,1)}, u32[]{:S(2)}, u32[]{:S(2)}) %collective-permute-start.13) | collective-permute-done | bytes 344096 | tf_op jit(solution)/shard_map/ppermute | solution.py:25
  113.8 10.3 %all-gather.2.cloned.1.call-done = bf16[512,5376]{1,0:T(8,128)(2,1)} async-done(((bf16[64,5376]{1,0:T(8,128)(2,1)}), bf16[512,5376]{1,0:T(8,128)(2,1)}) %all-gather.2.cloned.1.call-update) | async-done | bytes 5505040 | tf_op jit(solution)/shard_map/all_gather | solution.py:92
  124.1 1.0 bitcast_dynamic-update-slice_fusion.10
  125.1 5.0 %collective-permute-start.15 = (bf16[32,5376]{1,0:T(8,128)(2,1)}, bf16[32,5376]{1,0:T(8,128)(2,1)S(1)}, u32[]{:S(2)}, u32[]{:S(2)}) collective-permute-start(bf16[32,5376]{1,0:T(8,128)(2,1)} %param.16), channel_id=1, source_target_pairs={{0,112},{16,0},{32,16},{48,32},{64,48},{80,64},{96,80},{112,96},{1... | collective-permute-start | bytes 1032200 | tf_op jit(solution)/shard_map/ppermute | solution.py:25
  130.2 1.0 bitcast_dynamic-update-slice_fusion.9
  131.2 7.3 %collective-permute-done.15 = bf16[32,5376]{1,0:T(8,128)(2,1)S(1)} collective-permute-done((bf16[32,5376]{1,0:T(8,128)(2,1)}, bf16[32,5376]{1,0:T(8,128)(2,1)S(1)}, u32[]{:S(2)}, u32[]{:S(2)}) %collective-permute-start.15) | collective-permute-done | bytes 344096 | tf_op jit(solution)/shard_map/ppermute | solution.py:25
  138.5 2.0 collective-permute-start.3
  140.5 4.9 %collective-permute-start.4 = (bf16[672,512]{1,0:T(8,128)(2,1)}, bf16[672,512]{1,0:T(8,128)(2,1)S(1)}, u32[]{:S(2)}, u32[]{:S(2)}) collective-permute-start(bf16[672,512]{1,0:T(8,128)(2,1)} %constant_dynamic-update-slice_fusion), channel_id=1, source_target_pairs={{0,80},{16,96},{32,112},{48,0},{64,16},{80,32},{96,48},{112,64},{1... | collective-permute-start | bytes 2064392 | tf_op jit(solution)/shard_map/ppermute | solution.py:25
  145.3 2.0 bitcast_dynamic-update-slice_fusion.6
  147.3 2.8 collective-permute-start.5
  150.1 2.0 bitcast_dynamic-update-slice_fusion.5
  152.1 2.0 bitcast_dynamic-update-slice_fusion.4
  154.1 4.4 %collective-permute-done.3 = bf16[672,512]{1,0:T(8,128)(2,1)S(1)} collective-permute-done((bf16[672,512]{1,0:T(8,128)(2,1)}, bf16[672,512]{1,0:T(8,128)(2,1)S(1)}, u32[]{:S(2)}, u32[]{:S(2)}) %collective-permute-start.3) | collective-permute-done | bytes 688160 | tf_op jit(solution)/shard_map/ppermute | solution.py:25
  159.4 17.2 %collective-permute-done.4 = bf16[672,512]{1,0:T(8,128)(2,1)S(1)} collective-permute-done((bf16[672,512]{1,0:T(8,128)(2,1)}, bf16[672,512]{1,0:T(8,128)(2,1)S(1)}, u32[]{:S(2)}, u32[]{:S(2)}) %collective-permute-start.4) | collective-permute-done | bytes 688160 | tf_op jit(solution)/shard_map/ppermute | solution.py:25
  177.5 9.5 %collective-permute-done.5 = bf16[672,512]{1,0:T(8,128)(2,1)S(1)} collective-permute-done((bf16[672,512]{1,0:T(8,128)(2,1)}, bf16[672,512]{1,0:T(8,128)(2,1)S(1)}, u32[]{:S(2)}, u32[]{:S(2)}) %collective-permute-start.5) | collective-permute-done | bytes 688160 | tf_op jit(solution)/shard_map/ppermute | solution.py:25
  187.9 11.6 %collective-permute-done.6 = bf16[672,512]{1,0:T(8,128)(2,1)S(1)} collective-permute-done((bf16[672,512]{1,0:T(8,128)(2,1)}, bf16[672,512]{1,0:T(8,128)(2,1)S(1)}, u32[]{:S(2)}, u32[]{:S(2)}) %collective-permute-start.6) | collective-permute-done | bytes 688160 | tf_op jit(solution)/shard_map/ppermute | solution.py:25
  200.4 1.2 fusion
  201.6 1.2 fusion.3
  203.0 3.0 fusion.8
  206.0 3.1 broadcast_select_fusion.1
  209.9 1.1 slice.79
  211.3 2.4 fusion.47
  213.7 1.0 pad_maximum_fusion.1
  214.7 6.6 %collective-permute-start.8 = (bf16[2,1024,128]{2,1,0:T(8,128)(2,1)}, bf16[2,1024,128]{2,1,0:T(8,128)(2,1)}, u32[]{:S(2)}, u32[]{:S(2)}) collective-permute-start(bf16[2,1024,128]{2,1,0:T(8,128)(2,1)} %pad_maximum_fusion.1), channel_id=1, source_target_pairs={{0,16},{16,32},{32,48},{48,64},{64,80},{80,96},{96,112},{1,17},{17... | collective-permute-start | bytes 1572872 | tf_op jit(solution)/shard_map/ppermute | solution.py:19
  221.3 2.5 copy.16
  223.8 1.3 multiply_reduce_fusion
  225.1 2.6 copy.17
  227.7 1.6 multiply_multiply_fusion
  229.4 1.6 multiply_subtract_fusion
  231.4 1.4 maximum_maximum_fusion
  232.8 1.2 fusion.6
  234.0 1.2 fusion.16
  235.2 2.7 fusion.26
  237.9 1.8 copy.22
  239.8 2.3 fusion.7
  242.0 1.3 fusion.17
  243.3 3.7 %fusion.29 = bf16[128,2,512]{2,0,1:T(8,128)(2,1)} fusion(f32[2,512]{1,0:T(2,128)S(1)} %fusion.17, f32[2,512]{1,0:T(2,128)S(1)} %get-tuple-element.19, f32[1536,512,2]{1,0,2:T(8,128)S(1)} %get-tuple-element.20, pred[512,1536]{0,1:T(8,128)(4,1)S(1)} %and_and_fusion, bf16[2,2048,128]{2,1,0:T(8,128)(2,1)} %copy-done.4), kind=kOutput, calls=%fused_computation.43 | convolution fusion | flops 409075712 | bytes 7741440 | tf_op jit(solution)/shard_map/jgqk,kjd->qjgd/dot_general | solution.py:157
  247.1 1.1 copy.23
  248.1 1.0 pad_maximum_fusion.2
  249.2 1.6 convolution_convert_fusion
  251.2 1.6 convolution_convert_fusion.1
  252.8 7.5 %collective-permute-done.16 = bf16[512,5376]{1,0:T(8,128)(2,1)} collective-permute-done((bf16[512,5376]{1,0:T(8,128)(2,1)S(1)}, bf16[512,5376]{1,0:T(8,128)(2,1)}, u32[]{:S(2)}, u32[]{:S(2)}) %collective-permute-start.16) | collective-permute-done | bytes 5505056 | tf_op jit(solution)/shard_map/ppermute | solution.py:25
  260.3 6.2 %add_convert_fusion = bf16[512,5376]{1,0:T(8,128)(2,1)} fusion(bf16[512,5376]{1,0:T(8,128)(2,1)} %collective-permute-done.16, bf16[512,5376]{1,0:T(8,128)(2,1)S(1)} %convolution_convert_fusion.1), kind=kLoop, calls=%fused_computation.10 | loop fusion | flops 11010048 | bytes 16515072 | tf_op jit(solution)/shard_map/convert_element_type | solution.py:174
  266.6 66.3 %reduce-scatter.2.cloned.1.call-done = bf16[64,5376]{1,0:T(8,128)(2,1)} async-done(((bf16[512,5376]{1,0:T(8,128)(2,1)}), bf16[64,5376]{1,0:T(8,128)(2,1)}) %reduce-scatter.2.cloned.1.call-update) | async-done | bytes 688144 | tf_op jit(solution)/shard_map/reduce_scatter | solution.py:175
  332.9 1.3 fusion.22
  334.2 2.3 fusion.25
  (79 shorter events, 7.6 us)
Async XLA Ops:
  6.5 117.6 %all-gather.2.cloned.1.call-start = ((), (), s32[]{:S(2)}) async-start(), calls=%async_computation.1 | async-start | bytes 6193152 | tf_op jit(solution)/shard_map/all_gather | solution.py:92
  7.3 325.6 %reduce-scatter.2.cloned.1.call-start = ((), (), s32[]{:S(2)}) async-start(), calls=%async_computation.2 | async-start | bytes 6193152 | tf_op jit(solution)/shard_map/reduce_scatter | solution.py:175
  12.2 128.2 %collective-permute-start = (bf16[672,512]{1,0:T(8,128)(2,1)}, bf16[672,512]{1,0:T(8,128)(2,1)}, u32[]{:S(2)}, u32[]{:S(2)}) collective-permute-start(bf16[672,512]{1,0:T(8,128)(2,1)} %constant_dynamic-update-slice_fusion), channel_id=1, source_target_pairs={{0,16},{16,32},{32,48},{48,64},{64,80},{80,96},{96,112},{112,0},{1... | collective-permute-start | bytes 2064392 | tf_op jit(solution)/shard_map/ppermute | solution.py:25
  15.5 131.8 %collective-permute-start.1 = (bf16[672,512]{1,0:T(8,128)(2,1)}, bf16[672,512]{1,0:T(8,128)(2,1)}, u32[]{:S(2)}, u32[]{:S(2)}) collective-permute-start(bf16[672,512]{1,0:T(8,128)(2,1)} %constant_dynamic-update-slice_fusion), channel_id=1, source_target_pairs={{0,32},{16,48},{32,64},{48,80},{64,96},{80,112},{96,0},{112,16},{1... | collective-permute-start | bytes 2064392 | tf_op jit(solution)/shard_map/ppermute | solution.py:25
  17.0 135.1 %collective-permute-start.2 = (bf16[672,512]{1,0:T(8,128)(2,1)}, bf16[672,512]{1,0:T(8,128)(2,1)}, u32[]{:S(2)}, u32[]{:S(2)}) collective-permute-start(bf16[672,512]{1,0:T(8,128)(2,1)} %constant_dynamic-update-slice_fusion), channel_id=1, source_target_pairs={{0,48},{16,64},{32,80},{48,96},{64,112},{80,0},{96,16},{112,32},{1... | collective-permute-start | bytes 2064392 | tf_op jit(solution)/shard_map/ppermute | solution.py:25
  18.9 52.8 %collective-permute-start.9 = (bf16[32,5376]{1,0:T(8,128)(2,1)}, bf16[32,5376]{1,0:T(8,128)(2,1)}, u32[]{:S(2)}, u32[]{:S(2)}) collective-permute-start(bf16[32,5376]{1,0:T(8,128)(2,1)} %param.16), channel_id=1, source_target_pairs={{0,16},{16,32},{32,48},{48,64},{64,80},{80,96},{96,112},{112,0},{1... | collective-permute-start | bytes 1032200 | tf_op jit(solution)/shard_map/ppermute | solution.py:25
  22.7 54.8 %collective-permute-start.10 = (bf16[32,5376]{1,0:T(8,128)(2,1)}, bf16[32,5376]{1,0:T(8,128)(2,1)}, u32[]{:S(2)}, u32[]{:S(2)}) collective-permute-start(bf16[32,5376]{1,0:T(8,128)(2,1)} %param.16), channel_id=1, source_target_pairs={{0,32},{16,48},{32,64},{48,80},{64,96},{80,112},{96,0},{112,16},{1... | collective-permute-start | bytes 1032200 | tf_op jit(solution)/shard_map/ppermute | solution.py:25
  31.7 69.6 %copy-start.2 = (bf16[8,672,512]{2,1,0:T(8,128)(2,1)}, bf16[8,672,512]{2,1,0:T(8,128)(2,1)S(1)}, u32[]{:S(2)}) copy-start(bf16[8,672,512]{2,1,0:T(8,128)(2,1)S(1)} %bitcast_dynamic-update-slice_fusion.7) | copy-start | bytes 16515076
  71.7 29.3 %collective-permute-start.11 = (bf16[32,5376]{1,0:T(8,128)(2,1)}, bf16[32,5376]{1,0:T(8,128)(2,1)S(1)}, u32[]{:S(2)}, u32[]{:S(2)}) collective-permute-start(bf16[32,5376]{1,0:T(8,128)(2,1)} %param.16), channel_id=1, source_target_pairs={{0,48},{16,64},{32,80},{48,96},{64,112},{80,0},{96,16},{112,32},{1... | collective-permute-start | bytes 1032200 | tf_op jit(solution)/shard_map/ppermute | solution.py:25
  77.5 23.5 %collective-permute-start.12 = (bf16[32,5376]{1,0:T(8,128)(2,1)}, bf16[32,5376]{1,0:T(8,128)(2,1)S(1)}, u32[]{:S(2)}, u32[]{:S(2)}) collective-permute-start(bf16[32,5376]{1,0:T(8,128)(2,1)} %param.16), channel_id=1, source_target_pairs={{0,64},{16,80},{32,96},{48,112},{64,0},{80,16},{96,32},{112,48},{1... | collective-permute-start | bytes 1032200 | tf_op jit(solution)/shard_map/ppermute | solution.py:25
  101.0 12.9 %collective-permute-start.13 = (bf16[32,5376]{1,0:T(8,128)(2,1)}, bf16[32,5376]{1,0:T(8,128)(2,1)}, u32[]{:S(2)}, u32[]{:S(2)}) collective-permute-start(bf16[32,5376]{1,0:T(8,128)(2,1)} %param.16), channel_id=1, source_target_pairs={{0,80},{16,96},{32,112},{48,0},{64,16},{80,32},{96,48},{112,64},{1... | collective-permute-start | bytes 1032200 | tf_op jit(solution)/shard_map/ppermute | solution.py:25
  101.0 24.1 %collective-permute-start.14 = (bf16[32,5376]{1,0:T(8,128)(2,1)}, bf16[32,5376]{1,0:T(8,128)(2,1)}, u32[]{:S(2)}, u32[]{:S(2)}) collective-permute-start(bf16[32,5376]{1,0:T(8,128)(2,1)} %param.16), channel_id=1, source_target_pairs={{0,96},{16,112},{32,0},{48,16},{64,32},{80,48},{96,64},{112,80},{1... | collective-permute-start | bytes 1032200 | tf_op jit(solution)/shard_map/ppermute | solution.py:25
  124.1 77.5 %collective-permute-start.7 = (bf16[512,5376]{1,0:T(8,128)(2,1)}, bf16[512,5376]{1,0:T(8,128)(2,1)S(1)}, u32[]{:S(2)}, u32[]{:S(2)}) collective-permute-start(bf16[512,5376]{1,0:T(8,128)(2,1)} %all-gather.2.cloned.1.call-done), channel_id=1, source_target_pairs={{0,1},{1,0},{2,3},{3,2},{4,5},{5,4},{6,7},{7,6},{8,9},{9,8},{10,11... | collective-permute-start | bytes 16515080 | tf_op jit(solution)/shard_map/ppermute | solution.py:25
  125.1 75.3 %copy-start.1 = (bf16[512,5376]{1,0:T(8,128)(2,1)S(1)}, bf16[512,5376]{1,0:T(8,128)(2,1)}, u32[]{:S(2)}) copy-start(bf16[512,5376]{1,0:T(8,128)(2,1)} %all-gather.2.cloned.1.call-done) | copy-start | bytes 16515076
  125.1 13.3 %collective-permute-start.15 = (bf16[32,5376]{1,0:T(8,128)(2,1)}, bf16[32,5376]{1,0:T(8,128)(2,1)S(1)}, u32[]{:S(2)}, u32[]{:S(2)}) collective-permute-start(bf16[32,5376]{1,0:T(8,128)(2,1)} %param.16), channel_id=1, source_target_pairs={{0,112},{16,0},{32,16},{48,32},{64,48},{80,64},{96,80},{112,96},{1... | collective-permute-start | bytes 1032200 | tf_op jit(solution)/shard_map/ppermute | solution.py:25
  138.5 20.0 %collective-permute-start.3 = (bf16[672,512]{1,0:T(8,128)(2,1)}, bf16[672,512]{1,0:T(8,128)(2,1)S(1)}, u32[]{:S(2)}, u32[]{:S(2)}) collective-permute-start(bf16[672,512]{1,0:T(8,128)(2,1)} %constant_dynamic-update-slice_fusion), channel_id=1, source_target_pairs={{0,64},{16,80},{32,96},{48,112},{64,0},{80,16},{96,32},{112,48},{1... | collective-permute-start | bytes 2064392 | tf_op jit(solution)/shard_map/ppermute | solution.py:25
  140.5 36.1 %collective-permute-start.4 = (bf16[672,512]{1,0:T(8,128)(2,1)}, bf16[672,512]{1,0:T(8,128)(2,1)S(1)}, u32[]{:S(2)}, u32[]{:S(2)}) collective-permute-start(bf16[672,512]{1,0:T(8,128)(2,1)} %constant_dynamic-update-slice_fusion), channel_id=1, source_target_pairs={{0,80},{16,96},{32,112},{48,0},{64,16},{80,32},{96,48},{112,64},{1... | collective-permute-start | bytes 2064392 | tf_op jit(solution)/shard_map/ppermute | solution.py:25
  147.3 39.7 %collective-permute-start.5 = (bf16[672,512]{1,0:T(8,128)(2,1)}, bf16[672,512]{1,0:T(8,128)(2,1)S(1)}, u32[]{:S(2)}, u32[]{:S(2)}) collective-permute-start(bf16[672,512]{1,0:T(8,128)(2,1)} %constant_dynamic-update-slice_fusion), channel_id=1, source_target_pairs={{0,96},{16,112},{32,0},{48,16},{64,32},{80,48},{96,64},{112,80},{1... | collective-permute-start | bytes 2064392 | tf_op jit(solution)/shard_map/ppermute | solution.py:25
  152.1 47.4 %collective-permute-start.6 = (bf16[672,512]{1,0:T(8,128)(2,1)}, bf16[672,512]{1,0:T(8,128)(2,1)S(1)}, u32[]{:S(2)}, u32[]{:S(2)}) collective-permute-start(bf16[672,512]{1,0:T(8,128)(2,1)} %constant_dynamic-update-slice_fusion), channel_id=1, source_target_pairs={{0,112},{16,0},{32,16},{48,32},{64,48},{80,64},{96,80},{112,96},{1... | collective-permute-start | bytes 2064392 | tf_op jit(solution)/shard_map/ppermute | solution.py:25
  200.4 2.6 copy-start.3
  200.4 2.6 copy-start.16
  209.1 1.9 copy-start.14
  209.9 3.8 %copy-start.6 = (bf16[1,1024,128]{2,1,0:T(8,128)(2,1)}, bf16[1,1024,128]{2,1,0:T(8,128)(2,1)S(1)}, u32[]{:S(2)}) copy-start(bf16[1,1024,128]{2,1,0:T(8,128)(2,1)S(1)} %fusion.43) | copy-start | bytes 786436
  209.9 17.8 %copy-start.15 = (f32[128]{0:T(128)S(1)}, f32[128]{0:T(128)}, u32[]{:S(2)}) copy-start(f32[128]{0:T(128)} %param.14) | copy-start | bytes 1540
  213.7 1.0 copy-start.8
  213.7 1.0 copy-start.10
  214.7 16.7 %collective-permute-start.8 = (bf16[2,1024,128]{2,1,0:T(8,128)(2,1)}, bf16[2,1024,128]{2,1,0:T(8,128)(2,1)}, u32[]{:S(2)}, u32[]{:S(2)}) collective-permute-start(bf16[2,1024,128]{2,1,0:T(8,128)(2,1)} %pad_maximum_fusion.1), channel_id=1, source_target_pairs={{0,16},{16,32},{32,48},{48,64},{64,80},{80,96},{96,112},{1,17},{17... | collective-permute-start | bytes 1572872 | tf_op jit(solution)/shard_map/ppermute | solution.py:19
  227.7 3.7 %copy-start.7 = (bf16[1,1024,128]{2,1,0:T(8,128)(2,1)S(1)}, bf16[1,1024,128]{2,1,0:T(8,128)(2,1)}, u32[]{:S(2)}) copy-start(bf16[1,1024,128]{2,1,0:T(8,128)(2,1)} %copy-done.6) | copy-start | bytes 786436
  227.7 3.7 %copy-start.9 = (bf16[1,1024,64]{2,1,0:T(8,128)(2,1)S(1)}, bf16[1,1024,64]{2,1,0:T(8,128)(2,1)}, u32[]{:S(2)}) copy-start(bf16[1,1024,64]{2,1,0:T(8,128)(2,1)} %copy-done.8) | copy-start | bytes 393220
  227.7 3.7 %copy-start.11 = (bf16[1,1024,64]{2,1,0:T(8,128)(2,1)S(1)}, bf16[1,1024,64]{2,1,0:T(8,128)(2,1)}, u32[]{:S(2)}) copy-start(bf16[1,1024,64]{2,1,0:T(8,128)(2,1)} %copy-done.10) | copy-start | bytes 393220
  229.4 3.4 copy-start
  231.3 1.4 copy-start.12
  232.8 2.4 copy-start.4
  250.8 9.5 %collective-permute-start.16 = (bf16[512,5376]{1,0:T(8,128)(2,1)S(1)}, bf16[512,5376]{1,0:T(8,128)(2,1)}, u32[]{:S(2)}, u32[]{:S(2)}) collective-permute-start(bf16[512,5376]{1,0:T(8,128)(2,1)S(1)} %convolution_convert_fusion), channel_id=1, source_target_pairs={{0,1},{1,0},{2,3},{3,2},{4,5},{5,4},{6,7},{7,6},{8,9},{9,8},{10,11... | collective-permute-start | bytes 16515080 | tf_op jit(solution)/shard_map/ppermute | solution.py:25
  266.6 67.7 %copy-start.5 = (bf16[64,5376]{1,0:T(8,128)(2,1)S(1)}, bf16[64,5376]{1,0:T(8,128)(2,1)}, u32[]{:S(2)}) copy-start(bf16[64,5376]{1,0:T(8,128)(2,1)} %param.9) | copy-start | bytes 2064388
  266.6 67.7 %copy-start.13 = (f32[5376]{0:T(1024)S(1)}, f32[5376]{0:T(1024)}, u32[]{:S(2)}) copy-start(f32[5376]{0:T(1024)} %param.17) | copy-start | bytes 64516
Sparse Core Ops, SparseCore 0:
  9.0 115.0 all-gather.1
  266.7 66.1 reduce-scatter.1

commit v2 on v0

--- a/solution.py
+++ b/solution.py
@@ -1,7 +1,7 @@
 import jax
 import jax.numpy as jnp
 from jax import lax
-from jax.sharding import PartitionSpec as P
+from jax.sharding import Mesh, PartitionSpec as P
 
 HEAD_SIZE = 128
 WINDOW_SPAN = 1024
@@ -11,12 +11,38 @@
 query_scale = 168.0 ** (-0.5)
 rope_base = 10000.0
 mask_value = -1e30
+CTX = ("cx", "cy")
+HEAD = ("hc", "core")
 
 
 def passed_along(shard, axis, by):
     count = lax.axis_size(axis)
     pairs = [(i, i + by) for i in range(count) if 0 <= i + by < count]
     return lax.ppermute(shard, axis, pairs)
+
+
+def rotated(shard, axis, by):
+    count = lax.axis_size(axis)
+    pairs = [(i, (i + by) % count) for i in range(count)]
+    return lax.ppermute(shard, axis, pairs)
+
+
+def placed(parts, me, count):
+    stacked = jnp.zeros((count,) + parts[0].shape, parts[0].dtype)
+    for i, part in enumerate(parts):
+        stacked = lax.dynamic_update_index_in_dim(stacked, part, (me + i) % count, 0)
+    return stacked
+
+
+def gathered_over_ctx(piece):
+    cy = lax.axis_index("cy")
+    cx = lax.axis_index("cx")
+    pair = placed([piece, rotated(piece, "cy", 1)], cy, 2)
+    from_left = rotated(pair, "cx", 1)
+    from_right = rotated(pair, "cx", -1)
+    far = jnp.stack([rotated(from_left[0], "cx", 1), rotated(from_right[1], "cx", -1)])
+    ring = placed([pair, from_right, far, from_left], cx, 4)
+    return ring.reshape((8 * piece.shape[0],) + piece.shape[1:])
 
 
 def root_mean_scale(values, scaling):
@@ -54,20 +80,23 @@
     post_gain,
 ):
     own_rows = hidden_in.astype(jnp.float32)
-    raw_rows = lax.all_gather(hidden_in, "head", axis=0, tiled=True)
+    q_cols = w_query.shape[1]
+    k_cols = w_key.shape[1]
+    w_in = gathered_over_ctx(jnp.concatenate([w_query, w_key, value_weight], axis=1))
+    out_weight = gathered_over_ctx(w_output)
+
+    raw_rows = lax.all_gather(hidden_in, HEAD, axis=0, tiled=True)
     normed = root_mean_scale(raw_rows.astype(jnp.float32), pre_gain).astype(jnp.bfloat16)
     tok_count = normed.shape[0]
+    projected = jnp.dot(normed, w_in, preferred_element_type=jnp.float32)
+    query_raw = projected[:, :q_cols]
+    key_unnormed = projected[:, q_cols : q_cols + k_cols]
+    value_unnormed = projected[:, q_cols + k_cols :]
 
-    def add_rows(weight_piece):
-        return jnp.dot(normed, weight_piece, preferred_element_type=jnp.float32)
-
-    query_raw = add_rows(lax.all_gather(w_query, "ctx", axis=0, tiled=True))
-    key_unnormed = add_rows(lax.all_gather(w_key, "ctx", axis=0, tiled=True))
-    value_unnormed = add_rows(lax.all_gather(value_weight, "ctx", axis=0, tiled=True))
-    local_heads = w_query.shape[1] // HEAD_SIZE
-    local_groups = w_key.shape[1] // HEAD_SIZE
+    local_heads = q_cols // HEAD_SIZE
+    local_groups = k_cols // HEAD_SIZE
     heads_per_group = local_heads // local_groups
-    ctx_index = lax.axis_index("ctx")
+    ctx_index = lax.axis_index(CTX)
     token_places = ctx_index * tok_count + jnp.arange(tok_count, dtype=jnp.int32)
     query_matrix = (
         apply_rotary(
@@ -84,7 +113,7 @@
     key_value = jnp.stack(
         [projected_keys.reshape(tok_count, local_groups * HEAD_SIZE), projected_values]
     )
-    pieces = [passed_along(key_value, "ctx", 1)]
+    pieces = [passed_along(key_value, CTX, 1)]
     extended = jnp.concatenate(pieces + [key_value], axis=1)
     band_keys = extended[0].reshape(-1, local_groups, HEAD_SIZE)
     band_values = extended[1].reshape(-1, local_groups, HEAD_SIZE)
@@ -121,35 +150,38 @@
         )
         outputs.append(mixed.astype(jnp.bfloat16).reshape(block_rows, local_heads * HEAD_SIZE))
     attended = jnp.concatenate(outputs, axis=0)
-    out_weight = lax.all_gather(w_output, "ctx", axis=0, tiled=True)
+
     partial_value = jnp.dot(attended, out_weight, preferred_element_type=jnp.float32).astype(
         jnp.bfloat16
     )
     summed = lax.psum_scatter(
-        lax.optimization_barrier(partial_value).astype(jnp.float32).astype(jnp.bfloat16),
-        "head",
-        scatter_dimension=0,
-        tiled=True,
+        partial_value, HEAD, scatter_dimension=0, tiled=True
     ).astype(jnp.float32)
     result = own_rows + root_mean_scale(summed, post_gain)
     return result.astype(jnp.bfloat16)
 
 
 def solution(mesh):
+    ctx_size, head_size = mesh.devices.shape
+    view = Mesh(
+        mesh.devices.reshape(ctx_size // 2, 2, head_size // 2, 2), CTX + HEAD
+    )
+    rows_spec = P(CTX + HEAD, None)
+    cols_spec = P(CTX, HEAD)
     return jax.shard_map(
         body,
-        mesh=mesh,
+        mesh=view,
         in_specs=(
-            P(("ctx", "head"), None),
+            rows_spec,
             P(),
-            P("ctx", "head"),
-            P("ctx", "head"),
-            P("ctx", "head"),
+            cols_spec,
+            cols_spec,
+            cols_spec,
             P(),
             P(),
-            P(("head", "ctx"), None),
+            P(HEAD + CTX, None),
             P(),
         ),
-        out_specs=P(("ctx", "head"), None),
+        out_specs=rows_spec,
         check_vma=False,
     )

time: 401 us -> 274 us (0.68)
  waiting for transfers between devices: 312 us -> 165 us
  starting transfers between devices: 3.56 us -> 23 us
  local copies, waits for them, and re-layouts: 2.37 us -> 21.6 us
  matrix products: 39.9 us -> 23.2 us
    all_gather x5 -> x1, waiting for transfers between devices: 230 us -> 0.01 us  [body(): raw_rows = lax.all_gather(hidden_in, HEAD, axis=0, tiled=True)]
    ppermute x0 -> x10, waiting for transfers between devices: none -> 80.3 us  [rotated(): return lax.ppermute(shard, axis, pairs)]
    ppermute x0 -> x10, starting transfers between devices: none -> 16.4 us  [rotated(): return lax.ppermute(shard, axis, pairs)]
    dot_general x3 -> x1, matrix products: 25.4 us -> 10.7 us  [body(): projected = jnp.dot(normed, w_in, preferred_element_type=jnp.float32)]
    dynamic_update_slice x0 -> x10, local copies, waits for them, and re-layouts: none -> 8.69 us  [placed(): lax.dynamic_update_index_in_dim(stacked, part, (me + i) % count, 0)]
    convert_element_type x1, other arithmetic: 5.96 us -> 0.01 us  [apply_rotary(): angles = token_places.astype(jnp.float32)[:, None] * frequency[None, :]]
    reduce_scatter x1, waiting for transfers between devices: 78.9 us -> 84 us  [body(): lax.psum_scatter(partial_value, HEAD, scatter_dimension=0, tiled=True)]
  transfers between devices with their start and end apart: 7 -> 13, of which waited for: 6 -> 5; matrix products, arithmetic and copies ran while one was open for 15% -> 11% of each run, Pallas kernels for 0% -> 0%
where the time goes in v2:
time: 274 us; the launch traced here: 273 us
  waiting for transfers between devices  165 us (60%)
  other arithmetic  26.5 us (10%)
  matrix products  23.2 us (8%)
  starting transfers between devices  23 us (8%)
  local copies, waits for them, and re-layouts  21.6 us (8%)
  between operations  13.8 us (5%)
    reduce_scatter x1, waiting for transfers between devices, body(): lax.psum_scatter(partial_value, HEAD, scatter_dimension=0, tiled=True)  84 us
    ppermute x10, waiting for transfers between devices, rotated(): return lax.ppermute(shard, axis, pairs)  80.3 us
    ppermute x10, starting transfers between devices, rotated(): return lax.ppermute(shard, axis, pairs)  16.4 us
    dot_general x1, matrix products, body(): projected = jnp.dot(normed, w_in, preferred_element_type=jnp.float32)  10.7 us
    dynamic_update_slice x10, local copies, waits for them, and re-layouts, placed(): lax.dynamic_update_index_in_dim(stacked, part, (me + i) % count, 0)  8.69 us
    reduce_sum x4, other arithmetic, root_mean_scale(): mean_sq = jnp.mean(values * values, axis=-1, keepdims=True)  7.83 us
    ppermute x1, starting transfers between devices, passed_along(): return lax.ppermute(shard, axis, pairs)  6.59 us
    dot_general x1, matrix products, body(): jnp.dot(attended, out_weight, preferred_element_type=jnp.float32)  5.9 us
  transfers between devices with their start and end apart: 13, of which 5 were waited for; matrix products, arithmetic and copies ran while one was open for 11% of the time, Pallas kernels for 0%

profile of v2, /device:TPU:0, one launch (start us, length us, event | category | flops | bytes accessed | tf_op | source)
XLA Modules:
  0.0 273.2 jit_solution(8334479350814508100)
XLA Ops:
  6.5 0.7 all-gather.2.cloned.1.call-update
  7.3 0.0 reduce-scatter.2.cloned.1.call-start
  7.3 1.8 constant_dynamic-update-slice_fusion.2
  9.1 1.6 constant_dynamic-update-slice_fusion.1
  10.7 1.6 constant_dynamic-update-slice_fusion
  12.3 3.3 %collective-permute-start = (bf16[672,512]{1,0:T(8,128)(2,1)}, bf16[672,512]{1,0:T(8,128)(2,1)}, u32[]{:S(2)}, u32[]{:S(2)}) collective-permute-start(bf16[672,512]{1,0:T(8,128)(2,1)} %constant_dynamic-update-slice_fusion), channel_id=1, source_target_pairs={{0,16},{16,0},{1,17},{17,1},{2,18},{18,2},{3,19},{19,3},{4,20},{20... | collective-permute-start | bytes 2064392 | tf_op jit(solution)/shard_map/ppermute | solution.py:27
  15.6 0.2 collective-permute-start.6
  16.0 2.8 %and_and_fusion = (pred[512,1536]{0,1:T(8,128)(4,1)S(1)}, pred[512,1536]{0,1:T(8,128)(4,1)}) fusion(s32[512]{0:T(512)S(1)} %get-tuple-element.13, s32[512]{0:T(512)S(1)} %get-tuple-element.14, s32[1536]{0:T(1024)S(1)} %iota_add_fusion, pred[1536]{0:T(1024)(128)(4,1)S(1)} %broadcast_compare_fusion, pred[1536]{0:T(1024)(128)(4,1)S(1)} %broadcast_compare_fusion.1, ...), kind=kLoop, calls=%fused_computation.23 | loop fusion | flops 6291456 | bytes 1596416 | tf_op jit(solution)/shard_map/and | solution.py:139
  18.8 0.9 broadcast_in_dim.106
  19.6 0.8 bitcast_dynamic-update-slice_fusion.9
  20.4 3.0 %multiply_cosine_fusion = (f32[1024,64]{1,0:T(8,128)}, f32[1024,64]{1,0:T(8,128)}) fusion(f32[64]{0:T(128)S(1)} %multiply_power_fusion, f32[1024]{0:T(1024)S(1)} %fusion.46), kind=kLoop, calls=%fused_computation.46 | loop fusion | flops 65536 | bytes 528640 | tf_op jit(solution)/shard_map/cos | solution.py:58
  23.4 0.1 broadcast_in_dim.95
  23.5 1.2 bitcast_dynamic-update-slice_fusion.7
  24.7 31.8 %collective-permute-done.6 = bf16[32,5376]{1,0:T(8,128)(2,1)S(1)} collective-permute-done((bf16[32,5376]{1,0:T(8,128)(2,1)}, bf16[32,5376]{1,0:T(8,128)(2,1)S(1)}, u32[]{:S(2)}, u32[]{:S(2)}) %collective-permute-start.6) | collective-permute-done | bytes 344096 | tf_op jit(solution)/shard_map/ppermute | solution.py:27
  56.5 0.8 bitcast_dynamic-update-slice_fusion.8
  57.3 2.7 collective-permute-start.7
  59.9 0.0 collective-permute-start.8
  59.9 0.2 broadcast_in_dim.105
  60.1 1.2 bitcast_dynamic-update-slice_fusion.5
  61.3 1.2 bitcast_dynamic-update-slice_fusion.6
  62.5 3.3 %collective-permute-start.1 = (bf16[2,672,512]{2,1,0:T(8,128)(2,1)S(1)}, bf16[2,672,512]{2,1,0:T(8,128)(2,1)S(1)}, u32[]{:S(2)}, u32[]{:S(2)}) collective-permute-start(bf16[2,672,512]{2,1,0:T(8,128)(2,1)S(1)} %bitcast_dynamic-update-slice_fusion.6), channel_id=1, source_target_pairs={{0,96},{32,0},{64,32},{96,64},{1,97},{33,1},{65,33},{97,65},{2,98}... | collective-permute-start | bytes 4128776 | tf_op jit(solution)/shard_map/ppermute | solution.py:27
  65.8 2.8 %broadcast_in_dim.94 = bf16[4,2,672,512]{3,2,1,0:T(8,128)(2,1)} broadcast(bf16[]{:T(256)} %constant.124.clone.1), dimensions={} | broadcast | bytes 5505026 | tf_op jit(solution)/shard_map/broadcast_in_dim | solution.py:31
  68.6 1.2 bitcast_dynamic-update-slice_fusion.2
  69.8 9.9 %collective-permute-done.8 = bf16[2,32,5376]{2,1,0:T(8,128)(2,1)S(1)} collective-permute-done((bf16[2,32,5376]{2,1,0:T(8,128)(2,1)}, bf16[2,32,5376]{2,1,0:T(8,128)(2,1)S(1)}, u32[]{:S(2)}, u32[]{:S(2)}) %collective-permute-start.8) | collective-permute-done | bytes 688160 | tf_op jit(solution)/shard_map/ppermute | solution.py:27
  79.7 0.1 collective-permute-start.9
  79.8 3.3 %collective-permute-start.10 = (bf16[32,5376]{1,0:T(8,128)(2,1)S(1)}, bf16[32,5376]{1,0:T(8,128)(2,1)S(1)}, u32[]{:S(2)}, u32[]{:S(2)}) collective-permute-start(bf16[32,5376]{1,0:T(8,128)(2,1)S(1)} %slice_bitcast_fusion.10), channel_id=1, source_target_pairs={{0,96},{32,0},{64,32},{96,64},{1,97},{33,1},{65,33},{97,65},{2,98}... | collective-permute-start | bytes 1032200 | tf_op jit(solution)/shard_map/ppermute | solution.py:27
  83.1 0.1 bitcast_dynamic-update-slice_fusion.4
  83.2 29.3 %collective-permute-done.9 = bf16[32,5376]{1,0:T(8,128)(2,1)S(1)} collective-permute-done((bf16[32,5376]{1,0:T(8,128)(2,1)S(1)}, bf16[32,5376]{1,0:T(8,128)(2,1)S(1)}, u32[]{:S(2)}, u32[]{:S(2)}) %collective-permute-start.9) | collective-permute-done | bytes 344096 | tf_op jit(solution)/shard_map/ppermute | solution.py:27
  112.4 0.0 collective-permute-done.10
  112.4 0.1 fusion.27
  112.5 0.1 collective-permute-start.3
  112.7 3.5 %collective-permute-start.4 = (bf16[672,512]{1,0:T(8,128)(2,1)S(1)}, bf16[672,512]{1,0:T(8,128)(2,1)S(1)}, u32[]{:S(2)}, u32[]{:S(2)}) collective-permute-start(bf16[672,512]{1,0:T(8,128)(2,1)S(1)} %slice_bitcast_fusion), channel_id=1, source_target_pairs={{0,96},{32,0},{64,32},{96,64},{1,97},{33,1},{65,33},{97,65},{2,98}... | collective-permute-start | bytes 2064392 | tf_op jit(solution)/shard_map/ppermute | solution.py:27
  116.2 0.1 bitcast_dynamic-update-slice_fusion.3
  116.2 1.2 bitcast_dynamic-update-slice_fusion.1
  117.5 9.3 %collective-permute-done.3 = bf16[672,512]{1,0:T(8,128)(2,1)S(1)} collective-permute-done((bf16[672,512]{1,0:T(8,128)(2,1)S(1)}, bf16[672,512]{1,0:T(8,128)(2,1)S(1)}, u32[]{:S(2)}, u32[]{:S(2)}) %collective-permute-start.3) | collective-permute-done | bytes 688160 | tf_op jit(solution)/shard_map/ppermute | solution.py:27
  126.7 1.2 fusion.19
  127.9 1.2 bitcast_dynamic-update-slice_fusion
  129.1 6.3 %fusion = f32[1024]{0:T(1024)S(1)} fusion(bf16[1024,5376]{1,0:T(8,128)(2,1)} %all-gather.2.cloned.1.call-done), kind=kLoop, calls=%fused_computation.2 | loop fusion | flops 16514048 | bytes 11014144 | tf_op jit(solution)/shard_map/reduce_sum | solution.py:49
  135.5 10.7 %fusion.3 = f32[1024,512]{0,1:T(8,128)S(1)} fusion(bf16[5376,512]{1,0:T(8,128)(2,1)} %bitcast.10, bf16[1024,5376]{1,0:T(8,128)(2,1)} %all-gather.2.cloned.1.call-done, f32[5376]{0:T(1024)S(1)} %copy-done.11, f32[1024]{0:T(1024)S(1)} %add_rsqrt_fusion.2), kind=kOutput, calls=%fused_computation.6 | convolution fusion | flops 5659164672 | bytes 18637824 | tf_op jit(solution)/shard_map/dot_general | solution.py:91
  146.2 0.0 copy-start.10
  146.2 0.1 multiply_reduce_fusion.1
  146.4 1.1 slice.97
  147.4 0.1 multiply_reduce_fusion
  147.6 0.1 multiply_bitcast_fusion
  147.7 1.2 fusion.45
  148.9 0.8 pad_maximum_fusion
  149.7 6.6 %collective-permute-start.5 = (bf16[2,1024,128]{1,2,0:T(8,128)(2,1)}, bf16[2,1024,128]{1,2,0:T(8,128)(2,1)}, u32[]{:S(2)}, u32[]{:S(2)}) collective-permute-start(bf16[2,1024,128]{1,2,0:T(8,128)(2,1)} %pad_maximum_fusion), channel_id=1, source_target_pairs={{0,16},{16,32},{32,48},{48,64},{64,80},{80,96},{96,112},{1,17},{17... | collective-permute-start | bytes 1572872 | tf_op jit(solution)/shard_map/ppermute | solution.py:21
  156.3 2.6 copy.10
  158.9 1.6 multiply_multiply_fusion
  160.5 1.6 multiply_subtract_fusion
  162.1 0.3 fusion.26
  162.5 0.0 collective-permute-done.5
  162.5 1.1 maximum_maximum_fusion
  163.6 1.3 fusion.7
  164.9 1.2 fusion.9
  166.2 2.0 fusion.20
  168.2 1.3 fusion.8
  169.4 1.3 fusion.10
  170.7 2.0 fusion.23
  172.8 5.9 %convolution_convert_fusion = bf16[1024,5376]{1,0:T(8,128)(2,1)} fusion(bf16[256,5376]{1,0:T(8,128)(2,1)S(1)} %bitcast.130, bf16[512,256]{0,1:T(8,128)(2,1)S(1)} %bitcast.137, bf16[512,256]{0,1:T(8,128)(2,1)S(1)} %bitcast.136), kind=kOutput, calls=%fused_computation.5 | convolution fusion | flops 2825125888 | bytes 14286848 | tf_op jit(solution)/shard_map/dot_general | solution.py:154
  178.7 0.0 reduce-scatter.2.cloned.1.call-update
  178.7 84.0 %reduce-scatter.2.cloned.1.call-done = bf16[64,5376]{1,0:T(8,128)(2,1)} async-done(((bf16[1024,5376]{1,0:T(8,128)(2,1)}), bf16[64,5376]{1,0:T(8,128)(2,1)}) %reduce-scatter.2.cloned.1.call-update) | async-done | bytes 688144 | tf_op jit(solution)/shard_map/reduce_scatter | solution.py:157
  262.7 1.3 fusion.15
  264.1 2.3 fusion.18
  (48 shorter events, 0.3 us)
Async XLA Ops:
  6.5 13.1 %copy-start.8 = (bf16[32,5376]{1,0:T(8,128)(2,1)S(1)}, bf16[32,5376]{1,0:T(8,128)(2,1)}, u32[]{:S(2)}) copy-start(bf16[32,5376]{1,0:T(8,128)(2,1)} %param.16) | copy-start | bytes 1032196
  6.5 122.6 %all-gather.2.cloned.1.call-start = ((), (), s32[]{:S(2)}) async-start(), calls=%async_computation.1 | async-start | bytes 11698176 | tf_op jit(solution)/shard_map/all_gather | solution.py:88
  7.3 255.4 %reduce-scatter.2.cloned.1.call-start = ((), (), s32[]{:S(2)}) async-start(), calls=%async_computation.2 | async-start | bytes 11698176 | tf_op jit(solution)/shard_map/reduce_scatter | solution.py:157
  12.3 49.0 %collective-permute-start = (bf16[672,512]{1,0:T(8,128)(2,1)}, bf16[672,512]{1,0:T(8,128)(2,1)}, u32[]{:S(2)}, u32[]{:S(2)}) collective-permute-start(bf16[672,512]{1,0:T(8,128)(2,1)} %constant_dynamic-update-slice_fusion), channel_id=1, source_target_pairs={{0,16},{16,0},{1,17},{17,1},{2,18},{18,2},{3,19},{19,3},{4,20},{20... | collective-permute-start | bytes 2064392 | tf_op jit(solution)/shard_map/ppermute | solution.py:27
  15.6 40.9 %collective-permute-start.6 = (bf16[32,5376]{1,0:T(8,128)(2,1)}, bf16[32,5376]{1,0:T(8,128)(2,1)S(1)}, u32[]{:S(2)}, u32[]{:S(2)}) collective-permute-start(bf16[32,5376]{1,0:T(8,128)(2,1)} %param.16), channel_id=1, source_target_pairs={{0,16},{16,0},{1,17},{17,1},{2,18},{18,2},{3,19},{19,3},{4,20},{20... | collective-permute-start | bytes 1032200 | tf_op jit(solution)/shard_map/ppermute | solution.py:27
  57.3 22.5 %collective-permute-start.7 = (bf16[2,32,5376]{2,1,0:T(8,128)(2,1)}, bf16[2,32,5376]{2,1,0:T(8,128)(2,1)S(1)}, u32[]{:S(2)}, u32[]{:S(2)}) collective-permute-start(bf16[2,32,5376]{2,1,0:T(8,128)(2,1)} %bitcast_dynamic-update-slice_fusion.8), channel_id=1, source_target_pairs={{0,96},{32,0},{64,32},{96,64},{1,97},{33,1},{65,33},{97,65},{2,98}... | collective-permute-start | bytes 2064392 | tf_op jit(solution)/shard_map/ppermute | solution.py:27
  59.9 19.7 %collective-permute-start.8 = (bf16[2,32,5376]{2,1,0:T(8,128)(2,1)}, bf16[2,32,5376]{2,1,0:T(8,128)(2,1)S(1)}, u32[]{:S(2)}, u32[]{:S(2)}) collective-permute-start(bf16[2,32,5376]{2,1,0:T(8,128)(2,1)} %bitcast_dynamic-update-slice_fusion.8), channel_id=1, source_target_pairs={{0,32},{32,64},{64,96},{96,0},{1,33},{33,65},{65,97},{97,1},{2,34}... | collective-permute-start | bytes 2064392 | tf_op jit(solution)/shard_map/ppermute | solution.py:27
  62.5 50.2 %collective-permute-start.1 = (bf16[2,672,512]{2,1,0:T(8,128)(2,1)S(1)}, bf16[2,672,512]{2,1,0:T(8,128)(2,1)S(1)}, u32[]{:S(2)}, u32[]{:S(2)}) collective-permute-start(bf16[2,672,512]{2,1,0:T(8,128)(2,1)S(1)} %bitcast_dynamic-update-slice_fusion.6), channel_id=1, source_target_pairs={{0,96},{32,0},{64,32},{96,64},{1,97},{33,1},{65,33},{97,65},{2,98}... | collective-permute-start | bytes 4128776 | tf_op jit(solution)/shard_map/ppermute | solution.py:27
  65.8 46.7 %collective-permute-start.2 = (bf16[2,672,512]{2,1,0:T(8,128)(2,1)S(1)}, bf16[2,672,512]{2,1,0:T(8,128)(2,1)S(1)}, u32[]{:S(2)}, u32[]{:S(2)}) collective-permute-start(bf16[2,672,512]{2,1,0:T(8,128)(2,1)S(1)} %bitcast_dynamic-update-slice_fusion.6), channel_id=1, source_target_pairs={{0,32},{32,64},{64,96},{96,0},{1,33},{33,65},{65,97},{97,1},{2,34}... | collective-permute-start | bytes 4128776 | tf_op jit(solution)/shard_map/ppermute | solution.py:27
  79.7 32.7 %collective-permute-start.9 = (bf16[32,5376]{1,0:T(8,128)(2,1)S(1)}, bf16[32,5376]{1,0:T(8,128)(2,1)S(1)}, u32[]{:S(2)}, u32[]{:S(2)}) collective-permute-start(bf16[32,5376]{1,0:T(8,128)(2,1)S(1)} %slice_bitcast_fusion.11), channel_id=1, source_target_pairs={{0,32},{32,64},{64,96},{96,0},{1,33},{33,65},{65,97},{97,1},{2,34}... | collective-permute-start | bytes 1032200 | tf_op jit(solution)/shard_map/ppermute | solution.py:27
  79.8 32.6 %collective-permute-start.10 = (bf16[32,5376]{1,0:T(8,128)(2,1)S(1)}, bf16[32,5376]{1,0:T(8,128)(2,1)S(1)}, u32[]{:S(2)}, u32[]{:S(2)}) collective-permute-start(bf16[32,5376]{1,0:T(8,128)(2,1)S(1)} %slice_bitcast_fusion.10), channel_id=1, source_target_pairs={{0,96},{32,0},{64,32},{96,64},{1,97},{33,1},{65,33},{97,65},{2,98}... | collective-permute-start | bytes 1032200 | tf_op jit(solution)/shard_map/ppermute | solution.py:27
  112.5 14.2 %collective-permute-start.3 = (bf16[672,512]{1,0:T(8,128)(2,1)S(1)}, bf16[672,512]{1,0:T(8,128)(2,1)S(1)}, u32[]{:S(2)}, u32[]{:S(2)}) collective-permute-start(bf16[672,512]{1,0:T(8,128)(2,1)S(1)} %slice_bitcast_fusion.1), channel_id=1, source_target_pairs={{0,32},{32,64},{64,96},{96,0},{1,33},{33,65},{65,97},{97,1},{2,34}... | collective-permute-start | bytes 2064392 | tf_op jit(solution)/shard_map/ppermute | solution.py:27
  112.7 14.1 %collective-permute-start.4 = (bf16[672,512]{1,0:T(8,128)(2,1)S(1)}, bf16[672,512]{1,0:T(8,128)(2,1)S(1)}, u32[]{:S(2)}, u32[]{:S(2)}) collective-permute-start(bf16[672,512]{1,0:T(8,128)(2,1)S(1)} %slice_bitcast_fusion), channel_id=1, source_target_pairs={{0,96},{32,0},{64,32},{96,64},{1,97},{33,1},{65,33},{97,65},{2,98}... | collective-permute-start | bytes 2064392 | tf_op jit(solution)/shard_map/ppermute | solution.py:27
  129.1 6.4 %copy-start.11 = (f32[5376]{0:T(1024)S(1)}, f32[5376]{0:T(1024)}, u32[]{:S(2)}) copy-start(f32[5376]{0:T(1024)} %param.10) | copy-start | bytes 64516
  146.2 1.3 copy-start.10
  146.3 2.5 copy-start.2
  148.8 0.9 copy-start.4
  148.8 7.5 %copy-start.6 = (bf16[1,1024,64]{1,2,0:T(8,128)(2,1)}, bf16[1,1024,64]{1,2,0:T(8,128)(2,1)S(1)}, u32[]{:S(2)}) copy-start(bf16[1,1024,64]{1,2,0:T(8,128)(2,1)S(1)} %get-tuple-element.8) | copy-start | bytes 393220
  149.7 12.8 %collective-permute-start.5 = (bf16[2,1024,128]{1,2,0:T(8,128)(2,1)}, bf16[2,1024,128]{1,2,0:T(8,128)(2,1)}, u32[]{:S(2)}, u32[]{:S(2)}) collective-permute-start(bf16[2,1024,128]{1,2,0:T(8,128)(2,1)} %pad_maximum_fusion), channel_id=1, source_target_pairs={{0,16},{16,32},{32,48},{48,64},{64,80},{80,96},{96,112},{1,17},{17... | collective-permute-start | bytes 1572872 | tf_op jit(solution)/shard_map/ppermute | solution.py:21
  160.5 2.0 copy-start.3
  160.5 2.0 copy-start.5
  160.5 2.0 copy-start.7
  162.1 1.5 copy-start
  178.7 85.4 %copy-start.1 = (bf16[64,5376]{1,0:T(8,128)(2,1)S(1)}, bf16[64,5376]{1,0:T(8,128)(2,1)}, u32[]{:S(2)}) copy-start(bf16[64,5376]{1,0:T(8,128)(2,1)} %param.9) | copy-start | bytes 2064388
  178.7 85.4 %copy-start.9 = (f32[5376]{0:T(1024)S(1)}, f32[5376]{0:T(1024)}, u32[]{:S(2)}) copy-start(f32[5376]{0:T(1024)} %param.17) | copy-start | bytes 64516
Sparse Core Ops, SparseCore 0:
  9.0 83.1 all-gather.1
  178.8 83.8 reduce-scatter.1

commit v3 on v2

--- a/solution.py
+++ b/solution.py
@@ -34,14 +34,23 @@
     return stacked
 
 
+def ring_over_cx(piece):
+    half = piece.shape[0] // 2
+    from_left = rotated(piece, "cx", 1)
+    from_right = rotated(piece, "cx", -1)
+    far = jnp.concatenate(
+        [rotated(from_left[:half], "cx", 1), rotated(from_right[half:], "cx", -1)]
+    )
+    return [piece, from_right, far, from_left]
+
+
 def gathered_over_ctx(piece):
     cy = lax.axis_index("cy")
     cx = lax.axis_index("cx")
-    pair = placed([piece, rotated(piece, "cy", 1)], cy, 2)
-    from_left = rotated(pair, "cx", 1)
-    from_right = rotated(pair, "cx", -1)
-    far = jnp.stack([rotated(from_left[0], "cx", 1), rotated(from_right[1], "cx", -1)])
-    ring = placed([pair, from_right, far, from_left], cx, 4)
+    own = ring_over_cx(piece)
+    partner = ring_over_cx(rotated(piece, "cy", 1))
+    pairs = [placed([a, b], cy, 2) for a, b in zip(own, partner)]
+    ring = placed(pairs, cx, 4)
     return ring.reshape((8 * piece.shape[0],) + piece.shape[1:])
 
 
@@ -83,12 +92,13 @@
     q_cols = w_query.shape[1]
     k_cols = w_key.shape[1]
     w_in = gathered_over_ctx(jnp.concatenate([w_query, w_key, value_weight], axis=1))
-    out_weight = gathered_over_ctx(w_output)
 
     raw_rows = lax.all_gather(hidden_in, HEAD, axis=0, tiled=True)
     normed = root_mean_scale(raw_rows.astype(jnp.float32), pre_gain).astype(jnp.bfloat16)
     tok_count = normed.shape[0]
     projected = jnp.dot(normed, w_in, preferred_element_type=jnp.float32)
+    projected, w_output = lax.optimization_barrier((projected, w_output))
+    out_weight = gathered_over_ctx(w_output)
     query_raw = projected[:, :q_cols]
     key_unnormed = projected[:, q_cols : q_cols + k_cols]
     value_unnormed = projected[:, q_cols + k_cols :]

time: 274 us -> 244 us (0.89)
  waiting for transfers between devices: 165 us -> 126 us
  starting transfers between devices: 23 us -> 35.3 us
    ppermute x10 -> x18, waiting for transfers between devices: 80.3 us -> 31.8 us  [rotated(): return lax.ppermute(shard, axis, pairs)]
    ppermute x10 -> x18, starting transfers between devices: 16.4 us -> 30.9 us  [rotated(): return lax.ppermute(shard, axis, pairs)]
    all_gather x1, waiting for transfers between devices: 0.01 us -> 12.8 us  [body(): raw_rows = lax.all_gather(hidden_in, HEAD, axis=0, tiled=True)]
    reduce_scatter x1, waiting for transfers between devices: 84 us -> 81 us  [body(): lax.psum_scatter(partial_value, HEAD, scatter_dimension=0, tiled=True)]
    dynamic_update_slice x10 -> x20, local copies, waits for them, and re-layouts: 8.69 us -> 9.41 us  [placed(): lax.dynamic_update_index_in_dim(stacked, part, (me + i) % count, 0)]
  transfers between devices with their start and end apart: 13 -> 21, of which waited for: 5 -> 7; matrix products, arithmetic and copies ran while one was open for 11% -> 17% of each run, Pallas kernels for 0% -> 0%
where the time goes in v3:
time: 244 us; the launch traced here: 243 us
  waiting for transfers between devices  126 us (52%)
  starting transfers between devices  35.3 us (14%)
  other arithmetic  26.9 us (11%)
  matrix products  20.6 us (8%)
  local copies, waits for them, and re-layouts  20.3 us (8%)
  between operations  14 us (6%)
    reduce_scatter x1, waiting for transfers between devices, body(): lax.psum_scatter(partial_value, HEAD, scatter_dimension=0, tiled=True)  81 us
    ppermute x18, waiting for transfers between devices, rotated(): return lax.ppermute(shard, axis, pairs)  31.8 us
    ppermute x18, starting transfers between devices, rotated(): return lax.ppermute(shard, axis, pairs)  30.9 us
    all_gather x1, waiting for transfers between devices, body(): raw_rows = lax.all_gather(hidden_in, HEAD, axis=0, tiled=True)  12.8 us
    dynamic_update_slice x20, local copies, waits for them, and re-layouts, placed(): lax.dynamic_update_index_in_dim(stacked, part, (me + i) % count, 0)  9.41 us
    reduce_sum x4, other arithmetic, root_mean_scale(): mean_sq = jnp.mean(values * values, axis=-1, keepdims=True)  9.17 us
    dot_general x1, matrix products, body(): projected = jnp.dot(normed, w_in, preferred_element_type=jnp.float32)  8.35 us
    dot_general x1, matrix products, body(): jnp.dot(attended, out_weight, preferred_element_type=jnp.float32)  5.89 us
  transfers between devices with their start and end apart: 21, of which 7 were waited for; matrix products, arithmetic and copies ran while one was open for 17% of the time, Pallas kernels for 0%

profile of v3, /device:TPU:0, one launch (start us, length us, event | category | flops | bytes accessed | tf_op | source)
XLA Modules:
  0.0 243.4 jit_solution(12072345692120334166)
XLA Ops:
  6.5 0.7 all-gather.2.cloned.1.call-update
  7.3 1.0 constant_dynamic-update-slice_fusion.2
  8.3 1.0 constant_dynamic-update-slice_fusion.1
  9.3 1.0 constant_dynamic-update-slice_fusion
  10.2 3.4 %collective-permute-start = (bf16[672,512]{1,0:T(8,128)(2,1)S(1)}, bf16[672,512]{1,0:T(8,128)(2,1)S(1)}, u32[]{:S(2)}, u32[]{:S(2)}) collective-permute-start(bf16[672,512]{1,0:T(8,128)(2,1)S(1)} %constant_dynamic-update-slice_fusion), channel_id=1, source_target_pairs={{0,16},{16,0},{1,17},{17,1},{2,18},{18,2},{3,19},{19,3},{4,20},{20... | collective-permute-start | bytes 2064392 | tf_op jit(solution)/shard_map/ppermute | solution.py:27
  13.6 2.8 %collective-permute-start.1 = (bf16[672,512]{1,0:T(8,128)(2,1)S(1)}, bf16[672,512]{1,0:T(8,128)(2,1)S(1)}, u32[]{:S(2)}, u32[]{:S(2)}) collective-permute-start(bf16[672,512]{1,0:T(8,128)(2,1)S(1)} %constant_dynamic-update-slice_fusion), channel_id=1, source_target_pairs={{0,96},{32,0},{64,32},{96,64},{1,97},{33,1},{65,33},{97,65},{2,98}... | collective-permute-start | bytes 2064392 | tf_op jit(solution)/shard_map/ppermute | solution.py:27
  16.5 0.1 broadcast_in_dim.113.clone
  16.6 1.9 and_and_fusion.1
  18.5 3.0 %multiply_cosine_fusion = (f32[1024,64]{1,0:T(8,128)}, f32[1024,64]{1,0:T(8,128)}) fusion(f32[64]{0:T(128)S(1)} %multiply_power_fusion, f32[1024]{0:T(1024)S(1)} %get-tuple-element.26), kind=kLoop, calls=%fused_computation.42 | loop fusion | flops 65536 | bytes 528640 | tf_op jit(solution)/shard_map/cos | solution.py:67
  21.5 1.9 and_and_fusion
  23.4 10.8 %collective-permute-done.3 = bf16[672,512]{1,0:T(8,128)(2,1)S(1)} collective-permute-done((bf16[672,512]{1,0:T(8,128)(2,1)S(1)}, bf16[672,512]{1,0:T(8,128)(2,1)S(1)}, u32[]{:S(2)}, u32[]{:S(2)}) %collective-permute-start.3) | collective-permute-done | bytes 688160 | tf_op jit(solution)/shard_map/ppermute | solution.py:27
  34.4 3.3 %collective-permute-start.5 = (bf16[336,512]{1,0:T(8,128)(2,1)S(1)}, bf16[336,512]{1,0:T(8,128)(2,1)S(1)}, u32[]{:S(2)}, u32[]{:S(2)}) collective-permute-start(bf16[336,512]{1,0:T(8,128)(2,1)S(1)} %slice.106), channel_id=1, source_target_pairs={{0,96},{32,0},{64,32},{96,64},{1,97},{33,1},{65,33},{97,65},{2,98}... | collective-permute-start | bytes 1032200 | tf_op jit(solution)/shard_map/ppermute | solution.py:27
  37.6 2.2 collective-permute-start.2
  40.1 2.8 %broadcast_in_dim.112 = bf16[4,2,672,512]{3,2,1,0:T(8,128)(2,1)} broadcast(bf16[]{:T(256)} %constant.188.clone.1), dimensions={} | broadcast | bytes 5505026 | tf_op jit(solution)/shard_map/broadcast_in_dim | solution.py:31
  42.9 1.2 constant_dynamic-update-slice_fusion.10
  44.3 2.2 collective-permute-done.4
  46.6 12.0 %collective-permute-done.6 = bf16[672,512]{1,0:T(8,128)(2,1)S(1)} collective-permute-done((bf16[672,512]{1,0:T(8,128)(2,1)S(1)}, bf16[672,512]{1,0:T(8,128)(2,1)S(1)}, u32[]{:S(2)}, u32[]{:S(2)}) %collective-permute-start.6) | collective-permute-done | bytes 688160 | tf_op jit(solution)/shard_map/ppermute | solution.py:27
  58.8 3.5 %collective-permute-start.8 = (bf16[336,512]{1,0:T(8,128)(2,1)S(1)}, bf16[336,512]{1,0:T(8,128)(2,1)S(1)}, u32[]{:S(2)}, u32[]{:S(2)}) collective-permute-start(bf16[336,512]{1,0:T(8,128)(2,1)S(1)} %slice.108), channel_id=1, source_target_pairs={{0,96},{32,0},{64,32},{96,64},{1,97},{33,1},{65,33},{97,65},{2,98}... | collective-permute-start | bytes 1032200 | tf_op jit(solution)/shard_map/ppermute | solution.py:27
  62.3 1.2 constant_dynamic-update-slice_fusion.9
  63.6 3.9 %collective-permute-done.7 = bf16[336,512]{1,0:T(8,128)(2,1)S(1)} collective-permute-done((bf16[336,512]{1,0:T(8,128)(2,1)S(1)}, bf16[336,512]{1,0:T(8,128)(2,1)S(1)}, u32[]{:S(2)}, u32[]{:S(2)}) %collective-permute-start.7) | collective-permute-done | bytes 344096 | tf_op jit(solution)/shard_map/ppermute | solution.py:27
  67.5 1.2 constant_dynamic-update-slice_fusion.8
  68.7 1.2 constant_dynamic-update-slice_fusion.7
  69.9 12.8 %all-gather.2.cloned.1.call-done = bf16[1024,5376]{1,0:T(8,128)(2,1)} async-done(((bf16[64,5376]{1,0:T(8,128)(2,1)}), bf16[1024,5376]{1,0:T(8,128)(2,1)}) %all-gather.2.cloned.1.call-update) | async-done | bytes 11010064 | tf_op jit(solution)/shard_map/all_gather | solution.py:96
  82.7 6.5 %fusion = f32[1024]{0:T(1024)S(1)} fusion(bf16[1024,5376]{1,0:T(8,128)(2,1)} %all-gather.2.cloned.1.call-done), kind=kLoop, calls=%fused_computation.2 | loop fusion | flops 16514048 | bytes 11014144 | tf_op jit(solution)/shard_map/reduce_sum | solution.py:58
  89.2 0.8 copy-done
  89.9 8.3 %fusion.3 = f32[1024,512]{1,0:T(8,128)S(1)} fusion(bf16[5376,512]{1,0:T(8,128)(2,1)} %bitcast.8, bf16[1024,5376]{1,0:T(8,128)(2,1)S(1)} %copy-done, f32[5376]{0:T(1024)S(1)} %copy-done.13, f32[1024]{0:T(1024)S(1)} %add_rsqrt_fusion.2), kind=kOutput, calls=%fused_computation.6 | convolution fusion | flops 5659164672 | bytes 18637824 | tf_op jit(solution)/shard_map/dot_general | solution.py:99
  98.3 0.2 multiply_reduce_fusion.1
  98.6 0.1 fusion.53
  98.8 1.6 collective-permute-start.13
  100.3 1.8 collective-permute-start.10
  102.2 1.7 collective-permute-start.11
  103.9 0.2 multiply_bitcast_fusion
  104.1 2.4 fusion.48
  106.6 1.0 pad_maximum_fusion
  107.5 4.4 %collective-permute-start.9 = (bf16[2,1024,128]{2,1,0:T(8,128)(2,1)}, bf16[2,1024,128]{2,1,0:T(8,128)(2,1)}, u32[]{:S(2)}, u32[]{:S(2)}) collective-permute-start(bf16[2,1024,128]{2,1,0:T(8,128)(2,1)} %pad_maximum_fusion), channel_id=1, source_target_pairs={{0,16},{16,32},{32,48},{48,64},{64,80},{80,96},{96,112},{1,17},{17... | collective-permute-start | bytes 1572872 | tf_op jit(solution)/shard_map/ppermute | solution.py:21
  111.9 0.5 reshape.338
  112.5 1.2 multiply_reduce_fusion
  113.7 0.2 copy.21
  113.9 1.0 bitcast_dynamic-update-slice_fusion.11
  115.0 0.3 fusion.25
  115.3 0.5 multiply_subtract_fusion
  115.8 0.3 fusion.26
  116.2 0.9 slice.120
  117.2 0.9 slice.121
  118.2 3.5 %collective-permute-start.15 = (bf16[16,5376]{1,0:T(8,128)(2,1)S(1)}, bf16[16,5376]{1,0:T(8,128)(2,1)S(1)}, u32[]{:S(2)}, u32[]{:S(2)}) collective-permute-start(bf16[16,5376]{1,0:T(8,128)(2,1)S(1)} %slice.121), channel_id=1, source_target_pairs={{0,96},{32,0},{64,32},{96,64},{1,97},{33,1},{65,33},{97,65},{2,98}... | collective-permute-start | bytes 516104 | tf_op jit(solution)/shard_map/ppermute | solution.py:27
  121.7 3.2 %collective-permute-start.12 = (bf16[32,5376]{1,0:T(8,128)(2,1)}, bf16[32,5376]{1,0:T(8,128)(2,1)S(1)}, u32[]{:S(2)}, u32[]{:S(2)}) collective-permute-start(bf16[32,5376]{1,0:T(8,128)(2,1)} %collective-permute-done.10), channel_id=1, source_target_pairs={{0,96},{32,0},{64,32},{96,64},{1,97},{33,1},{65,33},{97,65},{2,98}... | collective-permute-start | bytes 1032200 | tf_op jit(solution)/shard_map/ppermute | solution.py:27
  125.0 1.0 bitcast_dynamic-update-slice_fusion.7
  126.0 1.0 bitcast_dynamic-update-slice_fusion.9
  127.0 1.0 bitcast_dynamic-update-slice_fusion.10
  128.1 0.2 broadcast_in_dim.125
  128.4 0.5 copy-done.5
  129.1 1.2 maximum_maximum_fusion
  130.3 1.2 fusion.7
  131.5 1.2 fusion.9
  132.8 2.0 fusion.19
  134.8 1.2 fusion.8
  136.0 1.2 fusion.10
  137.2 2.0 fusion.22
  139.4 3.5 %collective-permute-start.18 = (bf16[16,5376]{1,0:T(8,128)(2,1)S(1)}, bf16[16,5376]{1,0:T(8,128)(2,1)S(1)}, u32[]{:S(2)}, u32[]{:S(2)}) collective-permute-start(bf16[16,5376]{1,0:T(8,128)(2,1)S(1)} %slice.123), channel_id=1, source_target_pairs={{0,96},{32,0},{64,32},{96,64},{1,97},{33,1},{65,33},{97,65},{2,98}... | collective-permute-start | bytes 516104 | tf_op jit(solution)/shard_map/ppermute | solution.py:27
  143.0 2.9 %collective-permute-done.17 = bf16[16,5376]{1,0:T(8,128)(2,1)S(1)} collective-permute-done((bf16[16,5376]{1,0:T(8,128)(2,1)S(1)}, bf16[16,5376]{1,0:T(8,128)(2,1)S(1)}, u32[]{:S(2)}, u32[]{:S(2)}) %collective-permute-start.17) | collective-permute-done | bytes 172064 | tf_op jit(solution)/shard_map/ppermute | solution.py:27
  146.1 5.9 %convolution_convert_fusion = bf16[1024,5376]{1,0:T(8,128)(2,1)} fusion(bf16[256,5376]{1,0:T(8,128)(2,1)S(1)} %bitcast.134, bf16[512,256]{0,1:T(8,128)(2,1)S(1)} %bitcast.136, bf16[512,256]{0,1:T(8,128)(2,1)S(1)} %bitcast.135), kind=kOutput, calls=%fused_computation.5 | convolution fusion | flops 2825125888 | bytes 14286848 | tf_op jit(solution)/shard_map/dot_general | solution.py:164
  152.0 81.0 %reduce-scatter.2.cloned.1.call-done = bf16[64,5376]{1,0:T(8,128)(2,1)} async-done(((bf16[1024,5376]{1,0:T(8,128)(2,1)}), bf16[64,5376]{1,0:T(8,128)(2,1)}) %reduce-scatter.2.cloned.1.call-update) | async-done | bytes 688144 | tf_op jit(solution)/shard_map/reduce_scatter | solution.py:167
  233.0 1.3 fusion.15
  234.3 2.3 fusion.18
  (90 shorter events, 2.0 us)
Async XLA Ops:
  6.5 76.2 %all-gather.2.cloned.1.call-start = ((), (), s32[]{:S(2)}) async-start(), calls=%async_computation.1 | async-start | bytes 11698176 | tf_op jit(solution)/shard_map/all_gather | solution.py:96
  7.3 225.7 %reduce-scatter.2.cloned.1.call-start = ((), (), s32[]{:S(2)}) async-start(), calls=%async_computation.2 | async-start | bytes 11698176 | tf_op jit(solution)/shard_map/reduce_scatter | solution.py:167
  10.2 27.4 %collective-permute-start = (bf16[672,512]{1,0:T(8,128)(2,1)S(1)}, bf16[672,512]{1,0:T(8,128)(2,1)S(1)}, u32[]{:S(2)}, u32[]{:S(2)}) collective-permute-start(bf16[672,512]{1,0:T(8,128)(2,1)S(1)} %constant_dynamic-update-slice_fusion), channel_id=1, source_target_pairs={{0,16},{16,0},{1,17},{17,1},{2,18},{18,2},{3,19},{19,3},{4,20},{20... | collective-permute-start | bytes 2064392 | tf_op jit(solution)/shard_map/ppermute | solution.py:27
  13.6 20.7 %collective-permute-start.1 = (bf16[672,512]{1,0:T(8,128)(2,1)S(1)}, bf16[672,512]{1,0:T(8,128)(2,1)S(1)}, u32[]{:S(2)}, u32[]{:S(2)}) collective-permute-start(bf16[672,512]{1,0:T(8,128)(2,1)S(1)} %constant_dynamic-update-slice_fusion), channel_id=1, source_target_pairs={{0,96},{32,0},{64,32},{96,64},{1,97},{33,1},{65,33},{97,65},{2,98}... | collective-permute-start | bytes 2064392 | tf_op jit(solution)/shard_map/ppermute | solution.py:27
  16.4 17.8 %collective-permute-start.3 = (bf16[672,512]{1,0:T(8,128)(2,1)S(1)}, bf16[672,512]{1,0:T(8,128)(2,1)S(1)}, u32[]{:S(2)}, u32[]{:S(2)}) collective-permute-start(bf16[672,512]{1,0:T(8,128)(2,1)S(1)} %constant_dynamic-update-slice_fusion), channel_id=1, source_target_pairs={{0,32},{32,64},{64,96},{96,0},{1,33},{33,65},{65,97},{97,1},{2,34}... | collective-permute-start | bytes 2064392 | tf_op jit(solution)/shard_map/ppermute | solution.py:27
  34.2 12.2 %collective-permute-start.4 = (bf16[336,512]{1,0:T(8,128)(2,1)S(1)}, bf16[336,512]{1,0:T(8,128)(2,1)S(1)}, u32[]{:S(2)}, u32[]{:S(2)}) collective-permute-start(bf16[336,512]{1,0:T(8,128)(2,1)S(1)} %slice.105), channel_id=1, source_target_pairs={{0,32},{32,64},{64,96},{96,0},{1,33},{33,65},{65,97},{97,1},{2,34}... | collective-permute-start | bytes 1032200 | tf_op jit(solution)/shard_map/ppermute | solution.py:27
  34.4 12.1 %collective-permute-start.5 = (bf16[336,512]{1,0:T(8,128)(2,1)S(1)}, bf16[336,512]{1,0:T(8,128)(2,1)S(1)}, u32[]{:S(2)}, u32[]{:S(2)}) collective-permute-start(bf16[336,512]{1,0:T(8,128)(2,1)S(1)} %slice.106), channel_id=1, source_target_pairs={{0,96},{32,0},{64,32},{96,64},{1,97},{33,1},{65,33},{97,65},{2,98}... | collective-permute-start | bytes 1032200 | tf_op jit(solution)/shard_map/ppermute | solution.py:27
  37.6 21.1 %collective-permute-start.2 = (bf16[672,512]{1,0:T(8,128)(2,1)S(1)}, bf16[672,512]{1,0:T(8,128)(2,1)S(1)}, u32[]{:S(2)}, u32[]{:S(2)}) collective-permute-start(bf16[672,512]{1,0:T(8,128)(2,1)S(1)} %collective-permute-done), channel_id=1, source_target_pairs={{0,96},{32,0},{64,32},{96,64},{1,97},{33,1},{65,33},{97,65},{2,98}... | collective-permute-start | bytes 2064392 | tf_op jit(solution)/shard_map/ppermute | solution.py:27
  39.9 18.8 %collective-permute-start.6 = (bf16[672,512]{1,0:T(8,128)(2,1)S(1)}, bf16[672,512]{1,0:T(8,128)(2,1)S(1)}, u32[]{:S(2)}, u32[]{:S(2)}) collective-permute-start(bf16[672,512]{1,0:T(8,128)(2,1)S(1)} %collective-permute-done), channel_id=1, source_target_pairs={{0,32},{32,64},{64,96},{96,0},{1,33},{33,65},{65,97},{97,1},{2,34}... | collective-permute-start | bytes 2064392 | tf_op jit(solution)/shard_map/ppermute | solution.py:27
  58.7 8.8 %collective-permute-start.7 = (bf16[336,512]{1,0:T(8,128)(2,1)S(1)}, bf16[336,512]{1,0:T(8,128)(2,1)S(1)}, u32[]{:S(2)}, u32[]{:S(2)}) collective-permute-start(bf16[336,512]{1,0:T(8,128)(2,1)S(1)} %slice.107), channel_id=1, source_target_pairs={{0,32},{32,64},{64,96},{96,0},{1,33},{33,65},{65,97},{97,1},{2,34}... | collective-permute-start | bytes 1032200 | tf_op jit(solution)/shard_map/ppermute | solution.py:27
  58.8 8.7 %collective-permute-start.8 = (bf16[336,512]{1,0:T(8,128)(2,1)S(1)}, bf16[336,512]{1,0:T(8,128)(2,1)S(1)}, u32[]{:S(2)}, u32[]{:S(2)}) collective-permute-start(bf16[336,512]{1,0:T(8,128)(2,1)S(1)} %slice.108), channel_id=1, source_target_pairs={{0,96},{32,0},{64,32},{96,64},{1,97},{33,1},{65,33},{97,65},{2,98}... | collective-permute-start | bytes 1032200 | tf_op jit(solution)/shard_map/ppermute | solution.py:27
  68.7 20.5 %copy-start.13 = (f32[5376]{0:T(1024)S(1)}, f32[5376]{0:T(1024)}, u32[]{:S(2)}) copy-start(f32[5376]{0:T(1024)} %param.10) | copy-start | bytes 64516
  82.7 7.3 %copy-start = (bf16[1024,5376]{1,0:T(8,128)(2,1)S(1)}, bf16[1024,5376]{1,0:T(8,128)(2,1)}, u32[]{:S(2)}) copy-start(bf16[1024,5376]{1,0:T(8,128)(2,1)} %all-gather.2.cloned.1.call-done) | copy-start | bytes 33030148
  98.3 5.6 %copy-start.11 = (f32[128]{0:T(128)S(1)}, f32[128]{0:T(128)}, u32[]{:S(2)}) copy-start(f32[128]{0:T(128)} %param.15) | copy-start | bytes 1540
  98.8 17.4 %collective-permute-start.13 = (bf16[32,5376]{1,0:T(8,128)(2,1)}, bf16[32,5376]{1,0:T(8,128)(2,1)}, u32[]{:S(2)}, u32[]{:S(2)}) collective-permute-start(bf16[32,5376]{1,0:T(8,128)(2,1)} %param.16), channel_id=1, source_target_pairs={{0,32},{32,64},{64,96},{96,0},{1,33},{33,65},{65,97},{97,1},{2,34}... | collective-permute-start | bytes 1032200 | tf_op jit(solution)/shard_map/ppermute | solution.py:27
  100.3 21.3 %collective-permute-start.10 = (bf16[32,5376]{1,0:T(8,128)(2,1)}, bf16[32,5376]{1,0:T(8,128)(2,1)}, u32[]{:S(2)}, u32[]{:S(2)}) collective-permute-start(bf16[32,5376]{1,0:T(8,128)(2,1)} %param.16), channel_id=1, source_target_pairs={{0,16},{16,0},{1,17},{17,1},{2,18},{18,2},{3,19},{19,3},{4,20},{20... | collective-permute-start | bytes 1032200 | tf_op jit(solution)/shard_map/ppermute | solution.py:27
  102.2 15.1 %collective-permute-start.11 = (bf16[32,5376]{1,0:T(8,128)(2,1)}, bf16[32,5376]{1,0:T(8,128)(2,1)}, u32[]{:S(2)}, u32[]{:S(2)}) collective-permute-start(bf16[32,5376]{1,0:T(8,128)(2,1)} %param.16), channel_id=1, source_target_pairs={{0,96},{32,0},{64,32},{96,64},{1,97},{33,1},{65,33},{97,65},{2,98}... | collective-permute-start | bytes 1032200 | tf_op jit(solution)/shard_map/ppermute | solution.py:27
  106.6 5.4 %copy-start.4 = (bf16[1,1024,64]{2,1,0:T(8,128)(2,1)}, bf16[1,1024,64]{2,1,0:T(8,128)(2,1)S(1)}, u32[]{:S(2)}) copy-start(bf16[1,1024,64]{2,1,0:T(8,128)(2,1)S(1)} %get-tuple-element.13) | copy-start | bytes 393220
  106.6 5.4 %copy-start.6 = (bf16[1,1024,64]{2,1,0:T(8,128)(2,1)}, bf16[1,1024,64]{2,1,0:T(8,128)(2,1)S(1)}, u32[]{:S(2)}) copy-start(bf16[1,1024,64]{2,1,0:T(8,128)(2,1)S(1)} %get-tuple-element.14) | copy-start | bytes 393220
  107.5 20.9 %collective-permute-start.9 = (bf16[2,1024,128]{2,1,0:T(8,128)(2,1)}, bf16[2,1024,128]{2,1,0:T(8,128)(2,1)}, u32[]{:S(2)}, u32[]{:S(2)}) collective-permute-start(bf16[2,1024,128]{2,1,0:T(8,128)(2,1)} %pad_maximum_fusion), channel_id=1, source_target_pairs={{0,16},{16,32},{32,48},{48,64},{64,80},{80,96},{96,112},{1,17},{17... | collective-permute-start | bytes 1572872 | tf_op jit(solution)/shard_map/ppermute | solution.py:21
  111.9 3.0 %copy-start.12 = (f32[128]{0:T(128)S(1)}, f32[128]{0:T(128)}, u32[]{:S(2)}) copy-start(f32[128]{0:T(128)} %param.14) | copy-start | bytes 1540
  112.5 2.8 %copy-start.8 = (f32[1024,64]{1,0:T(8,128)S(1)}, f32[1024,64]{1,0:T(8,128)}, u32[]{:S(2)}) copy-start(f32[1024,64]{1,0:T(8,128)} %get-tuple-element.15) | copy-start | bytes 786436
  113.7 1.7 copy-start.9
  117.1 11.2 %collective-permute-start.14 = (bf16[16,5376]{1,0:T(8,128)(2,1)S(1)}, bf16[16,5376]{1,0:T(8,128)(2,1)S(1)}, u32[]{:S(2)}, u32[]{:S(2)}) collective-permute-start(bf16[16,5376]{1,0:T(8,128)(2,1)S(1)} %slice.120), channel_id=1, source_target_pairs={{0,32},{32,64},{64,96},{96,0},{1,33},{33,65},{65,97},{97,1},{2,34}... | collective-permute-start | bytes 516104 | tf_op jit(solution)/shard_map/ppermute | solution.py:27
  118.2 10.2 %collective-permute-start.15 = (bf16[16,5376]{1,0:T(8,128)(2,1)S(1)}, bf16[16,5376]{1,0:T(8,128)(2,1)S(1)}, u32[]{:S(2)}, u32[]{:S(2)}) collective-permute-start(bf16[16,5376]{1,0:T(8,128)(2,1)S(1)} %slice.121), channel_id=1, source_target_pairs={{0,96},{32,0},{64,32},{96,64},{1,97},{33,1},{65,33},{97,65},{2,98}... | collective-permute-start | bytes 516104 | tf_op jit(solution)/shard_map/ppermute | solution.py:27
  121.7 17.5 %collective-permute-start.16 = (bf16[32,5376]{1,0:T(8,128)(2,1)}, bf16[32,5376]{1,0:T(8,128)(2,1)S(1)}, u32[]{:S(2)}, u32[]{:S(2)}) collective-permute-start(bf16[32,5376]{1,0:T(8,128)(2,1)} %collective-permute-done.10), channel_id=1, source_target_pairs={{0,32},{32,64},{64,96},{96,0},{1,33},{33,65},{65,97},{97,1},{2,34}... | collective-permute-start | bytes 1032200 | tf_op jit(solution)/shard_map/ppermute | solution.py:27
  121.7 17.7 %collective-permute-start.12 = (bf16[32,5376]{1,0:T(8,128)(2,1)}, bf16[32,5376]{1,0:T(8,128)(2,1)S(1)}, u32[]{:S(2)}, u32[]{:S(2)}) collective-permute-start(bf16[32,5376]{1,0:T(8,128)(2,1)} %collective-permute-done.10), channel_id=1, source_target_pairs={{0,96},{32,0},{64,32},{96,64},{1,97},{33,1},{65,33},{97,65},{2,98}... | collective-permute-start | bytes 1032200 | tf_op jit(solution)/shard_map/ppermute | solution.py:27
  128.0 1.0 copy-start.5
  128.1 1.0 copy-start.7
  128.3 2.0 copy-start.1
  132.7 2.0 copy-start.2
  139.2 6.7 %collective-permute-start.17 = (bf16[16,5376]{1,0:T(8,128)(2,1)S(1)}, bf16[16,5376]{1,0:T(8,128)(2,1)S(1)}, u32[]{:S(2)}, u32[]{:S(2)}) collective-permute-start(bf16[16,5376]{1,0:T(8,128)(2,1)S(1)} %slice.122), channel_id=1, source_target_pairs={{0,32},{32,64},{64,96},{96,0},{1,33},{33,65},{65,97},{97,1},{2,34}... | collective-permute-start | bytes 516104 | tf_op jit(solution)/shard_map/ppermute | solution.py:27
  139.4 6.6 %collective-permute-start.18 = (bf16[16,5376]{1,0:T(8,128)(2,1)S(1)}, bf16[16,5376]{1,0:T(8,128)(2,1)S(1)}, u32[]{:S(2)}, u32[]{:S(2)}) collective-permute-start(bf16[16,5376]{1,0:T(8,128)(2,1)S(1)} %slice.123), channel_id=1, source_target_pairs={{0,96},{32,0},{64,32},{96,64},{1,97},{33,1},{65,33},{97,65},{2,98}... | collective-permute-start | bytes 516104 | tf_op jit(solution)/shard_map/ppermute | solution.py:27
  152.0 82.3 %copy-start.3 = (bf16[64,5376]{1,0:T(8,128)(2,1)S(1)}, bf16[64,5376]{1,0:T(8,128)(2,1)}, u32[]{:S(2)}) copy-start(bf16[64,5376]{1,0:T(8,128)(2,1)} %param.9) | copy-start | bytes 2064388
  152.0 82.3 %copy-start.10 = (f32[5376]{0:T(1024)S(1)}, f32[5376]{0:T(1024)}, u32[]{:S(2)}) copy-start(f32[5376]{0:T(1024)} %param.17) | copy-start | bytes 64516
Sparse Core Ops, SparseCore 0:
  9.0 73.6 all-gather.1
  152.1 80.7 reduce-scatter.1

commit v4 on v3

--- a/solution.py
+++ b/solution.py
@@ -94,11 +94,11 @@
     w_in = gathered_over_ctx(jnp.concatenate([w_query, w_key, value_weight], axis=1))
 
     raw_rows = lax.all_gather(hidden_in, HEAD, axis=0, tiled=True)
+    raw_rows, w_output = lax.optimization_barrier((raw_rows, w_output))
+    out_weight = lax.all_gather(w_output, CTX, axis=0, tiled=True)
     normed = root_mean_scale(raw_rows.astype(jnp.float32), pre_gain).astype(jnp.bfloat16)
     tok_count = normed.shape[0]
     projected = jnp.dot(normed, w_in, preferred_element_type=jnp.float32)
-    projected, w_output = lax.optimization_barrier((projected, w_output))
-    out_weight = gathered_over_ctx(w_output)
     query_raw = projected[:, :q_cols]
     key_unnormed = projected[:, q_cols : q_cols + k_cols]
     value_unnormed = projected[:, q_cols + k_cols :]

time: 244 us -> 265 us (1.086)
  waiting for transfers between devices: 126 us -> 170 us
  starting transfers between devices: 35.3 us -> 20.1 us
  local copies, waits for them, and re-layouts: 20.3 us -> 12.9 us
    all_gather x0 -> x1, waiting for transfers between devices: none -> 40.1 us  [body(): out_weight = lax.all_gather(w_output, CTX, axis=0, tiled=True)]
    ppermute x18 -> x9, starting transfers between devices: 30.9 us -> 15.3 us  [rotated(): return lax.ppermute(shard, axis, pairs)]
    ppermute x1, waiting for transfers between devices: 0.01 us -> 8.5 us  [passed_along(): return lax.ppermute(shard, axis, pairs)]
    dynamic_update_slice x20 -> x10, local copies, waits for them, and re-layouts: 9.41 us -> 5.12 us  [placed(): lax.dynamic_update_index_in_dim(stacked, part, (me + i) % count, 0)]
    ppermute x18 -> x9, waiting for transfers between devices: 31.8 us -> 28.9 us  [rotated(): return lax.ppermute(shard, axis, pairs)]
  transfers between devices with their start and end apart: 21 -> 13, of which waited for: 7 -> 8; matrix products, arithmetic and copies ran while one was open for 17% -> 12% of each run, Pallas kernels for 0% -> 0%
where the time goes in v4:
time: 265 us; the launch traced here: 264 us
  waiting for transfers between devices  170 us (64%)
  other arithmetic  24.8 us (9%)
  matrix products  23 us (9%)
  starting transfers between devices  20.1 us (8%)
  between operations  13.5 us (5%)
  local copies, waits for them, and re-layouts  12.9 us (5%)
    reduce_scatter x1, waiting for transfers between devices, body(): lax.psum_scatter(partial_value, HEAD, scatter_dimension=0, tiled=True)  78.7 us
    all_gather x1, waiting for transfers between devices, body(): out_weight = lax.all_gather(w_output, CTX, axis=0, tiled=True)  40.1 us
    ppermute x9, waiting for transfers between devices, rotated(): return lax.ppermute(shard, axis, pairs)  28.9 us
    ppermute x9, starting transfers between devices, rotated(): return lax.ppermute(shard, axis, pairs)  15.3 us
    all_gather x1, waiting for transfers between devices, body(): raw_rows = lax.all_gather(hidden_in, HEAD, axis=0, tiled=True)  12.8 us
    dot_general x1, matrix products, body(): projected = jnp.dot(normed, w_in, preferred_element_type=jnp.float32)  8.82 us
    ppermute x1, waiting for transfers between devices, passed_along(): return lax.ppermute(shard, axis, pairs)  8.5 us
    reduce_sum x4, other arithmetic, root_mean_scale(): mean_sq = jnp.mean(values * values, axis=-1, keepdims=True)  7.96 us
  transfers between devices with their start and end apart: 13, of which 8 were waited for; matrix products, arithmetic and copies ran while one was open for 12% of the time, Pallas kernels for 0%

profile of v4, /device:TPU:0, one launch (start us, length us, event | category | flops | bytes accessed | tf_op | source)
XLA Modules:
  0.0 264.1 jit_solution(11606708875707510296)
XLA Ops:
  6.5 0.7 all-gather.3.cloned.1.call-update
  7.3 0.0 all-gather.5.cloned.1.call-start
  7.3 1.0 constant_dynamic-update-slice_fusion.2
  8.3 1.0 constant_dynamic-update-slice_fusion.1
  9.3 1.0 constant_dynamic-update-slice_fusion
  10.2 3.4 %collective-permute-start = (bf16[672,512]{1,0:T(8,128)(2,1)S(1)}, bf16[672,512]{1,0:T(8,128)(2,1)S(1)}, u32[]{:S(2)}, u32[]{:S(2)}) collective-permute-start(bf16[672,512]{1,0:T(8,128)(2,1)S(1)} %constant_dynamic-update-slice_fusion), channel_id=1, source_target_pairs={{0,16},{16,0},{1,17},{17,1},{2,18},{18,2},{3,19},{19,3},{4,20},{20... | collective-permute-start | bytes 2064392 | tf_op jit(solution)/shard_map/ppermute | solution.py:27
  13.6 2.8 %collective-permute-start.1 = (bf16[672,512]{1,0:T(8,128)(2,1)S(1)}, bf16[672,512]{1,0:T(8,128)(2,1)S(1)}, u32[]{:S(2)}, u32[]{:S(2)}) collective-permute-start(bf16[672,512]{1,0:T(8,128)(2,1)S(1)} %constant_dynamic-update-slice_fusion), channel_id=1, source_target_pairs={{0,96},{32,0},{64,32},{96,64},{1,97},{33,1},{65,33},{97,65},{2,98}... | collective-permute-start | bytes 2064392 | tf_op jit(solution)/shard_map/ppermute | solution.py:27
  16.5 0.1 broadcast_in_dim.78.clone
  16.6 0.1 bitcast_dynamic-update-slice_fusion.5
  16.6 1.9 and_and_fusion.1
  18.5 3.0 %multiply_cosine_fusion = (f32[1024,64]{1,0:T(8,128)}, f32[1024,64]{1,0:T(8,128)}) fusion(f32[64]{0:T(128)S(1)} %multiply_power_fusion, f32[1024]{0:T(1024)S(1)} %get-tuple-element.24), kind=kLoop, calls=%fused_computation.41 | loop fusion | flops 65536 | bytes 528640 | tf_op jit(solution)/shard_map/cos | solution.py:67
  21.6 1.9 and_and_fusion
  23.4 10.8 %collective-permute-done.3 = bf16[672,512]{1,0:T(8,128)(2,1)S(1)} collective-permute-done((bf16[672,512]{1,0:T(8,128)(2,1)S(1)}, bf16[672,512]{1,0:T(8,128)(2,1)S(1)}, u32[]{:S(2)}, u32[]{:S(2)}) %collective-permute-start.3) | collective-permute-done | bytes 688160 | tf_op jit(solution)/shard_map/ppermute | solution.py:27
  34.2 0.1 collective-permute-start.4
  34.4 3.3 %collective-permute-start.5 = (bf16[336,512]{1,0:T(8,128)(2,1)S(1)}, bf16[336,512]{1,0:T(8,128)(2,1)S(1)}, u32[]{:S(2)}, u32[]{:S(2)}) collective-permute-start(bf16[336,512]{1,0:T(8,128)(2,1)S(1)} %slice.90), channel_id=1, source_target_pairs={{0,96},{32,0},{64,32},{96,64},{1,97},{33,1},{65,33},{97,65},{2,98}... | collective-permute-start | bytes 1032200 | tf_op jit(solution)/shard_map/ppermute | solution.py:27
  37.6 2.2 collective-permute-start.2
  39.9 0.1 broadcast_in_dim.78.clone.1
  40.0 0.1 bitcast_dynamic-update-slice_fusion.3
  40.0 0.1 bitcast_dynamic-update-slice_fusion.4
  40.1 2.8 %broadcast_in_dim.77 = bf16[4,2,672,512]{3,2,1,0:T(8,128)(2,1)} broadcast(bf16[]{:T(256)} %constant.126.clone.1), dimensions={} | broadcast | bytes 5505026 | tf_op jit(solution)/shard_map/broadcast_in_dim | solution.py:31
  42.9 1.2 constant_dynamic-update-slice_fusion.6
  44.1 0.1 broadcast_in_dim.78.clone.3
  44.2 0.1 bitcast_dynamic-update-slice_fusion.1
  44.3 2.2 collective-permute-done.4
  46.5 0.1 broadcast_in_dim.78.clone.2
  46.5 0.1 fusion.26
  46.6 12.0 %collective-permute-done.6 = bf16[672,512]{1,0:T(8,128)(2,1)S(1)} collective-permute-done((bf16[672,512]{1,0:T(8,128)(2,1)S(1)}, bf16[672,512]{1,0:T(8,128)(2,1)S(1)}, u32[]{:S(2)}, u32[]{:S(2)}) %collective-permute-start.6) | collective-permute-done | bytes 688160 | tf_op jit(solution)/shard_map/ppermute | solution.py:27
  58.7 0.1 collective-permute-start.7
  58.8 3.5 %collective-permute-start.8 = (bf16[336,512]{1,0:T(8,128)(2,1)S(1)}, bf16[336,512]{1,0:T(8,128)(2,1)S(1)}, u32[]{:S(2)}, u32[]{:S(2)}) collective-permute-start(bf16[336,512]{1,0:T(8,128)(2,1)S(1)} %slice.92), channel_id=1, source_target_pairs={{0,96},{32,0},{64,32},{96,64},{1,97},{33,1},{65,33},{97,65},{2,98}... | collective-permute-start | bytes 1032200 | tf_op jit(solution)/shard_map/ppermute | solution.py:27
  62.3 1.2 constant_dynamic-update-slice_fusion.5
  63.6 3.9 %collective-permute-done.7 = bf16[336,512]{1,0:T(8,128)(2,1)S(1)} collective-permute-done((bf16[336,512]{1,0:T(8,128)(2,1)S(1)}, bf16[336,512]{1,0:T(8,128)(2,1)S(1)}, u32[]{:S(2)}, u32[]{:S(2)}) %collective-permute-start.7) | collective-permute-done | bytes 344096 | tf_op jit(solution)/shard_map/ppermute | solution.py:27
  67.5 1.2 constant_dynamic-update-slice_fusion.4
  68.7 1.2 constant_dynamic-update-slice_fusion.3
  69.9 12.8 %all-gather.3.cloned.1.call-done = bf16[1024,5376]{1,0:T(8,128)(2,1)} async-done(((bf16[64,5376]{1,0:T(8,128)(2,1)}), bf16[1024,5376]{1,0:T(8,128)(2,1)}) %all-gather.3.cloned.1.call-update) | async-done | bytes 11010064 | tf_op jit(solution)/shard_map/all_gather | solution.py:96
  82.7 6.5 %fusion = f32[1024]{0:T(1024)S(1)} fusion(bf16[1024,5376]{1,0:T(8,128)(2,1)} %all-gather.3.cloned.1.call-done), kind=kLoop, calls=%fused_computation.2 | loop fusion | flops 16514048 | bytes 11014144 | tf_op jit(solution)/shard_map/reduce_sum | solution.py:58
  89.2 0.8 copy-done
  89.9 8.8 %fusion.3 = f32[1024,512]{0,1:T(8,128)S(1)} fusion(bf16[5376,512]{1,0:T(8,128)(2,1)} %bitcast.8, bf16[1024,5376]{1,0:T(8,128)(2,1)S(1)} %copy-done, f32[5376]{0:T(1024)S(1)} %copy-done.10, f32[1024]{0:T(1024)S(1)} %add_rsqrt_fusion.2), kind=kOutput, calls=%fused_computation.6 | convolution fusion | flops 5659164672 | bytes 18637824 | tf_op jit(solution)/shard_map/dot_general | solution.py:101
  98.8 0.1 multiply_reduce_fusion.1
  98.9 0.1 slice.99
  99.0 0.1 multiply_reduce_fusion
  99.1 0.4 copy-done.9
  99.4 0.1 multiply_bitcast_fusion
  99.6 1.2 fusion.45
  100.7 0.8 pad_maximum_fusion
  101.6 4.6 %collective-permute-start.9 = (bf16[2,1024,128]{1,2,0:T(8,128)(2,1)}, bf16[2,1024,128]{1,2,0:T(8,128)(2,1)}, u32[]{:S(2)}, u32[]{:S(2)}) collective-permute-start(bf16[2,1024,128]{1,2,0:T(8,128)(2,1)} %pad_maximum_fusion), channel_id=1, source_target_pairs={{0,16},{16,32},{32,48},{48,64},{64,80},{80,96},{96,112},{1,17},{17... | collective-permute-start | bytes 1572872 | tf_op jit(solution)/shard_map/ppermute | solution.py:21
  106.1 0.3 copy.10
  106.5 0.0 all-gather.5.cloned.1.call-update
  106.5 0.3 reduce-scatter.2.cloned.1.call-start
  106.8 1.0 multiply_multiply_fusion
  107.8 0.5 multiply_subtract_fusion
  108.3 0.3 fusion.25
  108.7 8.5 %collective-permute-done.9 = bf16[2,1024,128]{1,2,0:T(8,128)(2,1)} collective-permute-done((bf16[2,1024,128]{1,2,0:T(8,128)(2,1)}, bf16[2,1024,128]{1,2,0:T(8,128)(2,1)}, u32[]{:S(2)}, u32[]{:S(2)}) %collective-permute-start.9) | collective-permute-done | bytes 524320 | tf_op jit(solution)/shard_map/ppermute | solution.py:21
  117.2 1.1 maximum_maximum_fusion
  118.4 1.3 fusion.7
  119.7 1.3 fusion.8
  120.9 1.2 fusion.9
  122.2 1.2 fusion.10
  123.4 2.0 fusion.19
  125.4 2.0 fusion.22
  127.4 40.1 %all-gather.5.cloned.1.call-done = bf16[256,5376]{1,0:T(8,128)(2,1)} async-done(((bf16[32,5376]{1,0:T(8,128)(2,1)}), bf16[256,5376]{1,0:T(8,128)(2,1)}) %all-gather.5.cloned.1.call-update) | async-done | bytes 2752528 | tf_op jit(solution)/shard_map/all_gather | solution.py:98
  167.6 7.7 %convolution_convert_fusion = bf16[1024,5376]{1,0:T(8,128)(2,1)} fusion(bf16[256,5376]{1,0:T(8,128)(2,1)} %all-gather.5.cloned.1.call-done, bf16[512,256]{0,1:T(8,128)(2,1)S(1)} %bitcast.111, bf16[512,256]{0,1:T(8,128)(2,1)S(1)} %bitcast.110), kind=kOutput, calls=%fused_computation.5 | convolution fusion | flops 2825125888 | bytes 14286848 | tf_op jit(solution)/shard_map/dot_general | solution.py:164
  175.3 78.7 %reduce-scatter.2.cloned.1.call-done = bf16[64,5376]{1,0:T(8,128)(2,1)} async-done(((bf16[1024,5376]{1,0:T(8,128)(2,1)}), bf16[64,5376]{1,0:T(8,128)(2,1)}) %reduce-scatter.2.cloned.1.call-update) | async-done | bytes 688144 | tf_op jit(solution)/shard_map/reduce_scatter | solution.py:167
  254.0 1.3 fusion.15
  255.3 2.3 fusion.18
  (48 shorter events, 0.4 us)
Async XLA Ops:
  6.5 76.2 %all-gather.3.cloned.1.call-start = ((), (), s32[]{:S(2)}) async-start(), calls=%async_computation.1 | async-start | bytes 11698176 | tf_op jit(solution)/shard_map/all_gather | solution.py:96
  7.3 160.3 %all-gather.5.cloned.1.call-start = ((), (), s32[]{:S(2)}) async-start(), calls=%async_computation.2 | async-start | bytes 3096576 | tf_op jit(solution)/shard_map/all_gather | solution.py:98
  10.2 27.4 %collective-permute-start = (bf16[672,512]{1,0:T(8,128)(2,1)S(1)}, bf16[672,512]{1,0:T(8,128)(2,1)S(1)}, u32[]{:S(2)}, u32[]{:S(2)}) collective-permute-start(bf16[672,512]{1,0:T(8,128)(2,1)S(1)} %constant_dynamic-update-slice_fusion), channel_id=1, source_target_pairs={{0,16},{16,0},{1,17},{17,1},{2,18},{18,2},{3,19},{19,3},{4,20},{20... | collective-permute-start | bytes 2064392 | tf_op jit(solution)/shard_map/ppermute | solution.py:27
  13.6 20.7 %collective-permute-start.1 = (bf16[672,512]{1,0:T(8,128)(2,1)S(1)}, bf16[672,512]{1,0:T(8,128)(2,1)S(1)}, u32[]{:S(2)}, u32[]{:S(2)}) collective-permute-start(bf16[672,512]{1,0:T(8,128)(2,1)S(1)} %constant_dynamic-update-slice_fusion), channel_id=1, source_target_pairs={{0,96},{32,0},{64,32},{96,64},{1,97},{33,1},{65,33},{97,65},{2,98}... | collective-permute-start | bytes 2064392 | tf_op jit(solution)/shard_map/ppermute | solution.py:27
  16.4 17.8 %collective-permute-start.3 = (bf16[672,512]{1,0:T(8,128)(2,1)S(1)}, bf16[672,512]{1,0:T(8,128)(2,1)S(1)}, u32[]{:S(2)}, u32[]{:S(2)}) collective-permute-start(bf16[672,512]{1,0:T(8,128)(2,1)S(1)} %constant_dynamic-update-slice_fusion), channel_id=1, source_target_pairs={{0,32},{32,64},{64,96},{96,0},{1,33},{33,65},{65,97},{97,1},{2,34}... | collective-permute-start | bytes 2064392 | tf_op jit(solution)/shard_map/ppermute | solution.py:27
  34.2 12.2 %collective-permute-start.4 = (bf16[336,512]{1,0:T(8,128)(2,1)S(1)}, bf16[336,512]{1,0:T(8,128)(2,1)S(1)}, u32[]{:S(2)}, u32[]{:S(2)}) collective-permute-start(bf16[336,512]{1,0:T(8,128)(2,1)S(1)} %slice.89), channel_id=1, source_target_pairs={{0,32},{32,64},{64,96},{96,0},{1,33},{33,65},{65,97},{97,1},{2,34}... | collective-permute-start | bytes 1032200 | tf_op jit(solution)/shard_map/ppermute | solution.py:27
  34.4 12.1 %collective-permute-start.5 = (bf16[336,512]{1,0:T(8,128)(2,1)S(1)}, bf16[336,512]{1,0:T(8,128)(2,1)S(1)}, u32[]{:S(2)}, u32[]{:S(2)}) collective-permute-start(bf16[336,512]{1,0:T(8,128)(2,1)S(1)} %slice.90), channel_id=1, source_target_pairs={{0,96},{32,0},{64,32},{96,64},{1,97},{33,1},{65,33},{97,65},{2,98}... | collective-permute-start | bytes 1032200 | tf_op jit(solution)/shard_map/ppermute | solution.py:27
  37.6 21.1 %collective-permute-start.2 = (bf16[672,512]{1,0:T(8,128)(2,1)S(1)}, bf16[672,512]{1,0:T(8,128)(2,1)S(1)}, u32[]{:S(2)}, u32[]{:S(2)}) collective-permute-start(bf16[672,512]{1,0:T(8,128)(2,1)S(1)} %collective-permute-done), channel_id=1, source_target_pairs={{0,96},{32,0},{64,32},{96,64},{1,97},{33,1},{65,33},{97,65},{2,98}... | collective-permute-start | bytes 2064392 | tf_op jit(solution)/shard_map/ppermute | solution.py:27
  39.9 18.8 %collective-permute-start.6 = (bf16[672,512]{1,0:T(8,128)(2,1)S(1)}, bf16[672,512]{1,0:T(8,128)(2,1)S(1)}, u32[]{:S(2)}, u32[]{:S(2)}) collective-permute-start(bf16[672,512]{1,0:T(8,128)(2,1)S(1)} %collective-permute-done), channel_id=1, source_target_pairs={{0,32},{32,64},{64,96},{96,0},{1,33},{33,65},{65,97},{97,1},{2,34}... | collective-permute-start | bytes 2064392 | tf_op jit(solution)/shard_map/ppermute | solution.py:27
  58.7 8.8 %collective-permute-start.7 = (bf16[336,512]{1,0:T(8,128)(2,1)S(1)}, bf16[336,512]{1,0:T(8,128)(2,1)S(1)}, u32[]{:S(2)}, u32[]{:S(2)}) collective-permute-start(bf16[336,512]{1,0:T(8,128)(2,1)S(1)} %slice.91), channel_id=1, source_target_pairs={{0,32},{32,64},{64,96},{96,0},{1,33},{33,65},{65,97},{97,1},{2,34}... | collective-permute-start | bytes 1032200 | tf_op jit(solution)/shard_map/ppermute | solution.py:27
  58.8 8.7 %collective-permute-start.8 = (bf16[336,512]{1,0:T(8,128)(2,1)S(1)}, bf16[336,512]{1,0:T(8,128)(2,1)S(1)}, u32[]{:S(2)}, u32[]{:S(2)}) collective-permute-start(bf16[336,512]{1,0:T(8,128)(2,1)S(1)} %slice.92), channel_id=1, source_target_pairs={{0,96},{32,0},{64,32},{96,64},{1,97},{33,1},{65,33},{97,65},{2,98}... | collective-permute-start | bytes 1032200 | tf_op jit(solution)/shard_map/ppermute | solution.py:27
  68.7 20.5 %copy-start.10 = (f32[5376]{0:T(1024)S(1)}, f32[5376]{0:T(1024)}, u32[]{:S(2)}) copy-start(f32[5376]{0:T(1024)} %param.10) | copy-start | bytes 64516
  82.7 7.3 %copy-start = (bf16[1024,5376]{1,0:T(8,128)(2,1)S(1)}, bf16[1024,5376]{1,0:T(8,128)(2,1)}, u32[]{:S(2)}) copy-start(bf16[1024,5376]{1,0:T(8,128)(2,1)} %all-gather.3.cloned.1.call-done) | copy-start | bytes 33030148
  98.8 0.7 copy-start.9
  99.5 8.3 %copy-start.4 = (f32[1024,64]{1,0:T(8,128)S(1)}, f32[1024,64]{1,0:T(8,128)}, u32[]{:S(2)}) copy-start(f32[1024,64]{1,0:T(8,128)} %get-tuple-element.13) | copy-start | bytes 786436
  99.5 8.3 %copy-start.5 = (f32[1024,64]{1,0:T(8,128)S(1)}, f32[1024,64]{1,0:T(8,128)}, u32[]{:S(2)}) copy-start(f32[1024,64]{1,0:T(8,128)} %get-tuple-element.14) | copy-start | bytes 786436
  100.7 5.4 %copy-start.6 = (bf16[1,1024,64]{1,2,0:T(8,128)(2,1)}, bf16[1,1024,64]{1,2,0:T(8,128)(2,1)S(1)}, u32[]{:S(2)}) copy-start(bf16[1,1024,64]{1,2,0:T(8,128)(2,1)S(1)} %get-tuple-element.12) | copy-start | bytes 393220
  101.6 15.6 %collective-permute-start.9 = (bf16[2,1024,128]{1,2,0:T(8,128)(2,1)}, bf16[2,1024,128]{1,2,0:T(8,128)(2,1)}, u32[]{:S(2)}, u32[]{:S(2)}) collective-permute-start(bf16[2,1024,128]{1,2,0:T(8,128)(2,1)} %pad_maximum_fusion), channel_id=1, source_target_pairs={{0,16},{16,32},{32,48},{48,64},{64,80},{80,96},{96,112},{1,17},{17... | collective-permute-start | bytes 1572872 | tf_op jit(solution)/shard_map/ppermute | solution.py:21
  106.5 147.4 %reduce-scatter.2.cloned.1.call-start = ((), (), s32[]{:S(2)}) async-start(), calls=%async_computation.3 | async-start | bytes 11698176 | tf_op jit(solution)/shard_map/reduce_scatter | solution.py:167
  107.8 9.4 %copy-start.7 = (bf16[1,1024,64]{1,2,0:T(8,128)(2,1)S(1)}, bf16[1,1024,64]{1,2,0:T(8,128)(2,1)}, u32[]{:S(2)}) copy-start(bf16[1,1024,64]{1,2,0:T(8,128)(2,1)} %copy-done.6) | copy-start | bytes 393220
  108.3 10.0 %copy-start.1 = (pred[512,1536]{0,1:T(8,128)(4,1)S(1)}, pred[512,1536]{0,1:T(8,128)(4,1)}, u32[]{:S(2)}) copy-start(pred[512,1536]{0,1:T(8,128)(4,1)} %and_and_fusion.1) | copy-start | bytes 2359300
  118.4 1.3 copy-start.2
  175.2 80.1 %copy-start.3 = (bf16[64,5376]{1,0:T(8,128)(2,1)S(1)}, bf16[64,5376]{1,0:T(8,128)(2,1)}, u32[]{:S(2)}) copy-start(bf16[64,5376]{1,0:T(8,128)(2,1)} %param.9) | copy-start | bytes 2064388
  175.2 80.1 %copy-start.8 = (f32[5376]{0:T(1024)S(1)}, f32[5376]{0:T(1024)}, u32[]{:S(2)}) copy-start(f32[5376]{0:T(1024)} %param.17) | copy-start | bytes 64516
Sparse Core Ops, SparseCore 0:
  9.0 73.6 all-gather.2
  106.6 60.8 all-gather.4
  175.4 78.5 reduce-scatter.1

commit v5 on v4

--- a/solution.py
+++ b/solution.py
@@ -2,6 +2,7 @@
 import jax.numpy as jnp
 from jax import lax
 from jax.sharding import Mesh, PartitionSpec as P
+
 
 HEAD_SIZE = 128
 WINDOW_SPAN = 1024
@@ -52,6 +53,14 @@
     pairs = [placed([a, b], cy, 2) for a, b in zip(own, partner)]
     ring = placed(pairs, cx, 4)
     return ring.reshape((8 * piece.shape[0],) + piece.shape[1:])
+
+
+def gathered_directly(piece, axis):
+    count = lax.axis_size(axis)
+    me = lax.axis_index(axis)
+    parts = [piece] + [rotated(piece, axis, by) for by in range(count - 1, 0, -1)]
+    stacked = placed(parts, me, count)
+    return stacked.reshape((count * piece.shape[0],) + piece.shape[1:])
 
 
 def root_mean_scale(values, scaling):
@@ -77,7 +86,7 @@
     )
 
 
-def body(
+def layer(
     hidden_in,
     pre_gain,
     w_query,
@@ -93,11 +102,11 @@
     k_cols = w_key.shape[1]
     w_in = gathered_over_ctx(jnp.concatenate([w_query, w_key, value_weight], axis=1))
 
+    w_in, w_output = lax.optimization_barrier((w_in, w_output))
+    out_weight = gathered_directly(w_output, CTX)
     raw_rows = lax.all_gather(hidden_in, HEAD, axis=0, tiled=True)
-    raw_rows, w_output = lax.optimization_barrier((raw_rows, w_output))
-    out_weight = lax.all_gather(w_output, CTX, axis=0, tiled=True)
+    tok_count = raw_rows.shape[0]
     normed = root_mean_scale(raw_rows.astype(jnp.float32), pre_gain).astype(jnp.bfloat16)
-    tok_count = normed.shape[0]
     projected = jnp.dot(normed, w_in, preferred_element_type=jnp.float32)
     query_raw = projected[:, :q_cols]
     key_unnormed = projected[:, q_cols : q_cols + k_cols]
@@ -179,7 +188,7 @@
     rows_spec = P(CTX + HEAD, None)
     cols_spec = P(CTX, HEAD)
     return jax.shard_map(
-        body,
+        layer,
         mesh=view,
         in_specs=(
             rows_spec,

time: 265 us -> 256 us (0.966)
  waiting for transfers between devices: 170 us -> 156 us
  starting transfers between devices: 20.1 us -> 27.1 us
  local copies, waits for them, and re-layouts: 12.9 us -> 9.55 us
    all_gather x2 -> x1, waiting for transfers between devices: 52.9 us -> 0.02 us  [layer(): raw_rows = lax.all_gather(hidden_in, HEAD, axis=0, tiled=True)]
    ppermute x9 -> x16, waiting for transfers between devices: 28.9 us -> 70.6 us  [rotated(): return lax.ppermute(shard, axis, pairs)]
    ppermute x9 -> x16, starting transfers between devices: 15.3 us -> 24.9 us  [rotated(): return lax.ppermute(shard, axis, pairs)]
    ppermute x1, waiting for transfers between devices: 8.5 us -> 2.09 us  [passed_along(): return lax.ppermute(shard, axis, pairs)]
    reduce_scatter x1, waiting for transfers between devices: 78.7 us -> 82.7 us  [layer(): lax.psum_scatter(partial_value, HEAD, scatter_dimension=0, tiled=True)]
    dynamic_update_slice x10 -> x18, local copies, waits for them, and re-layouts: 5.12 us -> 1.14 us  [placed(): lax.dynamic_update_index_in_dim(stacked, part, (me + i) % count, 0)]
  transfers between devices with their start and end apart: 13 -> 19, of which waited for: 8 -> 9; matrix products, arithmetic and copies ran while one was open for 12% -> 7% of each run, Pallas kernels for 0% -> 0%
where the time goes in v5:
time: 256 us
  waiting for transfers between devices  156 us (61%)
  starting transfers between devices  27.1 us (11%)
  other arithmetic  25.6 us (10%)
  matrix products  23.2 us (9%)
  between operations  14 us (5%)
  local copies, waits for them, and re-layouts  9.55 us (4%)
    reduce_scatter x1, waiting for transfers between devices, layer(): lax.psum_scatter(partial_value, HEAD, scatter_dimension=0, tiled=True)  82.7 us
    ppermute x16, waiting for transfers between devices, rotated(): return lax.ppermute(shard, axis, pairs)  70.6 us
    ppermute x16, starting transfers between devices, rotated(): return lax.ppermute(shard, axis, pairs)  24.9 us
    dot_general x1, matrix products, layer(): projected = jnp.dot(normed, w_in, preferred_element_type=jnp.float32)  10.7 us
    reduce_sum x4, other arithmetic, root_mean_scale(): mean_sq = jnp.mean(values * values, axis=-1, keepdims=True)  7.82 us
    dot_general x1, matrix products, layer(): jnp.dot(attended, out_weight, preferred_element_type=jnp.float32)  5.86 us
  transfers between devices with their start and end apart: 19, of which 9 were waited for; matrix products, arithmetic and copies ran while one was open for 7% of the time, Pallas kernels for 0%

profile of v5, /device:TPU:0, one launch (start us, length us, event | category | flops | bytes accessed | tf_op | source)
XLA Modules:
  0.0 255.6 jit_solution(5726546504122908656)
XLA Ops:
  6.5 0.7 all-gather.2.cloned.1.call-update
  7.3 1.0 constant_dynamic-update-slice_fusion.2
  8.3 1.0 constant_dynamic-update-slice_fusion.1
  9.3 1.0 constant_dynamic-update-slice_fusion
  10.2 3.4 %collective-permute-start = (bf16[672,512]{1,0:T(8,128)(2,1)S(1)}, bf16[672,512]{1,0:T(8,128)(2,1)S(1)}, u32[]{:S(2)}, u32[]{:S(2)}) collective-permute-start(bf16[672,512]{1,0:T(8,128)(2,1)S(1)} %constant_dynamic-update-slice_fusion), channel_id=1, source_target_pairs={{0,16},{16,0},{1,17},{17,1},{2,18},{18,2},{3,19},{19,3},{4,20},{20... | collective-permute-start | bytes 2064392 | tf_op jit(solution)/shard_map/ppermute | solution.py:28
  13.6 2.8 %collective-permute-start.1 = (bf16[672,512]{1,0:T(8,128)(2,1)S(1)}, bf16[672,512]{1,0:T(8,128)(2,1)S(1)}, u32[]{:S(2)}, u32[]{:S(2)}) collective-permute-start(bf16[672,512]{1,0:T(8,128)(2,1)S(1)} %constant_dynamic-update-slice_fusion), channel_id=1, source_target_pairs={{0,96},{32,0},{64,32},{96,64},{1,97},{33,1},{65,33},{97,65},{2,98}... | collective-permute-start | bytes 2064392 | tf_op jit(solution)/shard_map/ppermute | solution.py:28
  16.5 0.1 broadcast_in_dim.106.clone
  16.6 0.1 bitcast_dynamic-update-slice_fusion.5
  16.6 1.9 and_and_fusion.1
  18.5 3.0 %multiply_cosine_fusion = (f32[1024,64]{1,0:T(8,128)}, f32[1024,64]{1,0:T(8,128)}) fusion(f32[64]{0:T(128)S(1)} %multiply_power_fusion, f32[1024]{0:T(1024)S(1)} %fusion.46), kind=kLoop, calls=%fused_computation.41 | loop fusion | flops 65536 | bytes 528640 | tf_op jit(solution)/shard_map/cos | solution.py:76
  21.6 1.1 and_and_fusion
  22.7 11.5 %collective-permute-done.3 = bf16[672,512]{1,0:T(8,128)(2,1)S(1)} collective-permute-done((bf16[672,512]{1,0:T(8,128)(2,1)S(1)}, bf16[672,512]{1,0:T(8,128)(2,1)S(1)}, u32[]{:S(2)}, u32[]{:S(2)}) %collective-permute-start.3) | collective-permute-done | bytes 688160 | tf_op jit(solution)/shard_map/ppermute | solution.py:28
  34.2 0.1 collective-permute-start.4
  34.4 3.3 %collective-permute-start.5 = (bf16[336,512]{1,0:T(8,128)(2,1)S(1)}, bf16[336,512]{1,0:T(8,128)(2,1)S(1)}, u32[]{:S(2)}, u32[]{:S(2)}) collective-permute-start(bf16[336,512]{1,0:T(8,128)(2,1)S(1)} %slice.90), channel_id=1, source_target_pairs={{0,96},{32,0},{64,32},{96,64},{1,97},{33,1},{65,33},{97,65},{2,98}... | collective-permute-start | bytes 1032200 | tf_op jit(solution)/shard_map/ppermute | solution.py:28
  37.6 2.2 collective-permute-start.2
  39.9 0.1 broadcast_in_dim.106.clone.1
  40.0 0.1 bitcast_dynamic-update-slice_fusion.3
  40.1 0.1 bitcast_dynamic-update-slice_fusion.4
  40.1 0.5 broadcast_in_dim.105
  40.6 0.2 constant_dynamic-update-slice_fusion.6
  40.7 0.1 broadcast_in_dim.106.clone.3
  40.9 5.5 %collective-permute-done.4 = bf16[336,512]{1,0:T(8,128)(2,1)S(1)} collective-permute-done((bf16[336,512]{1,0:T(8,128)(2,1)S(1)}, bf16[336,512]{1,0:T(8,128)(2,1)S(1)}, u32[]{:S(2)}, u32[]{:S(2)}) %collective-permute-start.4) | collective-permute-done | bytes 344096 | tf_op jit(solution)/shard_map/ppermute | solution.py:28
  46.5 0.1 broadcast_in_dim.106.clone.2
  46.6 12.0 %collective-permute-done.6 = bf16[672,512]{1,0:T(8,128)(2,1)S(1)} collective-permute-done((bf16[672,512]{1,0:T(8,128)(2,1)S(1)}, bf16[672,512]{1,0:T(8,128)(2,1)S(1)}, u32[]{:S(2)}, u32[]{:S(2)}) %collective-permute-start.6) | collective-permute-done | bytes 688160 | tf_op jit(solution)/shard_map/ppermute | solution.py:28
  58.7 0.1 collective-permute-start.7
  58.8 3.3 %collective-permute-start.8 = (bf16[336,512]{1,0:T(8,128)(2,1)S(1)}, bf16[336,512]{1,0:T(8,128)(2,1)S(1)}, u32[]{:S(2)}, u32[]{:S(2)}) collective-permute-start(bf16[336,512]{1,0:T(8,128)(2,1)S(1)} %slice.92), channel_id=1, source_target_pairs={{0,96},{32,0},{64,32},{96,64},{1,97},{33,1},{65,33},{97,65},{2,98}... | collective-permute-start | bytes 1032200 | tf_op jit(solution)/shard_map/ppermute | solution.py:28
  62.1 0.2 constant_dynamic-update-slice_fusion.5
  62.3 5.1 %collective-permute-done.7 = bf16[336,512]{1,0:T(8,128)(2,1)S(1)} collective-permute-done((bf16[336,512]{1,0:T(8,128)(2,1)S(1)}, bf16[336,512]{1,0:T(8,128)(2,1)S(1)}, u32[]{:S(2)}, u32[]{:S(2)}) %collective-permute-start.7) | collective-permute-done | bytes 344096 | tf_op jit(solution)/shard_map/ppermute | solution.py:28
  67.5 0.2 constant_dynamic-update-slice_fusion.4
  67.7 0.1 constant_dynamic-update-slice_fusion.3
  67.9 0.7 copy-done.9
  68.5 3.3 %collective-permute-start.10 = (bf16[32,5376]{1,0:T(8,128)(2,1)S(1)}, bf16[32,5376]{1,0:T(8,128)(2,1)S(1)}, u32[]{:S(2)}, u32[]{:S(2)}) collective-permute-start(bf16[32,5376]{1,0:T(8,128)(2,1)S(1)} %copy-done.9), channel_id=1, source_target_pairs={{0,112},{16,0},{32,16},{48,32},{64,48},{80,64},{96,80},{112,96},{1... | collective-permute-start | bytes 1032200 | tf_op jit(solution)/shard_map/ppermute | solution.py:28
  71.8 1.3 collective-permute-start.12
  73.0 5.0 %collective-permute-start.13 = (bf16[32,5376]{1,0:T(8,128)(2,1)S(1)}, bf16[32,5376]{1,0:T(8,128)(2,1)S(1)}, u32[]{:S(2)}, u32[]{:S(2)}) collective-permute-start(bf16[32,5376]{1,0:T(8,128)(2,1)S(1)} %copy-done.9), channel_id=1, source_target_pairs={{0,64},{16,80},{32,96},{48,112},{64,0},{80,16},{96,32},{112,48},{1... | collective-permute-start | bytes 1032200 | tf_op jit(solution)/shard_map/ppermute | solution.py:28
  78.1 0.2 broadcast_in_dim.118
  78.3 23.4 %collective-permute-done.10 = bf16[32,5376]{1,0:T(8,128)(2,1)S(1)} collective-permute-done((bf16[32,5376]{1,0:T(8,128)(2,1)S(1)}, bf16[32,5376]{1,0:T(8,128)(2,1)S(1)}, u32[]{:S(2)}, u32[]{:S(2)}) %collective-permute-start.10) | collective-permute-done | bytes 344096 | tf_op jit(solution)/shard_map/ppermute | solution.py:28
  101.7 0.3 collective-permute-start.16
  102.2 8.0 %collective-permute-done.15 = bf16[32,5376]{1,0:T(8,128)(2,1)S(1)} collective-permute-done((bf16[32,5376]{1,0:T(8,128)(2,1)S(1)}, bf16[32,5376]{1,0:T(8,128)(2,1)S(1)}, u32[]{:S(2)}, u32[]{:S(2)}) %collective-permute-start.15) | collective-permute-done | bytes 344096 | tf_op jit(solution)/shard_map/ppermute | solution.py:28
  110.2 5.0 %collective-permute-done.16 = bf16[32,5376]{1,0:T(8,128)(2,1)S(1)} collective-permute-done((bf16[32,5376]{1,0:T(8,128)(2,1)S(1)}, bf16[32,5376]{1,0:T(8,128)(2,1)S(1)}, u32[]{:S(2)}, u32[]{:S(2)}) %collective-permute-start.16) | collective-permute-done | bytes 344096 | tf_op jit(solution)/shard_map/ppermute | solution.py:28
  115.3 6.3 %fusion = f32[1024]{0:T(1024)S(1)} fusion(bf16[1024,5376]{1,0:T(8,128)(2,1)} %all-gather.2.cloned.1.call-done), kind=kLoop, calls=%fused_computation.2 | loop fusion | flops 16514048 | bytes 11014144 | tf_op jit(solution)/shard_map/reduce_sum | solution.py:67
  121.6 10.7 %fusion.3 = f32[1024,512]{0,1:T(8,128)S(1)} fusion(bf16[5376,512]{1,0:T(8,128)(2,1)} %bitcast.127, bf16[1024,5376]{1,0:T(8,128)(2,1)} %all-gather.2.cloned.1.call-done, f32[5376]{0:T(1024)S(1)} %copy-done.12, f32[1024]{0:T(1024)S(1)} %add_rsqrt_fusion.2), kind=kOutput, calls=%fused_computation.6 | convolution fusion | flops 5659164672 | bytes 18637824 | tf_op jit(solution)/shard_map/dot_general | solution.py:110
  132.4 0.1 multiply_reduce_fusion.1
  132.5 1.1 slice.99
  133.6 0.1 multiply_reduce_fusion
  133.7 0.1 multiply_bitcast_fusion
  133.8 1.2 fusion.45
  135.0 0.9 pad_maximum_fusion
  135.9 2.1 collective-permute-start.9
  138.0 2.5 copy.10
  140.6 1.6 multiply_multiply_fusion
  142.2 1.6 multiply_subtract_fusion
  143.8 0.3 fusion.25
  144.1 2.1 collective-permute-done.9
  146.2 1.1 maximum_maximum_fusion
  147.3 1.3 fusion.7
  148.6 1.2 fusion.9
  149.9 2.0 fusion.19
  151.9 1.3 fusion.8
  153.1 1.3 fusion.10
  154.5 2.0 fusion.22
  156.5 5.9 %convolution_convert_fusion = bf16[1024,5376]{1,0:T(8,128)(2,1)} fusion(bf16[256,5376]{1,0:T(8,128)(2,1)S(1)} %bitcast.126, bf16[512,256]{0,1:T(8,128)(2,1)S(1)} %bitcast.130, bf16[512,256]{0,1:T(8,128)(2,1)S(1)} %bitcast.129), kind=kOutput, calls=%fused_computation.5 | convolution fusion | flops 2825125888 | bytes 14286848 | tf_op jit(solution)/shard_map/dot_general | solution.py:173
  162.4 82.7 %reduce-scatter.2.cloned.1.call-done = bf16[64,5376]{1,0:T(8,128)(2,1)} async-done(((bf16[1024,5376]{1,0:T(8,128)(2,1)}), bf16[64,5376]{1,0:T(8,128)(2,1)}) %reduce-scatter.2.cloned.1.call-update) | async-done | bytes 688144 | tf_op jit(solution)/shard_map/reduce_scatter | solution.py:176
  245.1 1.3 fusion.15
  246.5 2.3 fusion.18
  (72 shorter events, 0.9 us)
Async XLA Ops:
  6.5 108.7 %all-gather.2.cloned.1.call-start = ((), (), s32[]{:S(2)}) async-start(), calls=%async_computation.1 | async-start | bytes 11698176 | tf_op jit(solution)/shard_map/all_gather | solution.py:107
  7.3 237.9 %reduce-scatter.2.cloned.1.call-start = ((), (), s32[]{:S(2)}) async-start(), calls=%async_computation.2 | async-start | bytes 11698176 | tf_op jit(solution)/shard_map/reduce_scatter | solution.py:176
  10.2 27.4 %collective-permute-start = (bf16[672,512]{1,0:T(8,128)(2,1)S(1)}, bf16[672,512]{1,0:T(8,128)(2,1)S(1)}, u32[]{:S(2)}, u32[]{:S(2)}) collective-permute-start(bf16[672,512]{1,0:T(8,128)(2,1)S(1)} %constant_dynamic-update-slice_fusion), channel_id=1, source_target_pairs={{0,16},{16,0},{1,17},{17,1},{2,18},{18,2},{3,19},{19,3},{4,20},{20... | collective-permute-start | bytes 2064392 | tf_op jit(solution)/shard_map/ppermute | solution.py:28
  13.6 20.7 %collective-permute-start.1 = (bf16[672,512]{1,0:T(8,128)(2,1)S(1)}, bf16[672,512]{1,0:T(8,128)(2,1)S(1)}, u32[]{:S(2)}, u32[]{:S(2)}) collective-permute-start(bf16[672,512]{1,0:T(8,128)(2,1)S(1)} %constant_dynamic-update-slice_fusion), channel_id=1, source_target_pairs={{0,96},{32,0},{64,32},{96,64},{1,97},{33,1},{65,33},{97,65},{2,98}... | collective-permute-start | bytes 2064392 | tf_op jit(solution)/shard_map/ppermute | solution.py:28
  16.4 17.8 %collective-permute-start.3 = (bf16[672,512]{1,0:T(8,128)(2,1)S(1)}, bf16[672,512]{1,0:T(8,128)(2,1)S(1)}, u32[]{:S(2)}, u32[]{:S(2)}) collective-permute-start(bf16[672,512]{1,0:T(8,128)(2,1)S(1)} %constant_dynamic-update-slice_fusion), channel_id=1, source_target_pairs={{0,32},{32,64},{64,96},{96,0},{1,33},{33,65},{65,97},{97,1},{2,34}... | collective-permute-start | bytes 2064392 | tf_op jit(solution)/shard_map/ppermute | solution.py:28
  34.2 12.2 %collective-permute-start.4 = (bf16[336,512]{1,0:T(8,128)(2,1)S(1)}, bf16[336,512]{1,0:T(8,128)(2,1)S(1)}, u32[]{:S(2)}, u32[]{:S(2)}) collective-permute-start(bf16[336,512]{1,0:T(8,128)(2,1)S(1)} %slice.89), channel_id=1, source_target_pairs={{0,32},{32,64},{64,96},{96,0},{1,33},{33,65},{65,97},{97,1},{2,34}... | collective-permute-start | bytes 1032200 | tf_op jit(solution)/shard_map/ppermute | solution.py:28
  34.4 12.1 %collective-permute-start.5 = (bf16[336,512]{1,0:T(8,128)(2,1)S(1)}, bf16[336,512]{1,0:T(8,128)(2,1)S(1)}, u32[]{:S(2)}, u32[]{:S(2)}) collective-permute-start(bf16[336,512]{1,0:T(8,128)(2,1)S(1)} %slice.90), channel_id=1, source_target_pairs={{0,96},{32,0},{64,32},{96,64},{1,97},{33,1},{65,33},{97,65},{2,98}... | collective-permute-start | bytes 1032200 | tf_op jit(solution)/shard_map/ppermute | solution.py:28
  37.6 21.1 %collective-permute-start.2 = (bf16[672,512]{1,0:T(8,128)(2,1)S(1)}, bf16[672,512]{1,0:T(8,128)(2,1)S(1)}, u32[]{:S(2)}, u32[]{:S(2)}) collective-permute-start(bf16[672,512]{1,0:T(8,128)(2,1)S(1)} %collective-permute-done), channel_id=1, source_target_pairs={{0,96},{32,0},{64,32},{96,64},{1,97},{33,1},{65,33},{97,65},{2,98}... | collective-permute-start | bytes 2064392 | tf_op jit(solution)/shard_map/ppermute | solution.py:28
  39.9 18.8 %collective-permute-start.6 = (bf16[672,512]{1,0:T(8,128)(2,1)S(1)}, bf16[672,512]{1,0:T(8,128)(2,1)S(1)}, u32[]{:S(2)}, u32[]{:S(2)}) collective-permute-start(bf16[672,512]{1,0:T(8,128)(2,1)S(1)} %collective-permute-done), channel_id=1, source_target_pairs={{0,32},{32,64},{64,96},{96,0},{1,33},{33,65},{65,97},{97,1},{2,34}... | collective-permute-start | bytes 2064392 | tf_op jit(solution)/shard_map/ppermute | solution.py:28
  58.7 8.8 %collective-permute-start.7 = (bf16[336,512]{1,0:T(8,128)(2,1)S(1)}, bf16[336,512]{1,0:T(8,128)(2,1)S(1)}, u32[]{:S(2)}, u32[]{:S(2)}) collective-permute-start(bf16[336,512]{1,0:T(8,128)(2,1)S(1)} %slice.91), channel_id=1, source_target_pairs={{0,32},{32,64},{64,96},{96,0},{1,33},{33,65},{65,97},{97,1},{2,34}... | collective-permute-start | bytes 1032200 | tf_op jit(solution)/shard_map/ppermute | solution.py:28
  58.8 8.7 %collective-permute-start.8 = (bf16[336,512]{1,0:T(8,128)(2,1)S(1)}, bf16[336,512]{1,0:T(8,128)(2,1)S(1)}, u32[]{:S(2)}, u32[]{:S(2)}) collective-permute-start(bf16[336,512]{1,0:T(8,128)(2,1)S(1)} %slice.92), channel_id=1, source_target_pairs={{0,96},{32,0},{64,32},{96,64},{1,97},{33,1},{65,33},{97,65},{2,98}... | collective-permute-start | bytes 1032200 | tf_op jit(solution)/shard_map/ppermute | solution.py:28
  67.5 1.0 copy-start.9
  67.9 34.2 %copy-start.1 = (bf16[4,2,672,512]{3,2,1,0:T(8,128)(2,1)}, bf16[4,2,672,512]{3,2,1,0:T(8,128)(2,1)S(1)}, u32[]{:S(2)}) copy-start(bf16[4,2,672,512]{3,2,1,0:T(8,128)(2,1)S(1)} %constant_dynamic-update-slice_fusion.3) | copy-start | bytes 16515076
  68.5 33.2 %collective-permute-start.10 = (bf16[32,5376]{1,0:T(8,128)(2,1)S(1)}, bf16[32,5376]{1,0:T(8,128)(2,1)S(1)}, u32[]{:S(2)}, u32[]{:S(2)}) collective-permute-start(bf16[32,5376]{1,0:T(8,128)(2,1)S(1)} %copy-done.9), channel_id=1, source_target_pairs={{0,112},{16,0},{32,16},{48,32},{64,48},{80,64},{96,80},{112,96},{1... | collective-permute-start | bytes 1032200 | tf_op jit(solution)/shard_map/ppermute | solution.py:28
  71.8 29.9 %collective-permute-start.11 = (bf16[32,5376]{1,0:T(8,128)(2,1)S(1)}, bf16[32,5376]{1,0:T(8,128)(2,1)S(1)}, u32[]{:S(2)}, u32[]{:S(2)}) collective-permute-start(bf16[32,5376]{1,0:T(8,128)(2,1)S(1)} %copy-done.9), channel_id=1, source_target_pairs={{0,96},{16,112},{32,0},{48,16},{64,32},{80,48},{96,64},{112,80},{1... | collective-permute-start | bytes 1032200 | tf_op jit(solution)/shard_map/ppermute | solution.py:28
  71.8 30.3 %collective-permute-start.12 = (bf16[32,5376]{1,0:T(8,128)(2,1)S(1)}, bf16[32,5376]{1,0:T(8,128)(2,1)S(1)}, u32[]{:S(2)}, u32[]{:S(2)}) collective-permute-start(bf16[32,5376]{1,0:T(8,128)(2,1)S(1)} %copy-done.9), channel_id=1, source_target_pairs={{0,80},{16,96},{32,112},{48,0},{64,16},{80,32},{96,48},{112,64},{1... | collective-permute-start | bytes 1032200 | tf_op jit(solution)/shard_map/ppermute | solution.py:28
  73.0 29.1 %collective-permute-start.13 = (bf16[32,5376]{1,0:T(8,128)(2,1)S(1)}, bf16[32,5376]{1,0:T(8,128)(2,1)S(1)}, u32[]{:S(2)}, u32[]{:S(2)}) collective-permute-start(bf16[32,5376]{1,0:T(8,128)(2,1)S(1)} %copy-done.9), channel_id=1, source_target_pairs={{0,64},{16,80},{32,96},{48,112},{64,0},{80,16},{96,32},{112,48},{1... | collective-permute-start | bytes 1032200 | tf_op jit(solution)/shard_map/ppermute | solution.py:28
  78.1 24.1 %collective-permute-start.14 = (bf16[32,5376]{1,0:T(8,128)(2,1)S(1)}, bf16[32,5376]{1,0:T(8,128)(2,1)S(1)}, u32[]{:S(2)}, u32[]{:S(2)}) collective-permute-start(bf16[32,5376]{1,0:T(8,128)(2,1)S(1)} %copy-done.9), channel_id=1, source_target_pairs={{0,48},{16,64},{32,80},{48,96},{64,112},{80,0},{96,16},{112,32},{1... | collective-permute-start | bytes 1032200 | tf_op jit(solution)/shard_map/ppermute | solution.py:28
  101.7 8.5 %collective-permute-start.15 = (bf16[32,5376]{1,0:T(8,128)(2,1)S(1)}, bf16[32,5376]{1,0:T(8,128)(2,1)S(1)}, u32[]{:S(2)}, u32[]{:S(2)}) collective-permute-start(bf16[32,5376]{1,0:T(8,128)(2,1)S(1)} %copy-done.9), channel_id=1, source_target_pairs={{0,32},{16,48},{32,64},{48,80},{64,96},{80,112},{96,0},{112,16},{1... | collective-permute-start | bytes 1032200 | tf_op jit(solution)/shard_map/ppermute | solution.py:28
  101.7 13.5 %collective-permute-start.16 = (bf16[32,5376]{1,0:T(8,128)(2,1)S(1)}, bf16[32,5376]{1,0:T(8,128)(2,1)S(1)}, u32[]{:S(2)}, u32[]{:S(2)}) collective-permute-start(bf16[32,5376]{1,0:T(8,128)(2,1)S(1)} %copy-done.9), channel_id=1, source_target_pairs={{0,16},{16,32},{32,48},{48,64},{64,80},{80,96},{96,112},{112,0},{1... | collective-permute-start | bytes 1032200 | tf_op jit(solution)/shard_map/ppermute | solution.py:28
  115.3 6.4 %copy-start.12 = (f32[5376]{0:T(1024)S(1)}, f32[5376]{0:T(1024)}, u32[]{:S(2)}) copy-start(f32[5376]{0:T(1024)} %param.10) | copy-start | bytes 64516
  132.4 1.3 copy-start.11
  132.5 3.4 %copy-start.3 = (bf16[1,1024,128]{1,2,0:T(8,128)(2,1)}, bf16[1,1024,128]{1,2,0:T(8,128)(2,1)S(1)}, u32[]{:S(2)}) copy-start(bf16[1,1024,128]{1,2,0:T(8,128)(2,1)S(1)} %fusion.41) | copy-start | bytes 786436
  135.0 3.0 %copy-start.5 = (bf16[1,1024,64]{1,2,0:T(8,128)(2,1)}, bf16[1,1024,64]{1,2,0:T(8,128)(2,1)S(1)}, u32[]{:S(2)}) copy-start(bf16[1,1024,64]{1,2,0:T(8,128)(2,1)S(1)} %get-tuple-element.11) | copy-start | bytes 393220
  135.0 3.0 %copy-start.7 = (bf16[1,1024,64]{1,2,0:T(8,128)(2,1)}, bf16[1,1024,64]{1,2,0:T(8,128)(2,1)S(1)}, u32[]{:S(2)}) copy-start(bf16[1,1024,64]{1,2,0:T(8,128)(2,1)S(1)} %get-tuple-element.12) | copy-start | bytes 393220
  135.9 10.3 %collective-permute-start.9 = (bf16[2,1024,128]{1,2,0:T(8,128)(2,1)}, bf16[2,1024,128]{1,2,0:T(8,128)(2,1)}, u32[]{:S(2)}, u32[]{:S(2)}) collective-permute-start(bf16[2,1024,128]{1,2,0:T(8,128)(2,1)} %pad_maximum_fusion), channel_id=1, source_target_pairs={{0,16},{16,32},{32,48},{48,64},{64,80},{80,96},{96,112},{1,17},{17... | collective-permute-start | bytes 1572872 | tf_op jit(solution)/shard_map/ppermute | solution.py:22
  142.1 4.1 %copy-start.4 = (bf16[1,1024,128]{1,2,0:T(8,128)(2,1)S(1)}, bf16[1,1024,128]{1,2,0:T(8,128)(2,1)}, u32[]{:S(2)}) copy-start(bf16[1,1024,128]{1,2,0:T(8,128)(2,1)} %copy-done.3) | copy-start | bytes 786436
  142.1 4.1 %copy-start.6 = (bf16[1,1024,64]{1,2,0:T(8,128)(2,1)S(1)}, bf16[1,1024,64]{1,2,0:T(8,128)(2,1)}, u32[]{:S(2)}) copy-start(bf16[1,1024,64]{1,2,0:T(8,128)(2,1)} %copy-done.5) | copy-start | bytes 393220
  142.1 4.1 %copy-start.8 = (bf16[1,1024,64]{1,2,0:T(8,128)(2,1)S(1)}, bf16[1,1024,64]{1,2,0:T(8,128)(2,1)}, u32[]{:S(2)}) copy-start(bf16[1,1024,64]{1,2,0:T(8,128)(2,1)} %copy-done.7) | copy-start | bytes 393220
  143.8 3.6 %copy-start = (pred[512,1536]{0,1:T(8,128)(4,1)S(1)}, pred[512,1536]{0,1:T(8,128)(4,1)}, u32[]{:S(2)}) copy-start(pred[512,1536]{0,1:T(8,128)(4,1)} %and_and_fusion.1) | copy-start | bytes 2359300
  162.4 84.1 %copy-start.2 = (bf16[64,5376]{1,0:T(8,128)(2,1)S(1)}, bf16[64,5376]{1,0:T(8,128)(2,1)}, u32[]{:S(2)}) copy-start(bf16[64,5376]{1,0:T(8,128)(2,1)} %param.9) | copy-start | bytes 2064388
  162.4 84.1 %copy-start.10 = (f32[5376]{0:T(1024)S(1)}, f32[5376]{0:T(1024)}, u32[]{:S(2)}) copy-start(f32[5376]{0:T(1024)} %param.17) | copy-start | bytes 64516
Sparse Core Ops, SparseCore 0:
  9.0 97.8 all-gather.1
  162.5 82.5 reduce-scatter.1

commit v6 on v4

--- a/solution.py
+++ b/solution.py
@@ -91,11 +91,18 @@
     own_rows = hidden_in.astype(jnp.float32)
     q_cols = w_query.shape[1]
     k_cols = w_key.shape[1]
-    w_in = gathered_over_ctx(jnp.concatenate([w_query, w_key, value_weight], axis=1))
+    out_rows = w_output.shape[0]
+    width = w_output.shape[1]
+    packed = jnp.concatenate(
+        [w_query, w_key, value_weight, w_output.reshape(w_query.shape[0], -1)], axis=1
+    )
+    weights = gathered_over_ctx(packed)
+    in_cols = q_cols + 2 * k_cols
+    w_in = weights[:, :in_cols]
+    ctx_count = weights.shape[0] // w_query.shape[0]
+    out_weight = weights[:, in_cols:].reshape(ctx_count * out_rows, width)
 
     raw_rows = lax.all_gather(hidden_in, HEAD, axis=0, tiled=True)
-    raw_rows, w_output = lax.optimization_barrier((raw_rows, w_output))
-    out_weight = lax.all_gather(w_output, CTX, axis=0, tiled=True)
     normed = root_mean_scale(raw_rows.astype(jnp.float32), pre_gain).astype(jnp.bfloat16)
     tok_count = normed.shape[0]
     projected = jnp.dot(normed, w_in, preferred_element_type=jnp.float32)

time: 265 us -> 246 us (0.928)
  waiting for transfers between devices: 170 us -> 139 us
  local copies, waits for them, and re-layouts: 12.9 us -> 22 us
    all_gather x1 -> x0, waiting for transfers between devices: 40.1 us -> none  [body(): out_weight = lax.all_gather(w_output, CTX, axis=0, tiled=True)]
    ppermute x9, waiting for transfers between devices: 28.9 us -> 53.8 us  [rotated(): return lax.ppermute(shard, axis, pairs)]
    all_gather x1, waiting for transfers between devices: 12.8 us -> 0.02 us  [body(): raw_rows = lax.all_gather(hidden_in, HEAD, axis=0, tiled=True)]
    ppermute x1, waiting for transfers between devices: 8.5 us -> 0.11 us  [passed_along(): return lax.ppermute(shard, axis, pairs)]
    reshape x0 -> x2, local copies, waits for them, and re-layouts: none -> 6.31 us  [the longest x1 4.91 us: body(): out_weight = weights[:, in_cols:].reshape(ctx_count * out_rows, width)]
    reduce_scatter x1, waiting for transfers between devices: 78.7 us -> 84.5 us  [body(): lax.psum_scatter(partial_value, HEAD, scatter_dimension=0, tiled=True)]
    unnamed x24 -> x21, local copies, waits for them, and re-layouts: 3.12 us -> 6.21 us
  transfers between devices with their start and end apart: 13 -> 12, of which waited for: 8 -> 6; matrix products, arithmetic and copies ran while one was open for 12% -> 11% of each run, Pallas kernels for 0% -> 0%
where the time goes in v6:
time: 246 us; the launch traced here: 245 us
  waiting for transfers between devices  139 us (57%)
  other arithmetic  25.7 us (10%)
  starting transfers between devices  22.5 us (9%)
  local copies, waits for them, and re-layouts  22 us (9%)
  matrix products  21.8 us (9%)
  between operations  13.9 us (6%)
    reduce_scatter x1, waiting for transfers between devices, body(): lax.psum_scatter(partial_value, HEAD, scatter_dimension=0, tiled=True)  84.5 us
    ppermute x9, waiting for transfers between devices, rotated(): return lax.ppermute(shard, axis, pairs)  53.8 us
    ppermute x9, starting transfers between devices, rotated(): return lax.ppermute(shard, axis, pairs)  15.7 us
    dot_general x1, matrix products, body(): projected = jnp.dot(normed, w_in, preferred_element_type=jnp.float32)  9.36 us
    reduce_sum x4, other arithmetic, root_mean_scale(): mean_sq = jnp.mean(values * values, axis=-1, keepdims=True)  7.96 us
    ppermute x1, starting transfers between devices, passed_along(): return lax.ppermute(shard, axis, pairs)  6.79 us
    unnamed x21, local copies, waits for them, and re-layouts  6.21 us
    dot_general x1, matrix products, body(): jnp.dot(attended, out_weight, preferred_element_type=jnp.float32)  5.89 us
  transfers between devices with their start and end apart: 12, of which 6 were waited for; matrix products, arithmetic and copies ran while one was open for 11% of the time, Pallas kernels for 0%

profile of v6, /device:TPU:0, one launch (start us, length us, event | category | flops | bytes accessed | tf_op | source)
XLA Modules:
  0.0 245.0 jit_solution(4009391211128390291)
XLA Ops:
  6.5 0.7 all-gather.2.cloned.1.call-update
  7.3 0.0 reduce-scatter.2.cloned.1.call-start
  7.3 1.4 reshape.314
  8.7 1.0 constant_dynamic-update-slice_fusion.3
  9.7 1.0 constant_dynamic-update-slice_fusion.2
  10.7 1.0 constant_dynamic-update-slice_fusion.1
  11.7 3.4 %collective-permute-start = (bf16[672,768]{1,0:T(8,128)(2,1)S(1)}, bf16[672,768]{1,0:T(8,128)(2,1)}, u32[]{:S(2)}, u32[]{:S(2)}) collective-permute-start(bf16[672,768]{1,0:T(8,128)(2,1)S(1)} %constant_dynamic-update-slice_fusion), channel_id=1, source_target_pairs={{0,16},{16,0},{1,17},{17,1},{2,18},{18,2},{3,19},{19,3},{4,20},{20... | collective-permute-start | bytes 3096584 | tf_op jit(solution)/shard_map/ppermute | solution.py:27
  15.1 2.8 %collective-permute-start.1 = (bf16[672,768]{1,0:T(8,128)(2,1)S(1)}, bf16[672,768]{1,0:T(8,128)(2,1)S(1)}, u32[]{:S(2)}, u32[]{:S(2)}) collective-permute-start(bf16[672,768]{1,0:T(8,128)(2,1)S(1)} %constant_dynamic-update-slice_fusion), channel_id=1, source_target_pairs={{0,96},{32,0},{64,32},{96,64},{1,97},{33,1},{65,33},{97,65},{2,98}... | collective-permute-start | bytes 3096584 | tf_op jit(solution)/shard_map/ppermute | solution.py:27
  17.9 3.1 %multiply_cosine_fusion = (f32[1024,64]{1,0:T(8,128)}, f32[1024,64]{1,0:T(8,128)}) fusion(f32[64]{0:T(128)S(1)} %multiply_power_fusion, f32[1024]{0:T(1024)S(1)} %fusion.47), kind=kLoop, calls=%fused_computation.52 | loop fusion | flops 65536 | bytes 528640 | tf_op jit(solution)/shard_map/cos | solution.py:67
  21.0 0.1 broadcast_in_dim.78.clone
  21.2 0.1 bitcast_dynamic-update-slice_fusion.5
  21.3 3.0 %and_and_fusion = (pred[512,1536]{0,1:T(8,128)(4,1)}, pred[512,1536]{0,1:T(8,128)(4,1)}) fusion(s32[512]{0:T(512)S(1)} %get-tuple-element.13, s32[512]{0:T(512)S(1)} %get-tuple-element.14, s32[1536]{0:T(1024)S(1)} %iota_add_fusion, pred[1536]{0:T(1024)(128)(4,1)S(1)} %broadcast_compare_fusion, pred[1536]{0:T(1024)(128)(4,1)S(1)} %broadcast_compare_fusion.1, ...), kind=kLoop, calls=%fused_computation.24 | loop fusion | flops 6291456 | bytes 1596416 | tf_op jit(solution)/shard_map/and | solution.py:156
  24.3 18.7 %collective-permute-done.3 = bf16[672,768]{1,0:T(8,128)(2,1)S(1)} collective-permute-done((bf16[672,768]{1,0:T(8,128)(2,1)S(1)}, bf16[672,768]{1,0:T(8,128)(2,1)S(1)}, u32[]{:S(2)}, u32[]{:S(2)}) %collective-permute-start.3) | collective-permute-done | bytes 1032224 | tf_op jit(solution)/shard_map/ppermute | solution.py:27
  43.1 0.1 collective-permute-start.4
  43.2 3.3 %collective-permute-start.5 = (bf16[336,768]{1,0:T(8,128)(2,1)S(1)}, bf16[336,768]{1,0:T(8,128)(2,1)S(1)}, u32[]{:S(2)}, u32[]{:S(2)}) collective-permute-start(bf16[336,768]{1,0:T(8,128)(2,1)S(1)} %slice.98), channel_id=1, source_target_pairs={{0,96},{32,0},{64,32},{96,64},{1,97},{33,1},{65,33},{97,65},{2,98}... | collective-permute-start | bytes 1548296 | tf_op jit(solution)/shard_map/ppermute | solution.py:27
  46.5 8.4 %collective-permute-done = bf16[672,768]{1,0:T(8,128)(2,1)} collective-permute-done((bf16[672,768]{1,0:T(8,128)(2,1)S(1)}, bf16[672,768]{1,0:T(8,128)(2,1)}, u32[]{:S(2)}, u32[]{:S(2)}) %collective-permute-start) | collective-permute-done | bytes 1032224 | tf_op jit(solution)/shard_map/ppermute | solution.py:27
  54.8 2.7 %collective-permute-start.2 = (bf16[672,768]{1,0:T(8,128)(2,1)}, bf16[672,768]{1,0:T(8,128)(2,1)S(1)}, u32[]{:S(2)}, u32[]{:S(2)}) collective-permute-start(bf16[672,768]{1,0:T(8,128)(2,1)} %collective-permute-done), channel_id=1, source_target_pairs={{0,96},{32,0},{64,32},{96,64},{1,97},{33,1},{65,33},{97,65},{2,98}... | collective-permute-start | bytes 3096584 | tf_op jit(solution)/shard_map/ppermute | solution.py:27
  57.5 1.4 bitcast_dynamic-update-slice_fusion.4
  58.9 0.5 broadcast_in_dim.77
  59.4 0.2 constant_dynamic-update-slice_fusion.7
  59.7 0.1 broadcast_in_dim.78.clone.1
  59.8 0.1 bitcast_dynamic-update-slice_fusion.3
  59.9 0.1 broadcast_in_dim.78.clone.3
  60.1 0.1 bitcast_dynamic-update-slice_fusion.1
  60.2 0.1 broadcast_in_dim.78.clone.2
  60.3 0.1 fusion.27
  60.4 20.2 %collective-permute-done.6 = bf16[672,768]{1,0:T(8,128)(2,1)S(1)} collective-permute-done((bf16[672,768]{1,0:T(8,128)(2,1)}, bf16[672,768]{1,0:T(8,128)(2,1)S(1)}, u32[]{:S(2)}, u32[]{:S(2)}) %collective-permute-start.6) | collective-permute-done | bytes 1032224 | tf_op jit(solution)/shard_map/ppermute | solution.py:27
  80.6 0.1 collective-permute-start.7
  80.8 3.5 %collective-permute-start.8 = (bf16[336,768]{1,0:T(8,128)(2,1)S(1)}, bf16[336,768]{1,0:T(8,128)(2,1)S(1)}, u32[]{:S(2)}, u32[]{:S(2)}) collective-permute-start(bf16[336,768]{1,0:T(8,128)(2,1)S(1)} %slice.100), channel_id=1, source_target_pairs={{0,96},{32,0},{64,32},{96,64},{1,97},{33,1},{65,33},{97,65},{2,98}... | collective-permute-start | bytes 1548296 | tf_op jit(solution)/shard_map/ppermute | solution.py:27
  84.2 0.1 bitcast_dynamic-update-slice_fusion.2
  84.3 0.2 constant_dynamic-update-slice_fusion.6
  84.6 0.1 bitcast_dynamic-update-slice_fusion
  84.7 6.5 %collective-permute-done.7 = bf16[336,768]{1,0:T(8,128)(2,1)S(1)} collective-permute-done((bf16[336,768]{1,0:T(8,128)(2,1)S(1)}, bf16[336,768]{1,0:T(8,128)(2,1)S(1)}, u32[]{:S(2)}, u32[]{:S(2)}) %collective-permute-start.7) | collective-permute-done | bytes 516128 | tf_op jit(solution)/shard_map/ppermute | solution.py:27
  91.1 0.1 fusion.28
  91.2 0.2 constant_dynamic-update-slice_fusion.5
  91.5 0.2 constant_dynamic-update-slice_fusion.4
  91.8 3.2 %copy-done = bf16[4,2,672,768]{3,2,1,0:T(8,128)(2,1)} copy-done((bf16[4,2,672,768]{3,2,1,0:T(8,128)(2,1)}, bf16[4,2,672,768]{3,2,1,0:T(8,128)(2,1)S(1)}, u32[]{:S(2)}) %copy-start) | copy-done | bytes 8257560
  95.0 1.7 slice.115
  96.7 4.9 %reshape.325 = bf16[256,5376]{1,0:T(8,128)(2,1)S(1)} reshape(bf16[5376,256]{1,0:T(8,128)(2,1)} %slice.115) | data formatting | bytes 5505024 | tf_op jit(solution)/shard_map/reshape | solution.py:103
  101.7 6.5 %fusion = f32[1024]{0:T(1024)S(1)} fusion(bf16[1024,5376]{1,0:T(8,128)(2,1)} %all-gather.2.cloned.1.call-done), kind=kLoop, calls=%fused_computation.2 | loop fusion | flops 16514048 | bytes 11014144 | tf_op jit(solution)/shard_map/reduce_sum | solution.py:58
  108.2 9.4 %fusion.3 = f32[1024,512]{0,1:T(8,128)S(1)} fusion(bf16[1024,5376]{1,0:T(8,128)(2,1)} %all-gather.2.cloned.1.call-done, f32[5376]{0:T(1024)S(1)} %copy-done.8, f32[1024]{0:T(1024)S(1)} %add_rsqrt_fusion.2, bf16[5376,768]{1,0:T(8,128)(2,1)S(1)} %bitcast.109), kind=kOutput, calls=%fused_computation.6 | convolution fusion | flops 5659164672 | bytes 18640896 | tf_op jit(solution)/shard_map/dot_general | solution.py:108
  117.6 0.1 multiply_reduce_fusion.1
  117.7 1.1 slice.108
  118.8 0.1 multiply_reduce_fusion
  118.9 0.1 multiply_bitcast_fusion
  119.0 1.2 fusion.46
  120.2 0.8 pad_maximum_fusion
  121.0 6.8 %collective-permute-start.9 = (bf16[2,1024,128]{1,2,0:T(8,128)(2,1)}, bf16[2,1024,128]{1,2,0:T(8,128)(2,1)}, u32[]{:S(2)}, u32[]{:S(2)}) collective-permute-start(bf16[2,1024,128]{1,2,0:T(8,128)(2,1)} %pad_maximum_fusion), channel_id=1, source_target_pairs={{0,16},{16,32},{32,48},{48,64},{64,80},{80,96},{96,112},{1,17},{17... | collective-permute-start | bytes 1572872 | tf_op jit(solution)/shard_map/ppermute | solution.py:21
  127.8 2.6 %copy.10 = f32[1024,2,128]{2,0,1:T(8,128)} copy(f32[1024,2,128]{0,2,1:T(8,128)} %bitcast.110) | data formatting | bytes 2097152 | tf_op jit(solution)/shard_map/reshape | solution.py:120
  130.4 1.6 multiply_multiply_fusion
  131.9 1.5 multiply_subtract_fusion
  133.5 0.3 fusion.26
  133.9 0.1 collective-permute-done.9
  134.0 1.1 maximum_maximum_fusion
  135.1 1.3 fusion.7
  136.4 1.2 fusion.10
  137.6 2.0 fusion.20
  139.6 1.3 fusion.8
  140.9 1.2 fusion.11
  142.2 2.0 fusion.23
  144.2 5.9 %convolution_convert_fusion = bf16[1024,5376]{1,0:T(8,128)(2,1)} fusion(bf16[256,5376]{1,0:T(8,128)(2,1)S(1)} %reshape.325, bf16[512,256]{0,1:T(8,128)(2,1)S(1)} %bitcast.112, bf16[512,256]{0,1:T(8,128)(2,1)S(1)} %bitcast.111), kind=kOutput, calls=%fused_computation.5 | convolution fusion | flops 2825125888 | bytes 14286848 | tf_op jit(solution)/shard_map/dot_general | solution.py:171
  150.1 84.5 %reduce-scatter.2.cloned.1.call-done = bf16[64,5376]{1,0:T(8,128)(2,1)} async-done(((bf16[1024,5376]{1,0:T(8,128)(2,1)}), bf16[64,5376]{1,0:T(8,128)(2,1)}) %reduce-scatter.2.cloned.1.call-update) | async-done | bytes 688144 | tf_op jit(solution)/shard_map/reduce_scatter | solution.py:174
  234.5 1.3 fusion.16
  235.9 2.3 fusion.19
  (45 shorter events, 0.4 us)
Async XLA Ops:
  6.5 95.1 %all-gather.2.cloned.1.call-start = ((), (), s32[]{:S(2)}) async-start(), calls=%async_computation.1 | async-start | bytes 11698176 | tf_op jit(solution)/shard_map/all_gather | solution.py:105
  7.3 227.3 %reduce-scatter.2.cloned.1.call-start = ((), (), s32[]{:S(2)}) async-start(), calls=%async_computation.2 | async-start | bytes 11698176 | tf_op jit(solution)/shard_map/reduce_scatter | solution.py:174
  11.7 43.2 %collective-permute-start = (bf16[672,768]{1,0:T(8,128)(2,1)S(1)}, bf16[672,768]{1,0:T(8,128)(2,1)}, u32[]{:S(2)}, u32[]{:S(2)}) collective-permute-start(bf16[672,768]{1,0:T(8,128)(2,1)S(1)} %constant_dynamic-update-slice_fusion), channel_id=1, source_target_pairs={{0,16},{16,0},{1,17},{17,1},{2,18},{18,2},{3,19},{19,3},{4,20},{20... | collective-permute-start | bytes 3096584 | tf_op jit(solution)/shard_map/ppermute | solution.py:27
  15.1 28.1 %collective-permute-start.1 = (bf16[672,768]{1,0:T(8,128)(2,1)S(1)}, bf16[672,768]{1,0:T(8,128)(2,1)S(1)}, u32[]{:S(2)}, u32[]{:S(2)}) collective-permute-start(bf16[672,768]{1,0:T(8,128)(2,1)S(1)} %constant_dynamic-update-slice_fusion), channel_id=1, source_target_pairs={{0,96},{32,0},{64,32},{96,64},{1,97},{33,1},{65,33},{97,65},{2,98}... | collective-permute-start | bytes 3096584 | tf_op jit(solution)/shard_map/ppermute | solution.py:27
  17.8 25.2 %collective-permute-start.3 = (bf16[672,768]{1,0:T(8,128)(2,1)S(1)}, bf16[672,768]{1,0:T(8,128)(2,1)S(1)}, u32[]{:S(2)}, u32[]{:S(2)}) collective-permute-start(bf16[672,768]{1,0:T(8,128)(2,1)S(1)} %constant_dynamic-update-slice_fusion), channel_id=1, source_target_pairs={{0,32},{32,64},{64,96},{96,0},{1,33},{33,65},{65,97},{97,1},{2,34}... | collective-permute-start | bytes 3096584 | tf_op jit(solution)/shard_map/ppermute | solution.py:27
  43.1 17.1 %collective-permute-start.4 = (bf16[336,768]{1,0:T(8,128)(2,1)S(1)}, bf16[336,768]{1,0:T(8,128)(2,1)S(1)}, u32[]{:S(2)}, u32[]{:S(2)}) collective-permute-start(bf16[336,768]{1,0:T(8,128)(2,1)S(1)} %slice.97), channel_id=1, source_target_pairs={{0,32},{32,64},{64,96},{96,0},{1,33},{33,65},{65,97},{97,1},{2,34}... | collective-permute-start | bytes 1548296 | tf_op jit(solution)/shard_map/ppermute | solution.py:27
  43.2 17.0 %collective-permute-start.5 = (bf16[336,768]{1,0:T(8,128)(2,1)S(1)}, bf16[336,768]{1,0:T(8,128)(2,1)S(1)}, u32[]{:S(2)}, u32[]{:S(2)}) collective-permute-start(bf16[336,768]{1,0:T(8,128)(2,1)S(1)} %slice.98), channel_id=1, source_target_pairs={{0,96},{32,0},{64,32},{96,64},{1,97},{33,1},{65,33},{97,65},{2,98}... | collective-permute-start | bytes 1548296 | tf_op jit(solution)/shard_map/ppermute | solution.py:27
  54.8 25.9 %collective-permute-start.2 = (bf16[672,768]{1,0:T(8,128)(2,1)}, bf16[672,768]{1,0:T(8,128)(2,1)S(1)}, u32[]{:S(2)}, u32[]{:S(2)}) collective-permute-start(bf16[672,768]{1,0:T(8,128)(2,1)} %collective-permute-done), channel_id=1, source_target_pairs={{0,96},{32,0},{64,32},{96,64},{1,97},{33,1},{65,33},{97,65},{2,98}... | collective-permute-start | bytes 3096584 | tf_op jit(solution)/shard_map/ppermute | solution.py:27
  57.5 23.1 %collective-permute-start.6 = (bf16[672,768]{1,0:T(8,128)(2,1)}, bf16[672,768]{1,0:T(8,128)(2,1)S(1)}, u32[]{:S(2)}, u32[]{:S(2)}) collective-permute-start(bf16[672,768]{1,0:T(8,128)(2,1)} %collective-permute-done), channel_id=1, source_target_pairs={{0,32},{32,64},{64,96},{96,0},{1,33},{33,65},{65,97},{97,1},{2,34}... | collective-permute-start | bytes 3096584 | tf_op jit(solution)/shard_map/ppermute | solution.py:27
  80.6 10.5 %collective-permute-start.7 = (bf16[336,768]{1,0:T(8,128)(2,1)S(1)}, bf16[336,768]{1,0:T(8,128)(2,1)S(1)}, u32[]{:S(2)}, u32[]{:S(2)}) collective-permute-start(bf16[336,768]{1,0:T(8,128)(2,1)S(1)} %slice.99), channel_id=1, source_target_pairs={{0,32},{32,64},{64,96},{96,0},{1,33},{33,65},{65,97},{97,1},{2,34}... | collective-permute-start | bytes 1548296 | tf_op jit(solution)/shard_map/ppermute | solution.py:27
  80.8 10.4 %collective-permute-start.8 = (bf16[336,768]{1,0:T(8,128)(2,1)S(1)}, bf16[336,768]{1,0:T(8,128)(2,1)S(1)}, u32[]{:S(2)}, u32[]{:S(2)}) collective-permute-start(bf16[336,768]{1,0:T(8,128)(2,1)S(1)} %slice.100), channel_id=1, source_target_pairs={{0,96},{32,0},{64,32},{96,64},{1,97},{33,1},{65,33},{97,65},{2,98}... | collective-permute-start | bytes 1548296 | tf_op jit(solution)/shard_map/ppermute | solution.py:27
  91.7 3.3 %copy-start = (bf16[4,2,672,768]{3,2,1,0:T(8,128)(2,1)}, bf16[4,2,672,768]{3,2,1,0:T(8,128)(2,1)S(1)}, u32[]{:S(2)}) copy-start(bf16[4,2,672,768]{3,2,1,0:T(8,128)(2,1)S(1)} %constant_dynamic-update-slice_fusion.4) | copy-start | bytes 24772612
  101.6 6.5 %copy-start.8 = (f32[5376]{0:T(1024)S(1)}, f32[5376]{0:T(1024)}, u32[]{:S(2)}) copy-start(f32[5376]{0:T(1024)} %param.10) | copy-start | bytes 64516
  101.7 6.5 %copy-start.1 = (bf16[4,2,672,768]{3,2,1,0:T(8,128)(2,1)S(1)}, bf16[4,2,672,768]{3,2,1,0:T(8,128)(2,1)}, u32[]{:S(2)}) copy-start(bf16[4,2,672,768]{3,2,1,0:T(8,128)(2,1)} %copy-done) | copy-start | bytes 24772612
  117.6 1.3 copy-start.6
  118.8 11.6 %copy-start.7 = (f32[128]{0:T(128)S(1)}, f32[128]{0:T(128)}, u32[]{:S(2)}) copy-start(f32[128]{0:T(128)} %param.14) | copy-start | bytes 1540
  121.0 13.0 %collective-permute-start.9 = (bf16[2,1024,128]{1,2,0:T(8,128)(2,1)}, bf16[2,1024,128]{1,2,0:T(8,128)(2,1)}, u32[]{:S(2)}, u32[]{:S(2)}) collective-permute-start(bf16[2,1024,128]{1,2,0:T(8,128)(2,1)} %pad_maximum_fusion), channel_id=1, source_target_pairs={{0,16},{16,32},{32,48},{48,64},{64,80},{80,96},{96,112},{1,17},{17... | collective-permute-start | bytes 1572872 | tf_op jit(solution)/shard_map/ppermute | solution.py:21
  133.5 1.6 copy-start.3
  137.6 2.0 copy-start.2
  150.1 85.8 %copy-start.4 = (bf16[64,5376]{1,0:T(8,128)(2,1)S(1)}, bf16[64,5376]{1,0:T(8,128)(2,1)}, u32[]{:S(2)}) copy-start(bf16[64,5376]{1,0:T(8,128)(2,1)} %param.9) | copy-start | bytes 2064388
  150.1 85.8 %copy-start.5 = (f32[5376]{0:T(1024)S(1)}, f32[5376]{0:T(1024)}, u32[]{:S(2)}) copy-start(f32[5376]{0:T(1024)} %param.17) | copy-start | bytes 64516
Sparse Core Ops, SparseCore 0:
  9.0 82.4 all-gather.1
  150.2 84.2 reduce-scatter.1

commit v7 on v3

--- a/solution.py
+++ b/solution.py
@@ -93,8 +93,8 @@
     k_cols = w_key.shape[1]
     w_in = gathered_over_ctx(jnp.concatenate([w_query, w_key, value_weight], axis=1))
 
-    raw_rows = lax.all_gather(hidden_in, HEAD, axis=0, tiled=True)
-    normed = root_mean_scale(raw_rows.astype(jnp.float32), pre_gain).astype(jnp.bfloat16)
+    own_normed = root_mean_scale(own_rows, pre_gain).astype(jnp.bfloat16)
+    normed = lax.all_gather(own_normed, HEAD, axis=0, tiled=True)
     tok_count = normed.shape[0]
     projected = jnp.dot(normed, w_in, preferred_element_type=jnp.float32)
     projected, w_output = lax.optimization_barrier((projected, w_output))

time: 244 us -> 246 us (level)
  local copies, waits for them, and re-layouts: 20.3 us -> 24.6 us
    reduce_sum x4, other arithmetic: 9.17 us -> 6.14 us  [root_mean_scale(): mean_sq = jnp.mean(values * values, axis=-1, keepdims=True)]
  transfers between devices with their start and end apart: 21 -> 21, of which waited for: 7 -> 7; matrix products, arithmetic and copies ran while one was open for 17% -> 19% of each run, Pallas kernels for 0% -> 0%
where the time goes in v7:
time: 246 us
  waiting for transfers between devices  125 us (51%)
  starting transfers between devices  35.1 us (14%)
  other arithmetic  24.8 us (10%)
  local copies, waits for them, and re-layouts  24.6 us (10%)
  matrix products  22.5 us (9%)
  between operations  14 us (6%)
    reduce_scatter x1, waiting for transfers between devices, body(): lax.psum_scatter(partial_value, HEAD, scatter_dimension=0, tiled=True)  80.9 us
    ppermute x18, waiting for transfers between devices, rotated(): return lax.ppermute(shard, axis, pairs)  31.2 us
    ppermute x18, starting transfers between devices, rotated(): return lax.ppermute(shard, axis, pairs)  30.7 us
    all_gather x1, waiting for transfers between devices, body(): normed = lax.all_gather(own_normed, HEAD, axis=0, tiled=True)  12.6 us
    dynamic_update_slice x20, local copies, waits for them, and re-layouts, placed(): lax.dynamic_update_index_in_dim(stacked, part, (me + i) % count, 0)  11.7 us
    dot_general x1, matrix products, body(): projected = jnp.dot(normed, w_in, preferred_element_type=jnp.float32)  10.2 us
    reduce_sum x4, other arithmetic, root_mean_scale(): mean_sq = jnp.mean(values * values, axis=-1, keepdims=True)  6.14 us
    dot_general x1, matrix products, body(): jnp.dot(attended, out_weight, preferred_element_type=jnp.float32)  5.87 us
  transfers between devices with their start and end apart: 21, of which 7 were waited for; matrix products, arithmetic and copies ran while one was open for 19% of the time, Pallas kernels for 0%

profile of v7, /device:TPU:0, one launch (start us, length us, event | category | flops | bytes accessed | tf_op | source)
XLA Modules:
  0.0 245.7 jit_solution(4182608681377991320)
XLA Ops:
  6.5 1.4 fusion.10
  8.0 2.2 fusion.12
  10.2 0.8 constant_dynamic-update-slice_fusion.2
  11.0 0.7 constant_dynamic-update-slice_fusion.1
  11.7 0.7 constant_dynamic-update-slice_fusion
  12.4 3.3 %collective-permute-start = (bf16[672,512]{1,0:T(8,128)(2,1)}, bf16[672,512]{1,0:T(8,128)(2,1)}, u32[]{:S(2)}, u32[]{:S(2)}) collective-permute-start(bf16[672,512]{1,0:T(8,128)(2,1)} %constant_dynamic-update-slice_fusion), channel_id=1, source_target_pairs={{0,16},{16,0},{1,17},{17,1},{2,18},{18,2},{3,19},{19,3},{4,20},{20... | collective-permute-start | bytes 2064392 | tf_op jit(solution)/shard_map/ppermute | solution.py:27
  15.7 2.8 %collective-permute-start.1 = (bf16[672,512]{1,0:T(8,128)(2,1)}, bf16[672,512]{1,0:T(8,128)(2,1)S(1)}, u32[]{:S(2)}, u32[]{:S(2)}) collective-permute-start(bf16[672,512]{1,0:T(8,128)(2,1)} %constant_dynamic-update-slice_fusion), channel_id=1, source_target_pairs={{0,96},{32,0},{64,32},{96,64},{1,97},{33,1},{65,33},{97,65},{2,98}... | collective-permute-start | bytes 2064392 | tf_op jit(solution)/shard_map/ppermute | solution.py:27
  18.5 0.1 broadcast_in_dim.113.clone
  18.6 1.2 bitcast_dynamic-update-slice_fusion.5
  19.8 1.1 and_and_fusion.1
  20.9 3.1 %multiply_cosine_fusion = (f32[1024,64]{1,0:T(8,128)}, f32[1024,64]{1,0:T(8,128)}) fusion(f32[64]{0:T(128)S(1)} %multiply_power_fusion, f32[1024]{0:T(1024)S(1)} %get-tuple-element.26), kind=kLoop, calls=%fused_computation.39 | loop fusion | flops 65536 | bytes 528640 | tf_op jit(solution)/shard_map/cos | solution.py:67
  24.0 1.1 and_and_fusion
  25.2 11.3 %collective-permute-done.3 = bf16[672,512]{1,0:T(8,128)(2,1)S(1)} collective-permute-done((bf16[672,512]{1,0:T(8,128)(2,1)}, bf16[672,512]{1,0:T(8,128)(2,1)S(1)}, u32[]{:S(2)}, u32[]{:S(2)}) %collective-permute-start.3) | collective-permute-done | bytes 688160 | tf_op jit(solution)/shard_map/ppermute | solution.py:27
  36.6 3.3 %collective-permute-start.5 = (bf16[336,512]{1,0:T(8,128)(2,1)S(1)}, bf16[336,512]{1,0:T(8,128)(2,1)S(1)}, u32[]{:S(2)}, u32[]{:S(2)}) collective-permute-start(bf16[336,512]{1,0:T(8,128)(2,1)S(1)} %slice.106), channel_id=1, source_target_pairs={{0,96},{32,0},{64,32},{96,64},{1,97},{33,1},{65,33},{97,65},{2,98}... | collective-permute-start | bytes 1032200 | tf_op jit(solution)/shard_map/ppermute | solution.py:27
  39.9 0.7 collective-permute-done
  40.6 2.7 %collective-permute-start.2 = (bf16[672,512]{1,0:T(8,128)(2,1)}, bf16[672,512]{1,0:T(8,128)(2,1)S(1)}, u32[]{:S(2)}, u32[]{:S(2)}) collective-permute-start(bf16[672,512]{1,0:T(8,128)(2,1)} %collective-permute-done), channel_id=1, source_target_pairs={{0,96},{32,0},{64,32},{96,64},{1,97},{33,1},{65,33},{97,65},{2,98}... | collective-permute-start | bytes 2064392 | tf_op jit(solution)/shard_map/ppermute | solution.py:27
  43.5 1.2 bitcast_dynamic-update-slice_fusion.4
  44.6 2.8 %broadcast_in_dim.112 = bf16[4,2,672,512]{3,2,1,0:T(8,128)(2,1)} broadcast(bf16[]{:T(256)} %constant.186.clone.1), dimensions={} | broadcast | bytes 5505026 | tf_op jit(solution)/shard_map/broadcast_in_dim | solution.py:31
  47.5 1.2 constant_dynamic-update-slice_fusion.10
  49.0 12.1 %collective-permute-done.6 = bf16[672,512]{1,0:T(8,128)(2,1)S(1)} collective-permute-done((bf16[672,512]{1,0:T(8,128)(2,1)}, bf16[672,512]{1,0:T(8,128)(2,1)S(1)}, u32[]{:S(2)}, u32[]{:S(2)}) %collective-permute-start.6) | collective-permute-done | bytes 688160 | tf_op jit(solution)/shard_map/ppermute | solution.py:27
  61.2 3.3 %collective-permute-start.8 = (bf16[336,512]{1,0:T(8,128)(2,1)S(1)}, bf16[336,512]{1,0:T(8,128)(2,1)S(1)}, u32[]{:S(2)}, u32[]{:S(2)}) collective-permute-start(bf16[336,512]{1,0:T(8,128)(2,1)S(1)} %slice.108), channel_id=1, source_target_pairs={{0,96},{32,0},{64,32},{96,64},{1,97},{33,1},{65,33},{97,65},{2,98}... | collective-permute-start | bytes 1032200 | tf_op jit(solution)/shard_map/ppermute | solution.py:27
  64.5 1.3 constant_dynamic-update-slice_fusion.9
  65.8 4.1 %collective-permute-done.7 = bf16[336,512]{1,0:T(8,128)(2,1)S(1)} collective-permute-done((bf16[336,512]{1,0:T(8,128)(2,1)S(1)}, bf16[336,512]{1,0:T(8,128)(2,1)S(1)}, u32[]{:S(2)}, u32[]{:S(2)}) %collective-permute-start.7) | collective-permute-done | bytes 344096 | tf_op jit(solution)/shard_map/ppermute | solution.py:27
  70.0 1.2 constant_dynamic-update-slice_fusion.8
  71.2 1.2 constant_dynamic-update-slice_fusion.7
  72.4 12.6 %all-gather.2.cloned.1.call-done = bf16[1024,5376]{1,0:T(8,128)(2,1)} async-done(((bf16[64,5376]{1,0:T(8,128)(2,1)}), bf16[1024,5376]{1,0:T(8,128)(2,1)}) %all-gather.2.cloned.1.call-update) | async-done | bytes 11010064 | tf_op jit(solution)/shard_map/all_gather | solution.py:97
  85.0 10.2 %fusion.50 = f32[1024,512]{1,0:T(8,128)S(1)} fusion(bf16[1024,5376]{1,0:T(8,128)(2,1)} %all-gather.2.cloned.1.call-done, bf16[5376,512]{1,0:T(8,128)(2,1)} %bitcast.8), kind=kOutput, calls=%fused_computation.118 | convolution fusion | flops 5637144576 | bytes 18612224 | tf_op jit(solution)/shard_map/dot_general | solution.py:99
  95.2 0.2 multiply_reduce_fusion.1
  95.5 1.1 fusion.48
  96.6 1.5 collective-permute-start.13
  98.1 1.8 collective-permute-start.10
  99.9 1.7 collective-permute-start.11
  101.7 0.2 multiply_bitcast_fusion
  101.9 2.4 fusion.43
  104.3 1.0 pad_maximum_fusion
  105.3 4.4 %collective-permute-start.9 = (bf16[2,1024,128]{2,1,0:T(8,128)(2,1)}, bf16[2,1024,128]{2,1,0:T(8,128)(2,1)}, u32[]{:S(2)}, u32[]{:S(2)}) collective-permute-start(bf16[2,1024,128]{2,1,0:T(8,128)(2,1)} %pad_maximum_fusion), channel_id=1, source_target_pairs={{0,16},{16,32},{32,48},{48,64},{64,80},{80,96},{96,112},{1,17},{17... | collective-permute-start | bytes 1572872 | tf_op jit(solution)/shard_map/ppermute | solution.py:21
  109.7 2.7 %reshape.338 = f32[1024,2,128]{2,1,0:T(2,128)} reshape(f32[1024,256]{1,0:T(8,128)} %get-tuple-element.11) | data formatting | bytes 2097152 | tf_op jit(solution)/shard_map/reshape | solution.py:113
  112.5 3.2 %multiply_reduce_fusion = f32[1024,2]{1,0:T(8,128)} fusion(f32[1024,2,128]{2,1,0:T(2,128)} %reshape.338), kind=kLoop, calls=%fused_computation.37 | loop fusion | flops 522240 | bytes 1056768 | tf_op jit(solution)/shard_map/reduce_sum | solution.py:58
  115.7 1.2 copy.21
  117.0 1.1 bitcast_dynamic-update-slice_fusion.11
  118.1 0.3 fusion.20
  118.4 0.5 multiply_subtract_fusion
  118.9 0.3 fusion.21
  119.3 0.9 slice.120
  120.3 0.9 slice.121
  121.3 3.3 %collective-permute-start.15 = (bf16[16,5376]{1,0:T(8,128)(2,1)S(1)}, bf16[16,5376]{1,0:T(8,128)(2,1)S(1)}, u32[]{:S(2)}, u32[]{:S(2)}) collective-permute-start(bf16[16,5376]{1,0:T(8,128)(2,1)S(1)} %slice.121), channel_id=1, source_target_pairs={{0,96},{32,0},{64,32},{96,64},{1,97},{33,1},{65,33},{97,65},{2,98}... | collective-permute-start | bytes 516104 | tf_op jit(solution)/shard_map/ppermute | solution.py:27
  124.5 3.2 %collective-permute-start.12 = (bf16[32,5376]{1,0:T(8,128)(2,1)}, bf16[32,5376]{1,0:T(8,128)(2,1)S(1)}, u32[]{:S(2)}, u32[]{:S(2)}) collective-permute-start(bf16[32,5376]{1,0:T(8,128)(2,1)} %collective-permute-done.10), channel_id=1, source_target_pairs={{0,96},{32,0},{64,32},{96,64},{1,97},{33,1},{65,33},{97,65},{2,98}... | collective-permute-start | bytes 1032200 | tf_op jit(solution)/shard_map/ppermute | solution.py:27
  127.8 1.0 bitcast_dynamic-update-slice_fusion.7
  128.9 1.0 bitcast_dynamic-update-slice_fusion.9
  129.9 1.0 bitcast_dynamic-update-slice_fusion.10
  130.9 0.2 broadcast_in_dim.125
  131.3 1.2 maximum_maximum_fusion
  132.5 1.2 fusion
  133.7 1.3 fusion.2
  135.0 2.0 fusion.14
  137.0 1.2 fusion.1
  138.2 1.3 fusion.3
  139.6 2.0 fusion.17
  141.7 3.5 %collective-permute-start.18 = (bf16[16,5376]{1,0:T(8,128)(2,1)S(1)}, bf16[16,5376]{1,0:T(8,128)(2,1)S(1)}, u32[]{:S(2)}, u32[]{:S(2)}) collective-permute-start(bf16[16,5376]{1,0:T(8,128)(2,1)S(1)} %slice.123), channel_id=1, source_target_pairs={{0,96},{32,0},{64,32},{96,64},{1,97},{33,1},{65,33},{97,65},{2,98}... | collective-permute-start | bytes 516104 | tf_op jit(solution)/shard_map/ppermute | solution.py:27
  145.3 2.9 %collective-permute-done.17 = bf16[16,5376]{1,0:T(8,128)(2,1)S(1)} collective-permute-done((bf16[16,5376]{1,0:T(8,128)(2,1)S(1)}, bf16[16,5376]{1,0:T(8,128)(2,1)S(1)}, u32[]{:S(2)}, u32[]{:S(2)}) %collective-permute-start.17) | collective-permute-done | bytes 172064 | tf_op jit(solution)/shard_map/ppermute | solution.py:27
  148.4 5.9 %convolution_convert_fusion = bf16[1024,5376]{1,0:T(8,128)(2,1)} fusion(bf16[256,5376]{1,0:T(8,128)(2,1)S(1)} %bitcast.135, bf16[512,256]{0,1:T(8,128)(2,1)S(1)} %bitcast.137, bf16[512,256]{0,1:T(8,128)(2,1)S(1)} %bitcast.136), kind=kOutput, calls=%fused_computation | convolution fusion | flops 2825125888 | bytes 14286848 | tf_op jit(solution)/shard_map/dot_general | solution.py:164
  154.3 80.9 %reduce-scatter.2.cloned.1.call-done = bf16[64,5376]{1,0:T(8,128)(2,1)} async-done(((bf16[1024,5376]{1,0:T(8,128)(2,1)}), bf16[64,5376]{1,0:T(8,128)(2,1)}) %reduce-scatter.2.cloned.1.call-update) | async-done | bytes 688144 | tf_op jit(solution)/shard_map/reduce_scatter | solution.py:167
  235.2 1.3 fusion.8
  236.6 2.3 fusion.13
  (81 shorter events, 1.8 us)
Async XLA Ops:
  6.5 3.7 %copy-start.3 = (bf16[672,256]{1,0:T(8,128)(2,1)S(1)}, bf16[672,256]{1,0:T(8,128)(2,1)}, u32[]{:S(2)}) copy-start(bf16[672,256]{1,0:T(8,128)(2,1)} %param.11) | copy-start | bytes 1032196
  6.5 4.4 %copy-start.4 = (bf16[672,128]{1,0:T(8,128)(2,1)S(1)}, bf16[672,128]{1,0:T(8,128)(2,1)}, u32[]{:S(2)}) copy-start(bf16[672,128]{1,0:T(8,128)(2,1)} %param.12) | copy-start | bytes 516100
  6.5 5.1 %copy-start.5 = (bf16[672,128]{1,0:T(8,128)(2,1)S(1)}, bf16[672,128]{1,0:T(8,128)(2,1)}, u32[]{:S(2)}) copy-start(bf16[672,128]{1,0:T(8,128)(2,1)} %param.13) | copy-start | bytes 516100
  6.5 78.4 %all-gather.2.cloned.1.call-start = ((), (), s32[]{:S(2)}) async-start(), calls=%async_computation.1 | async-start | bytes 11698176 | tf_op jit(solution)/shard_map/all_gather | solution.py:97
  10.2 225.1 %reduce-scatter.2.cloned.1.call-start = ((), (), s32[]{:S(2)}) async-start(), calls=%async_computation.2 | async-start | bytes 11698176 | tf_op jit(solution)/shard_map/reduce_scatter | solution.py:167
  12.4 28.3 %collective-permute-start = (bf16[672,512]{1,0:T(8,128)(2,1)}, bf16[672,512]{1,0:T(8,128)(2,1)}, u32[]{:S(2)}, u32[]{:S(2)}) collective-permute-start(bf16[672,512]{1,0:T(8,128)(2,1)} %constant_dynamic-update-slice_fusion), channel_id=1, source_target_pairs={{0,16},{16,0},{1,17},{17,1},{2,18},{18,2},{3,19},{19,3},{4,20},{20... | collective-permute-start | bytes 2064392 | tf_op jit(solution)/shard_map/ppermute | solution.py:27
  15.7 20.9 %collective-permute-start.1 = (bf16[672,512]{1,0:T(8,128)(2,1)}, bf16[672,512]{1,0:T(8,128)(2,1)S(1)}, u32[]{:S(2)}, u32[]{:S(2)}) collective-permute-start(bf16[672,512]{1,0:T(8,128)(2,1)} %constant_dynamic-update-slice_fusion), channel_id=1, source_target_pairs={{0,96},{32,0},{64,32},{96,64},{1,97},{33,1},{65,33},{97,65},{2,98}... | collective-permute-start | bytes 2064392 | tf_op jit(solution)/shard_map/ppermute | solution.py:27
  18.5 18.0 %collective-permute-start.3 = (bf16[672,512]{1,0:T(8,128)(2,1)}, bf16[672,512]{1,0:T(8,128)(2,1)S(1)}, u32[]{:S(2)}, u32[]{:S(2)}) collective-permute-start(bf16[672,512]{1,0:T(8,128)(2,1)} %constant_dynamic-update-slice_fusion), channel_id=1, source_target_pairs={{0,32},{32,64},{64,96},{96,0},{1,33},{33,65},{65,97},{97,1},{2,34}... | collective-permute-start | bytes 2064392 | tf_op jit(solution)/shard_map/ppermute | solution.py:27
  36.5 12.3 %collective-permute-start.4 = (bf16[336,512]{1,0:T(8,128)(2,1)S(1)}, bf16[336,512]{1,0:T(8,128)(2,1)S(1)}, u32[]{:S(2)}, u32[]{:S(2)}) collective-permute-start(bf16[336,512]{1,0:T(8,128)(2,1)S(1)} %slice.105), channel_id=1, source_target_pairs={{0,32},{32,64},{64,96},{96,0},{1,33},{33,65},{65,97},{97,1},{2,34}... | collective-permute-start | bytes 1032200 | tf_op jit(solution)/shard_map/ppermute | solution.py:27
  36.6 12.2 %collective-permute-start.5 = (bf16[336,512]{1,0:T(8,128)(2,1)S(1)}, bf16[336,512]{1,0:T(8,128)(2,1)S(1)}, u32[]{:S(2)}, u32[]{:S(2)}) collective-permute-start(bf16[336,512]{1,0:T(8,128)(2,1)S(1)} %slice.106), channel_id=1, source_target_pairs={{0,96},{32,0},{64,32},{96,64},{1,97},{33,1},{65,33},{97,65},{2,98}... | collective-permute-start | bytes 1032200 | tf_op jit(solution)/shard_map/ppermute | solution.py:27
  40.6 20.5 %collective-permute-start.2 = (bf16[672,512]{1,0:T(8,128)(2,1)}, bf16[672,512]{1,0:T(8,128)(2,1)S(1)}, u32[]{:S(2)}, u32[]{:S(2)}) collective-permute-start(bf16[672,512]{1,0:T(8,128)(2,1)} %collective-permute-done), channel_id=1, source_target_pairs={{0,96},{32,0},{64,32},{96,64},{1,97},{33,1},{65,33},{97,65},{2,98}... | collective-permute-start | bytes 2064392 | tf_op jit(solution)/shard_map/ppermute | solution.py:27
  43.3 17.7 %collective-permute-start.6 = (bf16[672,512]{1,0:T(8,128)(2,1)}, bf16[672,512]{1,0:T(8,128)(2,1)S(1)}, u32[]{:S(2)}, u32[]{:S(2)}) collective-permute-start(bf16[672,512]{1,0:T(8,128)(2,1)} %collective-permute-done), channel_id=1, source_target_pairs={{0,32},{32,64},{64,96},{96,0},{1,33},{33,65},{65,97},{97,1},{2,34}... | collective-permute-start | bytes 2064392 | tf_op jit(solution)/shard_map/ppermute | solution.py:27
  61.1 8.9 %collective-permute-start.7 = (bf16[336,512]{1,0:T(8,128)(2,1)S(1)}, bf16[336,512]{1,0:T(8,128)(2,1)S(1)}, u32[]{:S(2)}, u32[]{:S(2)}) collective-permute-start(bf16[336,512]{1,0:T(8,128)(2,1)S(1)} %slice.107), channel_id=1, source_target_pairs={{0,32},{32,64},{64,96},{96,0},{1,33},{33,65},{65,97},{97,1},{2,34}... | collective-permute-start | bytes 1032200 | tf_op jit(solution)/shard_map/ppermute | solution.py:27
  61.2 8.8 %collective-permute-start.8 = (bf16[336,512]{1,0:T(8,128)(2,1)S(1)}, bf16[336,512]{1,0:T(8,128)(2,1)S(1)}, u32[]{:S(2)}, u32[]{:S(2)}) collective-permute-start(bf16[336,512]{1,0:T(8,128)(2,1)S(1)} %slice.108), channel_id=1, source_target_pairs={{0,96},{32,0},{64,32},{96,64},{1,97},{33,1},{65,33},{97,65},{2,98}... | collective-permute-start | bytes 1032200 | tf_op jit(solution)/shard_map/ppermute | solution.py:27
  95.2 6.5 %copy-start.7 = (f32[128]{0:T(128)S(1)}, f32[128]{0:T(128)}, u32[]{:S(2)}) copy-start(f32[128]{0:T(128)} %param.15) | copy-start | bytes 1540
  96.6 22.7 %collective-permute-start.13 = (bf16[32,5376]{1,0:T(8,128)(2,1)}, bf16[32,5376]{1,0:T(8,128)(2,1)}, u32[]{:S(2)}, u32[]{:S(2)}) collective-permute-start(bf16[32,5376]{1,0:T(8,128)(2,1)} %param.16), channel_id=1, source_target_pairs={{0,32},{32,64},{64,96},{96,0},{1,33},{33,65},{65,97},{97,1},{2,34}... | collective-permute-start | bytes 1032200 | tf_op jit(solution)/shard_map/ppermute | solution.py:27
  98.1 26.4 %collective-permute-start.10 = (bf16[32,5376]{1,0:T(8,128)(2,1)}, bf16[32,5376]{1,0:T(8,128)(2,1)}, u32[]{:S(2)}, u32[]{:S(2)}) collective-permute-start(bf16[32,5376]{1,0:T(8,128)(2,1)} %param.16), channel_id=1, source_target_pairs={{0,16},{16,0},{1,17},{17,1},{2,18},{18,2},{3,19},{19,3},{4,20},{20... | collective-permute-start | bytes 1032200 | tf_op jit(solution)/shard_map/ppermute | solution.py:27
  99.9 20.4 %collective-permute-start.11 = (bf16[32,5376]{1,0:T(8,128)(2,1)}, bf16[32,5376]{1,0:T(8,128)(2,1)}, u32[]{:S(2)}, u32[]{:S(2)}) collective-permute-start(bf16[32,5376]{1,0:T(8,128)(2,1)} %param.16), channel_id=1, source_target_pairs={{0,96},{32,0},{64,32},{96,64},{1,97},{33,1},{65,33},{97,65},{2,98}... | collective-permute-start | bytes 1032200 | tf_op jit(solution)/shard_map/ppermute | solution.py:27
  105.3 26.0 %collective-permute-start.9 = (bf16[2,1024,128]{2,1,0:T(8,128)(2,1)}, bf16[2,1024,128]{2,1,0:T(8,128)(2,1)}, u32[]{:S(2)}, u32[]{:S(2)}) collective-permute-start(bf16[2,1024,128]{2,1,0:T(8,128)(2,1)} %pad_maximum_fusion), channel_id=1, source_target_pairs={{0,16},{16,32},{32,48},{48,64},{64,80},{80,96},{96,112},{1,17},{17... | collective-permute-start | bytes 1572872 | tf_op jit(solution)/shard_map/ppermute | solution.py:21
  109.7 8.3 %copy-start.8 = (f32[128]{0:T(128)S(1)}, f32[128]{0:T(128)}, u32[]{:S(2)}) copy-start(f32[128]{0:T(128)} %param.14) | copy-start | bytes 1540
  116.9 1.5 copy-start.1
  116.9 1.5 copy-start.2
  120.2 10.9 %collective-permute-start.14 = (bf16[16,5376]{1,0:T(8,128)(2,1)S(1)}, bf16[16,5376]{1,0:T(8,128)(2,1)S(1)}, u32[]{:S(2)}, u32[]{:S(2)}) collective-permute-start(bf16[16,5376]{1,0:T(8,128)(2,1)S(1)} %slice.120), channel_id=1, source_target_pairs={{0,32},{32,64},{64,96},{96,0},{1,33},{33,65},{65,97},{97,1},{2,34}... | collective-permute-start | bytes 516104 | tf_op jit(solution)/shard_map/ppermute | solution.py:27
  121.3 9.9 %collective-permute-start.15 = (bf16[16,5376]{1,0:T(8,128)(2,1)S(1)}, bf16[16,5376]{1,0:T(8,128)(2,1)S(1)}, u32[]{:S(2)}, u32[]{:S(2)}) collective-permute-start(bf16[16,5376]{1,0:T(8,128)(2,1)S(1)} %slice.121), channel_id=1, source_target_pairs={{0,96},{32,0},{64,32},{96,64},{1,97},{33,1},{65,33},{97,65},{2,98}... | collective-permute-start | bytes 516104 | tf_op jit(solution)/shard_map/ppermute | solution.py:27
  124.5 17.0 %collective-permute-start.16 = (bf16[32,5376]{1,0:T(8,128)(2,1)}, bf16[32,5376]{1,0:T(8,128)(2,1)S(1)}, u32[]{:S(2)}, u32[]{:S(2)}) collective-permute-start(bf16[32,5376]{1,0:T(8,128)(2,1)} %collective-permute-done.10), channel_id=1, source_target_pairs={{0,32},{32,64},{64,96},{96,0},{1,33},{33,65},{65,97},{97,1},{2,34}... | collective-permute-start | bytes 1032200 | tf_op jit(solution)/shard_map/ppermute | solution.py:27
  124.5 17.1 %collective-permute-start.12 = (bf16[32,5376]{1,0:T(8,128)(2,1)}, bf16[32,5376]{1,0:T(8,128)(2,1)S(1)}, u32[]{:S(2)}, u32[]{:S(2)}) collective-permute-start(bf16[32,5376]{1,0:T(8,128)(2,1)} %collective-permute-done.10), channel_id=1, source_target_pairs={{0,96},{32,0},{64,32},{96,64},{1,97},{33,1},{65,33},{97,65},{2,98}... | collective-permute-start | bytes 1032200 | tf_op jit(solution)/shard_map/ppermute | solution.py:27
  141.6 6.7 %collective-permute-start.17 = (bf16[16,5376]{1,0:T(8,128)(2,1)S(1)}, bf16[16,5376]{1,0:T(8,128)(2,1)S(1)}, u32[]{:S(2)}, u32[]{:S(2)}) collective-permute-start(bf16[16,5376]{1,0:T(8,128)(2,1)S(1)} %slice.122), channel_id=1, source_target_pairs={{0,32},{32,64},{64,96},{96,0},{1,33},{33,65},{65,97},{97,1},{2,34}... | collective-permute-start | bytes 516104 | tf_op jit(solution)/shard_map/ppermute | solution.py:27
  141.7 6.6 %collective-permute-start.18 = (bf16[16,5376]{1,0:T(8,128)(2,1)S(1)}, bf16[16,5376]{1,0:T(8,128)(2,1)S(1)}, u32[]{:S(2)}, u32[]{:S(2)}) collective-permute-start(bf16[16,5376]{1,0:T(8,128)(2,1)S(1)} %slice.123), channel_id=1, source_target_pairs={{0,96},{32,0},{64,32},{96,64},{1,97},{33,1},{65,33},{97,65},{2,98}... | collective-permute-start | bytes 516104 | tf_op jit(solution)/shard_map/ppermute | solution.py:27
  154.3 82.3 %copy-start = (bf16[64,5376]{1,0:T(8,128)(2,1)S(1)}, bf16[64,5376]{1,0:T(8,128)(2,1)}, u32[]{:S(2)}) copy-start(bf16[64,5376]{1,0:T(8,128)(2,1)} %param.9) | copy-start | bytes 2064388
  154.3 82.3 %copy-start.6 = (f32[5376]{0:T(1024)S(1)}, f32[5376]{0:T(1024)}, u32[]{:S(2)}) copy-start(f32[5376]{0:T(1024)} %param.17) | copy-start | bytes 64516
Sparse Core Ops, SparseCore 0:
  10.3 74.6 all-gather.1
  154.5 80.7 reduce-scatter.1

commit v8 on v7

--- a/solution.py
+++ b/solution.py
@@ -95,10 +95,10 @@
 
     own_normed = root_mean_scale(own_rows, pre_gain).astype(jnp.bfloat16)
     normed = lax.all_gather(own_normed, HEAD, axis=0, tiled=True)
+    normed, w_output = lax.optimization_barrier((normed, w_output))
+    out_weight = gathered_over_ctx(w_output)
     tok_count = normed.shape[0]
     projected = jnp.dot(normed, w_in, preferred_element_type=jnp.float32)
-    projected, w_output = lax.optimization_barrier((projected, w_output))
-    out_weight = gathered_over_ctx(w_output)
     query_raw = projected[:, :q_cols]
     key_unnormed = projected[:, q_cols : q_cols + k_cols]
     value_unnormed = projected[:, q_cols + k_cols :]

time: 246 us -> 241 us (0.980)
  other arithmetic: 24.8 us -> 19.8 us
    reduce_sum x4, other arithmetic: 6.14 us -> 2.88 us  [root_mean_scale(): mean_sq = jnp.mean(values * values, axis=-1, keepdims=True)]
  transfers between devices with their start and end apart: 21 -> 21, of which waited for: 7 -> 10; matrix products, arithmetic and copies ran while one was open for 19% -> 17% of each run, Pallas kernels for 0% -> 0%
where the time goes in v8:
time: 241 us
  waiting for transfers between devices  126 us (52%)
  starting transfers between devices  33.8 us (14%)
  local copies, waits for them, and re-layouts  24.7 us (10%)
  matrix products  22.8 us (9%)
  other arithmetic  19.8 us (8%)
  between operations  14 us (6%)
    reduce_scatter x1, waiting for transfers between devices, body(): lax.psum_scatter(partial_value, HEAD, scatter_dimension=0, tiled=True)  83 us
    ppermute x18, waiting for transfers between devices, rotated(): return lax.ppermute(shard, axis, pairs)  30.2 us
    ppermute x18, starting transfers between devices, rotated(): return lax.ppermute(shard, axis, pairs)  29.3 us
    dynamic_update_slice x20, local copies, waits for them, and re-layouts, placed(): lax.dynamic_update_index_in_dim(stacked, part, (me + i) % count, 0)  12.8 us
    all_gather x1, waiting for transfers between devices, body(): normed = lax.all_gather(own_normed, HEAD, axis=0, tiled=True)  12.5 us
    dot_general x1, matrix products, body(): projected = jnp.dot(normed, w_in, preferred_element_type=jnp.float32)  10.3 us
    dot_general x1, matrix products, body(): jnp.dot(attended, out_weight, preferred_element_type=jnp.float32)  5.86 us
  transfers between devices with their start and end apart: 21, of which 10 were waited for; matrix products, arithmetic and copies ran while one was open for 17% of the time, Pallas kernels for 0%

profile of v8, /device:TPU:0, one launch (start us, length us, event | category | flops | bytes accessed | tf_op | source)
XLA Modules:
  0.0 240.7 jit_solution(18410239072865604457)
XLA Ops:
  6.5 1.4 fusion.10
  8.0 2.2 fusion.12
  10.2 0.8 constant_dynamic-update-slice_fusion.2
  11.0 0.7 constant_dynamic-update-slice_fusion.1
  11.7 0.7 constant_dynamic-update-slice_fusion
  12.4 3.3 %collective-permute-start = (bf16[672,512]{1,0:T(8,128)(2,1)}, bf16[672,512]{1,0:T(8,128)(2,1)}, u32[]{:S(2)}, u32[]{:S(2)}) collective-permute-start(bf16[672,512]{1,0:T(8,128)(2,1)} %constant_dynamic-update-slice_fusion), channel_id=1, source_target_pairs={{0,16},{16,0},{1,17},{17,1},{2,18},{18,2},{3,19},{19,3},{4,20},{20... | collective-permute-start | bytes 2064392 | tf_op jit(solution)/shard_map/ppermute | solution.py:27
  15.7 2.8 %collective-permute-start.1 = (bf16[672,512]{1,0:T(8,128)(2,1)}, bf16[672,512]{1,0:T(8,128)(2,1)}, u32[]{:S(2)}, u32[]{:S(2)}) collective-permute-start(bf16[672,512]{1,0:T(8,128)(2,1)} %constant_dynamic-update-slice_fusion), channel_id=1, source_target_pairs={{0,96},{32,0},{64,32},{96,64},{1,97},{33,1},{65,33},{97,65},{2,98}... | collective-permute-start | bytes 2064392 | tf_op jit(solution)/shard_map/ppermute | solution.py:27
  18.7 1.2 bitcast_dynamic-update-slice_fusion.5
  19.8 1.1 and_and_fusion.1
  21.0 2.9 %multiply_cosine_fusion = (f32[1024,64]{1,0:T(8,128)S(1)}, f32[1024,64]{1,0:T(8,128)}) fusion(f32[64]{0:T(128)S(1)} %multiply_power_fusion, f32[1024]{0:T(1024)S(1)} %get-tuple-element.24), kind=kLoop, calls=%fused_computation.38 | loop fusion | flops 65536 | bytes 528640 | tf_op jit(solution)/shard_map/cos | solution.py:67
  23.9 1.1 and_and_fusion
  25.0 11.5 %collective-permute-done.3 = bf16[672,512]{1,0:T(8,128)(2,1)S(1)} collective-permute-done((bf16[672,512]{1,0:T(8,128)(2,1)}, bf16[672,512]{1,0:T(8,128)(2,1)S(1)}, u32[]{:S(2)}, u32[]{:S(2)}) %collective-permute-start.3) | collective-permute-done | bytes 688160 | tf_op jit(solution)/shard_map/ppermute | solution.py:27
  36.6 1.0 slice.106
  37.7 3.3 %collective-permute-start.5 = (bf16[336,512]{1,0:T(8,128)(2,1)S(1)}, bf16[336,512]{1,0:T(8,128)(2,1)S(1)}, u32[]{:S(2)}, u32[]{:S(2)}) collective-permute-start(bf16[336,512]{1,0:T(8,128)(2,1)S(1)} %slice.106), channel_id=1, source_target_pairs={{0,96},{32,0},{64,32},{96,64},{1,97},{33,1},{65,33},{97,65},{2,98}... | collective-permute-start | bytes 1032200 | tf_op jit(solution)/shard_map/ppermute | solution.py:27
  40.9 2.4 %collective-permute-start.2 = (bf16[672,512]{1,0:T(8,128)(2,1)}, bf16[672,512]{1,0:T(8,128)(2,1)S(1)}, u32[]{:S(2)}, u32[]{:S(2)}) collective-permute-start(bf16[672,512]{1,0:T(8,128)(2,1)} %collective-permute-done), channel_id=1, source_target_pairs={{0,96},{32,0},{64,32},{96,64},{1,97},{33,1},{65,33},{97,65},{2,98}... | collective-permute-start | bytes 2064392 | tf_op jit(solution)/shard_map/ppermute | solution.py:27
  43.5 1.2 bitcast_dynamic-update-slice_fusion.3
  44.6 1.2 bitcast_dynamic-update-slice_fusion.4
  45.8 2.8 %broadcast_in_dim.112 = bf16[4,2,672,512]{3,2,1,0:T(8,128)(2,1)} broadcast(bf16[]{:T(256)} %constant.186.clone.1), dimensions={} | broadcast | bytes 5505026 | tf_op jit(solution)/shard_map/broadcast_in_dim | solution.py:31
  48.6 1.2 constant_dynamic-update-slice_fusion.10
  50.1 10.9 %collective-permute-done.6 = bf16[672,512]{1,0:T(8,128)(2,1)S(1)} collective-permute-done((bf16[672,512]{1,0:T(8,128)(2,1)}, bf16[672,512]{1,0:T(8,128)(2,1)S(1)}, u32[]{:S(2)}, u32[]{:S(2)}) %collective-permute-start.6) | collective-permute-done | bytes 688160 | tf_op jit(solution)/shard_map/ppermute | solution.py:27
  61.2 0.3 collective-permute-done.2
  61.6 3.7 %collective-permute-start.8 = (bf16[336,512]{1,0:T(8,128)(2,1)S(1)}, bf16[336,512]{1,0:T(8,128)(2,1)S(1)}, u32[]{:S(2)}, u32[]{:S(2)}) collective-permute-start(bf16[336,512]{1,0:T(8,128)(2,1)S(1)} %slice.108), channel_id=1, source_target_pairs={{0,96},{32,0},{64,32},{96,64},{1,97},{33,1},{65,33},{97,65},{2,98}... | collective-permute-start | bytes 1032200 | tf_op jit(solution)/shard_map/ppermute | solution.py:27
  65.3 1.3 constant_dynamic-update-slice_fusion.9
  66.6 3.4 %collective-permute-done.7 = bf16[336,512]{1,0:T(8,128)(2,1)S(1)} collective-permute-done((bf16[336,512]{1,0:T(8,128)(2,1)S(1)}, bf16[336,512]{1,0:T(8,128)(2,1)S(1)}, u32[]{:S(2)}, u32[]{:S(2)}) %collective-permute-start.7) | collective-permute-done | bytes 344096 | tf_op jit(solution)/shard_map/ppermute | solution.py:27
  70.1 1.2 constant_dynamic-update-slice_fusion.8
  71.3 1.2 constant_dynamic-update-slice_fusion.7
  72.5 12.5 %all-gather.2.cloned.1.call-done = bf16[1024,5376]{1,0:T(8,128)(2,1)} async-done(((bf16[64,5376]{1,0:T(8,128)(2,1)}), bf16[1024,5376]{1,0:T(8,128)(2,1)}) %all-gather.2.cloned.1.call-update) | async-done | bytes 11010064 | tf_op jit(solution)/shard_map/all_gather | solution.py:97
  85.0 10.3 %fusion.48 = f32[1024,512]{0,1:T(8,128)S(1)} fusion(bf16[1024,5376]{1,0:T(8,128)(2,1)} %all-gather.2.cloned.1.call-done, bf16[5376,512]{1,0:T(8,128)(2,1)} %bitcast.8), kind=kOutput, calls=%fused_computation.115 | convolution fusion | flops 5637144576 | bytes 18612224 | tf_op jit(solution)/shard_map/dot_general | solution.py:101
  95.4 1.1 slice.115
  96.6 1.9 collective-permute-start.10
  98.6 2.8 %collective-permute-start.11 = (bf16[32,5376]{1,0:T(8,128)(2,1)}, bf16[32,5376]{1,0:T(8,128)(2,1)}, u32[]{:S(2)}, u32[]{:S(2)}) collective-permute-start(bf16[32,5376]{1,0:T(8,128)(2,1)} %param.16), channel_id=1, source_target_pairs={{0,96},{32,0},{64,32},{96,64},{1,97},{33,1},{65,33},{97,65},{2,98}... | collective-permute-start | bytes 1032200 | tf_op jit(solution)/shard_map/ppermute | solution.py:27
  101.4 1.2 fusion.42
  102.6 0.8 pad_maximum_fusion
  103.5 4.4 %collective-permute-start.9 = (bf16[2,1024,128]{1,2,0:T(8,128)(2,1)}, bf16[2,1024,128]{1,2,0:T(8,128)(2,1)}, u32[]{:S(2)}, u32[]{:S(2)}) collective-permute-start(bf16[2,1024,128]{1,2,0:T(8,128)(2,1)} %pad_maximum_fusion), channel_id=1, source_target_pairs={{0,16},{16,32},{32,48},{48,64},{64,80},{80,96},{96,112},{1,17},{17... | collective-permute-start | bytes 1572872 | tf_op jit(solution)/shard_map/ppermute | solution.py:21
  107.9 1.5 copy.10
  109.5 1.1 bitcast_dynamic-update-slice_fusion.11
  110.6 0.3 multiply_multiply_fusion
  110.9 0.5 multiply_subtract_fusion
  111.4 0.3 fusion.20
  111.8 0.7 collective-permute-done.13
  112.5 0.9 slice.122
  113.5 0.9 slice.123
  114.4 3.3 %collective-permute-start.15 = (bf16[16,5376]{1,0:T(8,128)(2,1)S(1)}, bf16[16,5376]{1,0:T(8,128)(2,1)S(1)}, u32[]{:S(2)}, u32[]{:S(2)}) collective-permute-start(bf16[16,5376]{1,0:T(8,128)(2,1)S(1)} %slice.123), channel_id=1, source_target_pairs={{0,96},{32,0},{64,32},{96,64},{1,97},{33,1},{65,33},{97,65},{2,98}... | collective-permute-start | bytes 516104 | tf_op jit(solution)/shard_map/ppermute | solution.py:27
  117.7 0.5 collective-permute-start.12
  118.3 1.5 collective-permute-start.16
  119.8 1.0 bitcast_dynamic-update-slice_fusion.10
  120.8 1.0 bitcast_dynamic-update-slice_fusion.9
  121.9 1.0 bitcast_dynamic-update-slice_fusion.7
  123.3 0.5 copy-done.3
  123.8 1.1 maximum_maximum_fusion
  124.9 1.3 fusion
  126.2 1.3 fusion.2
  127.5 2.0 fusion.14
  129.6 1.3 fusion.1
  130.9 1.3 fusion.3
  132.2 2.0 fusion.17
  134.2 1.2 collective-permute-start.17
  135.5 2.4 %collective-permute-start.18 = (bf16[16,5376]{1,0:T(8,128)(2,1)S(1)}, bf16[16,5376]{1,0:T(8,128)(2,1)S(1)}, u32[]{:S(2)}, u32[]{:S(2)}) collective-permute-start(bf16[16,5376]{1,0:T(8,128)(2,1)S(1)} %slice.125), channel_id=1, source_target_pairs={{0,96},{32,0},{64,32},{96,64},{1,97},{33,1},{65,33},{97,65},{2,98}... | collective-permute-start | bytes 516104 | tf_op jit(solution)/shard_map/ppermute | solution.py:27
  138.0 2.9 %collective-permute-done.17 = bf16[16,5376]{1,0:T(8,128)(2,1)S(1)} collective-permute-done((bf16[16,5376]{1,0:T(8,128)(2,1)S(1)}, bf16[16,5376]{1,0:T(8,128)(2,1)S(1)}, u32[]{:S(2)}, u32[]{:S(2)}) %collective-permute-start.17) | collective-permute-done | bytes 172064 | tf_op jit(solution)/shard_map/ppermute | solution.py:27
  140.9 0.3 collective-permute-done.18
  141.3 5.9 %convolution_convert_fusion = bf16[1024,5376]{1,0:T(8,128)(2,1)} fusion(bf16[256,5376]{1,0:T(8,128)(2,1)S(1)} %bitcast.131, bf16[512,256]{0,1:T(8,128)(2,1)S(1)} %bitcast.134, bf16[512,256]{0,1:T(8,128)(2,1)S(1)} %bitcast.133), kind=kOutput, calls=%fused_computation | convolution fusion | flops 2825125888 | bytes 14286848 | tf_op jit(solution)/shard_map/dot_general | solution.py:164
  147.2 83.0 %reduce-scatter.2.cloned.1.call-done = bf16[64,5376]{1,0:T(8,128)(2,1)} async-done(((bf16[1024,5376]{1,0:T(8,128)(2,1)}), bf16[64,5376]{1,0:T(8,128)(2,1)}) %reduce-scatter.2.cloned.1.call-update) | async-done | bytes 688144 | tf_op jit(solution)/shard_map/reduce_scatter | solution.py:167
  230.3 1.3 fusion.8
  231.6 2.3 fusion.13
  (82 shorter events, 2.2 us)
Async XLA Ops:
  6.5 3.7 %copy-start.4 = (bf16[672,256]{1,0:T(8,128)(2,1)S(1)}, bf16[672,256]{1,0:T(8,128)(2,1)}, u32[]{:S(2)}) copy-start(bf16[672,256]{1,0:T(8,128)(2,1)} %param.11) | copy-start | bytes 1032196
  6.5 4.5 %copy-start.5 = (bf16[672,128]{1,0:T(8,128)(2,1)S(1)}, bf16[672,128]{1,0:T(8,128)(2,1)}, u32[]{:S(2)}) copy-start(bf16[672,128]{1,0:T(8,128)(2,1)} %param.12) | copy-start | bytes 516100
  6.5 5.2 %copy-start.6 = (bf16[672,128]{1,0:T(8,128)(2,1)S(1)}, bf16[672,128]{1,0:T(8,128)(2,1)}, u32[]{:S(2)}) copy-start(bf16[672,128]{1,0:T(8,128)(2,1)} %param.13) | copy-start | bytes 516100
  6.5 78.5 %all-gather.2.cloned.1.call-start = ((), (), s32[]{:S(2)}) async-start(), calls=%async_computation.1 | async-start | bytes 11698176 | tf_op jit(solution)/shard_map/all_gather | solution.py:97
  10.2 220.1 %reduce-scatter.2.cloned.1.call-start = ((), (), s32[]{:S(2)}) async-start(), calls=%async_computation.2 | async-start | bytes 11698176 | tf_op jit(solution)/shard_map/reduce_scatter | solution.py:167
  12.4 28.5 %collective-permute-start = (bf16[672,512]{1,0:T(8,128)(2,1)}, bf16[672,512]{1,0:T(8,128)(2,1)}, u32[]{:S(2)}, u32[]{:S(2)}) collective-permute-start(bf16[672,512]{1,0:T(8,128)(2,1)} %constant_dynamic-update-slice_fusion), channel_id=1, source_target_pairs={{0,16},{16,0},{1,17},{17,1},{2,18},{18,2},{3,19},{19,3},{4,20},{20... | collective-permute-start | bytes 2064392 | tf_op jit(solution)/shard_map/ppermute | solution.py:27
  15.7 20.9 %collective-permute-start.1 = (bf16[672,512]{1,0:T(8,128)(2,1)}, bf16[672,512]{1,0:T(8,128)(2,1)}, u32[]{:S(2)}, u32[]{:S(2)}) collective-permute-start(bf16[672,512]{1,0:T(8,128)(2,1)} %constant_dynamic-update-slice_fusion), channel_id=1, source_target_pairs={{0,96},{32,0},{64,32},{96,64},{1,97},{33,1},{65,33},{97,65},{2,98}... | collective-permute-start | bytes 2064392 | tf_op jit(solution)/shard_map/ppermute | solution.py:27
  18.5 18.0 %collective-permute-start.3 = (bf16[672,512]{1,0:T(8,128)(2,1)}, bf16[672,512]{1,0:T(8,128)(2,1)S(1)}, u32[]{:S(2)}, u32[]{:S(2)}) collective-permute-start(bf16[672,512]{1,0:T(8,128)(2,1)} %constant_dynamic-update-slice_fusion), channel_id=1, source_target_pairs={{0,32},{32,64},{64,96},{96,0},{1,33},{33,65},{65,97},{97,1},{2,34}... | collective-permute-start | bytes 2064392 | tf_op jit(solution)/shard_map/ppermute | solution.py:27
  36.6 13.4 %collective-permute-start.4 = (bf16[336,512]{1,0:T(8,128)(2,1)S(1)}, bf16[336,512]{1,0:T(8,128)(2,1)S(1)}, u32[]{:S(2)}, u32[]{:S(2)}) collective-permute-start(bf16[336,512]{1,0:T(8,128)(2,1)S(1)} %slice.105), channel_id=1, source_target_pairs={{0,32},{32,64},{64,96},{96,0},{1,33},{33,65},{65,97},{97,1},{2,34}... | collective-permute-start | bytes 1032200 | tf_op jit(solution)/shard_map/ppermute | solution.py:27
  37.7 12.3 %collective-permute-start.5 = (bf16[336,512]{1,0:T(8,128)(2,1)S(1)}, bf16[336,512]{1,0:T(8,128)(2,1)S(1)}, u32[]{:S(2)}, u32[]{:S(2)}) collective-permute-start(bf16[336,512]{1,0:T(8,128)(2,1)S(1)} %slice.106), channel_id=1, source_target_pairs={{0,96},{32,0},{64,32},{96,64},{1,97},{33,1},{65,33},{97,65},{2,98}... | collective-permute-start | bytes 1032200 | tf_op jit(solution)/shard_map/ppermute | solution.py:27
  40.9 20.6 %collective-permute-start.2 = (bf16[672,512]{1,0:T(8,128)(2,1)}, bf16[672,512]{1,0:T(8,128)(2,1)S(1)}, u32[]{:S(2)}, u32[]{:S(2)}) collective-permute-start(bf16[672,512]{1,0:T(8,128)(2,1)} %collective-permute-done), channel_id=1, source_target_pairs={{0,96},{32,0},{64,32},{96,64},{1,97},{33,1},{65,33},{97,65},{2,98}... | collective-permute-start | bytes 2064392 | tf_op jit(solution)/shard_map/ppermute | solution.py:27
  43.4 17.7 %collective-permute-start.6 = (bf16[672,512]{1,0:T(8,128)(2,1)}, bf16[672,512]{1,0:T(8,128)(2,1)S(1)}, u32[]{:S(2)}, u32[]{:S(2)}) collective-permute-start(bf16[672,512]{1,0:T(8,128)(2,1)} %collective-permute-done), channel_id=1, source_target_pairs={{0,32},{32,64},{64,96},{96,0},{1,33},{33,65},{65,97},{97,1},{2,34}... | collective-permute-start | bytes 2064392 | tf_op jit(solution)/shard_map/ppermute | solution.py:27
  61.1 8.9 %collective-permute-start.7 = (bf16[336,512]{1,0:T(8,128)(2,1)S(1)}, bf16[336,512]{1,0:T(8,128)(2,1)S(1)}, u32[]{:S(2)}, u32[]{:S(2)}) collective-permute-start(bf16[336,512]{1,0:T(8,128)(2,1)S(1)} %slice.107), channel_id=1, source_target_pairs={{0,32},{32,64},{64,96},{96,0},{1,33},{33,65},{65,97},{97,1},{2,34}... | collective-permute-start | bytes 1032200 | tf_op jit(solution)/shard_map/ppermute | solution.py:27
  61.6 8.5 %collective-permute-start.8 = (bf16[336,512]{1,0:T(8,128)(2,1)S(1)}, bf16[336,512]{1,0:T(8,128)(2,1)S(1)}, u32[]{:S(2)}, u32[]{:S(2)}) collective-permute-start(bf16[336,512]{1,0:T(8,128)(2,1)S(1)} %slice.108), channel_id=1, source_target_pairs={{0,96},{32,0},{64,32},{96,64},{1,97},{33,1},{65,33},{97,65},{2,98}... | collective-permute-start | bytes 1032200 | tf_op jit(solution)/shard_map/ppermute | solution.py:27
  95.3 6.0 %copy-start.8 = (f32[128]{0:T(128)S(1)}, f32[128]{0:T(128)}, u32[]{:S(2)}) copy-start(f32[128]{0:T(128)} %param.15) | copy-start | bytes 1540
  96.6 21.1 %collective-permute-start.10 = (bf16[32,5376]{1,0:T(8,128)(2,1)}, bf16[32,5376]{1,0:T(8,128)(2,1)}, u32[]{:S(2)}, u32[]{:S(2)}) collective-permute-start(bf16[32,5376]{1,0:T(8,128)(2,1)} %param.16), channel_id=1, source_target_pairs={{0,16},{16,0},{1,17},{17,1},{2,18},{18,2},{3,19},{19,3},{4,20},{20... | collective-permute-start | bytes 1032200 | tf_op jit(solution)/shard_map/ppermute | solution.py:27
  98.6 14.9 %collective-permute-start.11 = (bf16[32,5376]{1,0:T(8,128)(2,1)}, bf16[32,5376]{1,0:T(8,128)(2,1)}, u32[]{:S(2)}, u32[]{:S(2)}) collective-permute-start(bf16[32,5376]{1,0:T(8,128)(2,1)} %param.16), channel_id=1, source_target_pairs={{0,96},{32,0},{64,32},{96,64},{1,97},{33,1},{65,33},{97,65},{2,98}... | collective-permute-start | bytes 1032200 | tf_op jit(solution)/shard_map/ppermute | solution.py:27
  101.3 11.2 %collective-permute-start.13 = (bf16[32,5376]{1,0:T(8,128)(2,1)}, bf16[32,5376]{1,0:T(8,128)(2,1)}, u32[]{:S(2)}, u32[]{:S(2)}) collective-permute-start(bf16[32,5376]{1,0:T(8,128)(2,1)} %param.16), channel_id=1, source_target_pairs={{0,32},{32,64},{64,96},{96,0},{1,33},{33,65},{65,97},{97,1},{2,34}... | collective-permute-start | bytes 1032200 | tf_op jit(solution)/shard_map/ppermute | solution.py:27
  101.4 9.1 %copy-start.9 = (f32[128]{0:T(128)S(1)}, f32[128]{0:T(128)}, u32[]{:S(2)}) copy-start(f32[128]{0:T(128)} %param.14) | copy-start | bytes 1540
  102.6 5.3 %copy-start.2 = (bf16[1,1024,64]{1,2,0:T(8,128)(2,1)}, bf16[1,1024,64]{1,2,0:T(8,128)(2,1)S(1)}, u32[]{:S(2)}) copy-start(bf16[1,1024,64]{1,2,0:T(8,128)(2,1)S(1)} %get-tuple-element.12) | copy-start | bytes 393220
  103.5 19.8 %collective-permute-start.9 = (bf16[2,1024,128]{1,2,0:T(8,128)(2,1)}, bf16[2,1024,128]{1,2,0:T(8,128)(2,1)}, u32[]{:S(2)}, u32[]{:S(2)}) collective-permute-start(bf16[2,1024,128]{1,2,0:T(8,128)(2,1)} %pad_maximum_fusion), channel_id=1, source_target_pairs={{0,16},{16,32},{32,48},{48,64},{64,80},{80,96},{96,112},{1,17},{17... | collective-permute-start | bytes 1572872 | tf_op jit(solution)/shard_map/ppermute | solution.py:21
  109.4 1.5 copy-start.1
  113.4 9.8 %collective-permute-start.14 = (bf16[16,5376]{1,0:T(8,128)(2,1)S(1)}, bf16[16,5376]{1,0:T(8,128)(2,1)S(1)}, u32[]{:S(2)}, u32[]{:S(2)}) collective-permute-start(bf16[16,5376]{1,0:T(8,128)(2,1)S(1)} %slice.122), channel_id=1, source_target_pairs={{0,32},{32,64},{64,96},{96,0},{1,33},{33,65},{65,97},{97,1},{2,34}... | collective-permute-start | bytes 516104 | tf_op jit(solution)/shard_map/ppermute | solution.py:27
  114.4 8.8 %collective-permute-start.15 = (bf16[16,5376]{1,0:T(8,128)(2,1)S(1)}, bf16[16,5376]{1,0:T(8,128)(2,1)S(1)}, u32[]{:S(2)}, u32[]{:S(2)}) collective-permute-start(bf16[16,5376]{1,0:T(8,128)(2,1)S(1)} %slice.123), channel_id=1, source_target_pairs={{0,96},{32,0},{64,32},{96,64},{1,97},{33,1},{65,33},{97,65},{2,98}... | collective-permute-start | bytes 516104 | tf_op jit(solution)/shard_map/ppermute | solution.py:27
  117.7 17.7 %collective-permute-start.12 = (bf16[32,5376]{1,0:T(8,128)(2,1)}, bf16[32,5376]{1,0:T(8,128)(2,1)S(1)}, u32[]{:S(2)}, u32[]{:S(2)}) collective-permute-start(bf16[32,5376]{1,0:T(8,128)(2,1)} %collective-permute-done.10), channel_id=1, source_target_pairs={{0,96},{32,0},{64,32},{96,64},{1,97},{33,1},{65,33},{97,65},{2,98}... | collective-permute-start | bytes 1032200 | tf_op jit(solution)/shard_map/ppermute | solution.py:27
  118.3 15.9 %collective-permute-start.16 = (bf16[32,5376]{1,0:T(8,128)(2,1)}, bf16[32,5376]{1,0:T(8,128)(2,1)S(1)}, u32[]{:S(2)}, u32[]{:S(2)}) collective-permute-start(bf16[32,5376]{1,0:T(8,128)(2,1)} %collective-permute-done.10), channel_id=1, source_target_pairs={{0,32},{32,64},{64,96},{96,0},{1,33},{33,65},{65,97},{97,1},{2,34}... | collective-permute-start | bytes 1032200 | tf_op jit(solution)/shard_map/ppermute | solution.py:27
  122.9 0.9 copy-start.3
  134.2 6.7 %collective-permute-start.17 = (bf16[16,5376]{1,0:T(8,128)(2,1)S(1)}, bf16[16,5376]{1,0:T(8,128)(2,1)S(1)}, u32[]{:S(2)}, u32[]{:S(2)}) collective-permute-start(bf16[16,5376]{1,0:T(8,128)(2,1)S(1)} %slice.124), channel_id=1, source_target_pairs={{0,32},{32,64},{64,96},{96,0},{1,33},{33,65},{65,97},{97,1},{2,34}... | collective-permute-start | bytes 516104 | tf_op jit(solution)/shard_map/ppermute | solution.py:27
  135.5 5.7 %collective-permute-start.18 = (bf16[16,5376]{1,0:T(8,128)(2,1)S(1)}, bf16[16,5376]{1,0:T(8,128)(2,1)S(1)}, u32[]{:S(2)}, u32[]{:S(2)}) collective-permute-start(bf16[16,5376]{1,0:T(8,128)(2,1)S(1)} %slice.125), channel_id=1, source_target_pairs={{0,96},{32,0},{64,32},{96,64},{1,97},{33,1},{65,33},{97,65},{2,98}... | collective-permute-start | bytes 516104 | tf_op jit(solution)/shard_map/ppermute | solution.py:27
  147.2 84.4 %copy-start = (bf16[64,5376]{1,0:T(8,128)(2,1)S(1)}, bf16[64,5376]{1,0:T(8,128)(2,1)}, u32[]{:S(2)}) copy-start(bf16[64,5376]{1,0:T(8,128)(2,1)} %param.9) | copy-start | bytes 2064388
  147.2 84.4 %copy-start.7 = (f32[5376]{0:T(1024)S(1)}, f32[5376]{0:T(1024)}, u32[]{:S(2)}) copy-start(f32[5376]{0:T(1024)} %param.17) | copy-start | bytes 64516
Sparse Core Ops, SparseCore 0:
  10.3 74.6 all-gather.1
  147.4 82.8 reduce-scatter.1

commit v9 on v8

--- a/solution.py
+++ b/solution.py
@@ -2,6 +2,7 @@
 import jax.numpy as jnp
 from jax import lax
 from jax.sharding import Mesh, PartitionSpec as P
+
 
 HEAD_SIZE = 128
 WINDOW_SPAN = 1024
@@ -48,7 +49,8 @@
     cy = lax.axis_index("cy")
     cx = lax.axis_index("cx")
     own = ring_over_cx(piece)
-    partner = ring_over_cx(rotated(piece, "cy", 1))
+    crossed = rotated(piece, "cy", 1)
+    partner = ring_over_cx(crossed)
     pairs = [placed([a, b], cy, 2) for a, b in zip(own, partner)]
     ring = placed(pairs, cx, 4)
     return ring.reshape((8 * piece.shape[0],) + piece.shape[1:])
@@ -77,7 +79,7 @@
     )
 
 
-def body(
+def layer(
     hidden_in,
     pre_gain,
     w_query,
@@ -179,7 +181,7 @@
     rows_spec = P(CTX + HEAD, None)
     cols_spec = P(CTX, HEAD)
     return jax.shard_map(
-        body,
+        layer,
         mesh=view,
         in_specs=(
             rows_spec,

time: 241 us -> 241 us (level)
  no operation moved by 1% of the time
where the time goes in v9:
time: 241 us
  waiting for transfers between devices  126 us (52%)
  starting transfers between devices  33.8 us (14%)
  local copies, waits for them, and re-layouts  24.7 us (10%)
  matrix products  22.8 us (9%)
  other arithmetic  19.8 us (8%)
  between operations  14 us (6%)
    reduce_scatter x1, waiting for transfers between devices, layer(): lax.psum_scatter(partial_value, HEAD, scatter_dimension=0, tiled=True)  83 us
    ppermute x18, waiting for transfers between devices, rotated(): return lax.ppermute(shard, axis, pairs)  30.2 us
    ppermute x18, starting transfers between devices, rotated(): return lax.ppermute(shard, axis, pairs)  29.3 us
    dynamic_update_slice x20, local copies, waits for them, and re-layouts, placed(): lax.dynamic_update_index_in_dim(stacked, part, (me + i) % count, 0)  12.8 us
    all_gather x1, waiting for transfers between devices, layer(): normed = lax.all_gather(own_normed, HEAD, axis=0, tiled=True)  12.5 us
    dot_general x1, matrix products, layer(): projected = jnp.dot(normed, w_in, preferred_element_type=jnp.float32)  10.3 us
    dot_general x1, matrix products, layer(): jnp.dot(attended, out_weight, preferred_element_type=jnp.float32)  5.86 us
  transfers between devices with their start and end apart: 21, of which 10 were waited for; matrix products, arithmetic and copies ran while one was open for 17% of the time, Pallas kernels for 0%

profile of v9, /device:TPU:0, one launch (start us, length us, event | category | flops | bytes accessed | tf_op | source)
XLA Modules:
  0.0 240.7 jit_solution(18410239072865604457)
XLA Ops:
  6.5 1.4 fusion.10
  8.0 2.2 fusion.12
  10.2 0.8 constant_dynamic-update-slice_fusion.2
  11.0 0.7 constant_dynamic-update-slice_fusion.1
  11.7 0.7 constant_dynamic-update-slice_fusion
  12.4 3.3 %collective-permute-start = (bf16[672,512]{1,0:T(8,128)(2,1)}, bf16[672,512]{1,0:T(8,128)(2,1)}, u32[]{:S(2)}, u32[]{:S(2)}) collective-permute-start(bf16[672,512]{1,0:T(8,128)(2,1)} %constant_dynamic-update-slice_fusion), channel_id=1, source_target_pairs={{0,16},{16,0},{1,17},{17,1},{2,18},{18,2},{3,19},{19,3},{4,20},{20... | collective-permute-start | bytes 2064392 | tf_op jit(solution)/shard_map/ppermute | solution.py:28
  15.7 2.8 %collective-permute-start.1 = (bf16[672,512]{1,0:T(8,128)(2,1)}, bf16[672,512]{1,0:T(8,128)(2,1)}, u32[]{:S(2)}, u32[]{:S(2)}) collective-permute-start(bf16[672,512]{1,0:T(8,128)(2,1)} %constant_dynamic-update-slice_fusion), channel_id=1, source_target_pairs={{0,96},{32,0},{64,32},{96,64},{1,97},{33,1},{65,33},{97,65},{2,98}... | collective-permute-start | bytes 2064392 | tf_op jit(solution)/shard_map/ppermute | solution.py:28
  18.7 1.2 bitcast_dynamic-update-slice_fusion.5
  19.8 1.1 and_and_fusion.1
  21.0 2.9 %multiply_cosine_fusion = (f32[1024,64]{1,0:T(8,128)S(1)}, f32[1024,64]{1,0:T(8,128)}) fusion(f32[64]{0:T(128)S(1)} %multiply_power_fusion, f32[1024]{0:T(1024)S(1)} %get-tuple-element.24), kind=kLoop, calls=%fused_computation.38 | loop fusion | flops 65536 | bytes 528640 | tf_op jit(solution)/shard_map/cos | solution.py:69
  23.9 1.1 and_and_fusion
  25.0 11.5 %collective-permute-done.3 = bf16[672,512]{1,0:T(8,128)(2,1)S(1)} collective-permute-done((bf16[672,512]{1,0:T(8,128)(2,1)}, bf16[672,512]{1,0:T(8,128)(2,1)S(1)}, u32[]{:S(2)}, u32[]{:S(2)}) %collective-permute-start.3) | collective-permute-done | bytes 688160 | tf_op jit(solution)/shard_map/ppermute | solution.py:28
  36.6 1.0 slice.106
  37.7 3.3 %collective-permute-start.5 = (bf16[336,512]{1,0:T(8,128)(2,1)S(1)}, bf16[336,512]{1,0:T(8,128)(2,1)S(1)}, u32[]{:S(2)}, u32[]{:S(2)}) collective-permute-start(bf16[336,512]{1,0:T(8,128)(2,1)S(1)} %slice.106), channel_id=1, source_target_pairs={{0,96},{32,0},{64,32},{96,64},{1,97},{33,1},{65,33},{97,65},{2,98}... | collective-permute-start | bytes 1032200 | tf_op jit(solution)/shard_map/ppermute | solution.py:28
  40.9 2.4 %collective-permute-start.2 = (bf16[672,512]{1,0:T(8,128)(2,1)}, bf16[672,512]{1,0:T(8,128)(2,1)S(1)}, u32[]{:S(2)}, u32[]{:S(2)}) collective-permute-start(bf16[672,512]{1,0:T(8,128)(2,1)} %collective-permute-done), channel_id=1, source_target_pairs={{0,96},{32,0},{64,32},{96,64},{1,97},{33,1},{65,33},{97,65},{2,98}... | collective-permute-start | bytes 2064392 | tf_op jit(solution)/shard_map/ppermute | solution.py:28
  43.5 1.2 bitcast_dynamic-update-slice_fusion.3
  44.6 1.2 bitcast_dynamic-update-slice_fusion.4
  45.8 2.8 %broadcast_in_dim.112 = bf16[4,2,672,512]{3,2,1,0:T(8,128)(2,1)} broadcast(bf16[]{:T(256)} %constant.186.clone.1), dimensions={} | broadcast | bytes 5505026 | tf_op jit(solution)/shard_map/broadcast_in_dim | solution.py:32
  48.6 1.2 constant_dynamic-update-slice_fusion.10
  50.1 10.9 %collective-permute-done.6 = bf16[672,512]{1,0:T(8,128)(2,1)S(1)} collective-permute-done((bf16[672,512]{1,0:T(8,128)(2,1)}, bf16[672,512]{1,0:T(8,128)(2,1)S(1)}, u32[]{:S(2)}, u32[]{:S(2)}) %collective-permute-start.6) | collective-permute-done | bytes 688160 | tf_op jit(solution)/shard_map/ppermute | solution.py:28
  61.2 0.3 collective-permute-done.2
  61.6 3.7 %collective-permute-start.8 = (bf16[336,512]{1,0:T(8,128)(2,1)S(1)}, bf16[336,512]{1,0:T(8,128)(2,1)S(1)}, u32[]{:S(2)}, u32[]{:S(2)}) collective-permute-start(bf16[336,512]{1,0:T(8,128)(2,1)S(1)} %slice.108), channel_id=1, source_target_pairs={{0,96},{32,0},{64,32},{96,64},{1,97},{33,1},{65,33},{97,65},{2,98}... | collective-permute-start | bytes 1032200 | tf_op jit(solution)/shard_map/ppermute | solution.py:28
  65.3 1.3 constant_dynamic-update-slice_fusion.9
  66.6 3.4 %collective-permute-done.7 = bf16[336,512]{1,0:T(8,128)(2,1)S(1)} collective-permute-done((bf16[336,512]{1,0:T(8,128)(2,1)S(1)}, bf16[336,512]{1,0:T(8,128)(2,1)S(1)}, u32[]{:S(2)}, u32[]{:S(2)}) %collective-permute-start.7) | collective-permute-done | bytes 344096 | tf_op jit(solution)/shard_map/ppermute | solution.py:28
  70.1 1.2 constant_dynamic-update-slice_fusion.8
  71.3 1.2 constant_dynamic-update-slice_fusion.7
  72.5 12.5 %all-gather.2.cloned.1.call-done = bf16[1024,5376]{1,0:T(8,128)(2,1)} async-done(((bf16[64,5376]{1,0:T(8,128)(2,1)}), bf16[1024,5376]{1,0:T(8,128)(2,1)}) %all-gather.2.cloned.1.call-update) | async-done | bytes 11010064 | tf_op jit(solution)/shard_map/all_gather | solution.py:99
  85.0 10.3 %fusion.48 = f32[1024,512]{0,1:T(8,128)S(1)} fusion(bf16[1024,5376]{1,0:T(8,128)(2,1)} %all-gather.2.cloned.1.call-done, bf16[5376,512]{1,0:T(8,128)(2,1)} %bitcast.8), kind=kOutput, calls=%fused_computation.115 | convolution fusion | flops 5637144576 | bytes 18612224 | tf_op jit(solution)/shard_map/dot_general | solution.py:103
  95.4 1.1 slice.115
  96.6 1.9 collective-permute-start.10
  98.6 2.8 %collective-permute-start.11 = (bf16[32,5376]{1,0:T(8,128)(2,1)}, bf16[32,5376]{1,0:T(8,128)(2,1)}, u32[]{:S(2)}, u32[]{:S(2)}) collective-permute-start(bf16[32,5376]{1,0:T(8,128)(2,1)} %param.16), channel_id=1, source_target_pairs={{0,96},{32,0},{64,32},{96,64},{1,97},{33,1},{65,33},{97,65},{2,98}... | collective-permute-start | bytes 1032200 | tf_op jit(solution)/shard_map/ppermute | solution.py:28
  101.4 1.2 fusion.42
  102.6 0.8 pad_maximum_fusion
  103.5 4.4 %collective-permute-start.9 = (bf16[2,1024,128]{1,2,0:T(8,128)(2,1)}, bf16[2,1024,128]{1,2,0:T(8,128)(2,1)}, u32[]{:S(2)}, u32[]{:S(2)}) collective-permute-start(bf16[2,1024,128]{1,2,0:T(8,128)(2,1)} %pad_maximum_fusion), channel_id=1, source_target_pairs={{0,16},{16,32},{32,48},{48,64},{64,80},{80,96},{96,112},{1,17},{17... | collective-permute-start | bytes 1572872 | tf_op jit(solution)/shard_map/ppermute | solution.py:22
  107.9 1.5 copy.10
  109.5 1.1 bitcast_dynamic-update-slice_fusion.11
  110.6 0.3 multiply_multiply_fusion
  110.9 0.5 multiply_subtract_fusion
  111.4 0.3 fusion.20
  111.8 0.7 collective-permute-done.13
  112.5 0.9 slice.122
  113.5 0.9 slice.123
  114.4 3.3 %collective-permute-start.15 = (bf16[16,5376]{1,0:T(8,128)(2,1)S(1)}, bf16[16,5376]{1,0:T(8,128)(2,1)S(1)}, u32[]{:S(2)}, u32[]{:S(2)}) collective-permute-start(bf16[16,5376]{1,0:T(8,128)(2,1)S(1)} %slice.123), channel_id=1, source_target_pairs={{0,96},{32,0},{64,32},{96,64},{1,97},{33,1},{65,33},{97,65},{2,98}... | collective-permute-start | bytes 516104 | tf_op jit(solution)/shard_map/ppermute | solution.py:28
  117.7 0.5 collective-permute-start.12
  118.3 1.5 collective-permute-start.16
  119.8 1.0 bitcast_dynamic-update-slice_fusion.10
  120.8 1.0 bitcast_dynamic-update-slice_fusion.9
  121.9 1.0 bitcast_dynamic-update-slice_fusion.7
  123.3 0.5 copy-done.3
  123.8 1.1 maximum_maximum_fusion
  124.9 1.3 fusion
  126.2 1.3 fusion.2
  127.5 2.0 fusion.14
  129.6 1.3 fusion.1
  130.9 1.3 fusion.3
  132.2 2.0 fusion.17
  134.2 1.2 collective-permute-start.17
  135.5 2.4 %collective-permute-start.18 = (bf16[16,5376]{1,0:T(8,128)(2,1)S(1)}, bf16[16,5376]{1,0:T(8,128)(2,1)S(1)}, u32[]{:S(2)}, u32[]{:S(2)}) collective-permute-start(bf16[16,5376]{1,0:T(8,128)(2,1)S(1)} %slice.125), channel_id=1, source_target_pairs={{0,96},{32,0},{64,32},{96,64},{1,97},{33,1},{65,33},{97,65},{2,98}... | collective-permute-start | bytes 516104 | tf_op jit(solution)/shard_map/ppermute | solution.py:28
  138.0 2.9 %collective-permute-done.17 = bf16[16,5376]{1,0:T(8,128)(2,1)S(1)} collective-permute-done((bf16[16,5376]{1,0:T(8,128)(2,1)S(1)}, bf16[16,5376]{1,0:T(8,128)(2,1)S(1)}, u32[]{:S(2)}, u32[]{:S(2)}) %collective-permute-start.17) | collective-permute-done | bytes 172064 | tf_op jit(solution)/shard_map/ppermute | solution.py:28
  140.9 0.3 collective-permute-done.18
  141.3 5.9 %convolution_convert_fusion = bf16[1024,5376]{1,0:T(8,128)(2,1)} fusion(bf16[256,5376]{1,0:T(8,128)(2,1)S(1)} %bitcast.131, bf16[512,256]{0,1:T(8,128)(2,1)S(1)} %bitcast.134, bf16[512,256]{0,1:T(8,128)(2,1)S(1)} %bitcast.133), kind=kOutput, calls=%fused_computation | convolution fusion | flops 2825125888 | bytes 14286848 | tf_op jit(solution)/shard_map/dot_general | solution.py:166
  147.2 83.0 %reduce-scatter.2.cloned.1.call-done = bf16[64,5376]{1,0:T(8,128)(2,1)} async-done(((bf16[1024,5376]{1,0:T(8,128)(2,1)}), bf16[64,5376]{1,0:T(8,128)(2,1)}) %reduce-scatter.2.cloned.1.call-update) | async-done | bytes 688144 | tf_op jit(solution)/shard_map/reduce_scatter | solution.py:169
  230.3 1.3 fusion.8
  231.6 2.3 fusion.13
  (82 shorter events, 2.2 us)
Async XLA Ops:
  6.5 3.7 %copy-start.4 = (bf16[672,256]{1,0:T(8,128)(2,1)S(1)}, bf16[672,256]{1,0:T(8,128)(2,1)}, u32[]{:S(2)}) copy-start(bf16[672,256]{1,0:T(8,128)(2,1)} %param.11) | copy-start | bytes 1032196
  6.5 4.5 %copy-start.5 = (bf16[672,128]{1,0:T(8,128)(2,1)S(1)}, bf16[672,128]{1,0:T(8,128)(2,1)}, u32[]{:S(2)}) copy-start(bf16[672,128]{1,0:T(8,128)(2,1)} %param.12) | copy-start | bytes 516100
  6.5 5.2 %copy-start.6 = (bf16[672,128]{1,0:T(8,128)(2,1)S(1)}, bf16[672,128]{1,0:T(8,128)(2,1)}, u32[]{:S(2)}) copy-start(bf16[672,128]{1,0:T(8,128)(2,1)} %param.13) | copy-start | bytes 516100
  6.5 78.5 %all-gather.2.cloned.1.call-start = ((), (), s32[]{:S(2)}) async-start(), calls=%async_computation.1 | async-start | bytes 11698176 | tf_op jit(solution)/shard_map/all_gather | solution.py:99
  10.2 220.1 %reduce-scatter.2.cloned.1.call-start = ((), (), s32[]{:S(2)}) async-start(), calls=%async_computation.2 | async-start | bytes 11698176 | tf_op jit(solution)/shard_map/reduce_scatter | solution.py:169
  12.4 28.5 %collective-permute-start = (bf16[672,512]{1,0:T(8,128)(2,1)}, bf16[672,512]{1,0:T(8,128)(2,1)}, u32[]{:S(2)}, u32[]{:S(2)}) collective-permute-start(bf16[672,512]{1,0:T(8,128)(2,1)} %constant_dynamic-update-slice_fusion), channel_id=1, source_target_pairs={{0,16},{16,0},{1,17},{17,1},{2,18},{18,2},{3,19},{19,3},{4,20},{20... | collective-permute-start | bytes 2064392 | tf_op jit(solution)/shard_map/ppermute | solution.py:28
  15.7 20.9 %collective-permute-start.1 = (bf16[672,512]{1,0:T(8,128)(2,1)}, bf16[672,512]{1,0:T(8,128)(2,1)}, u32[]{:S(2)}, u32[]{:S(2)}) collective-permute-start(bf16[672,512]{1,0:T(8,128)(2,1)} %constant_dynamic-update-slice_fusion), channel_id=1, source_target_pairs={{0,96},{32,0},{64,32},{96,64},{1,97},{33,1},{65,33},{97,65},{2,98}... | collective-permute-start | bytes 2064392 | tf_op jit(solution)/shard_map/ppermute | solution.py:28
  18.5 18.0 %collective-permute-start.3 = (bf16[672,512]{1,0:T(8,128)(2,1)}, bf16[672,512]{1,0:T(8,128)(2,1)S(1)}, u32[]{:S(2)}, u32[]{:S(2)}) collective-permute-start(bf16[672,512]{1,0:T(8,128)(2,1)} %constant_dynamic-update-slice_fusion), channel_id=1, source_target_pairs={{0,32},{32,64},{64,96},{96,0},{1,33},{33,65},{65,97},{97,1},{2,34}... | collective-permute-start | bytes 2064392 | tf_op jit(solution)/shard_map/ppermute | solution.py:28
  36.6 13.4 %collective-permute-start.4 = (bf16[336,512]{1,0:T(8,128)(2,1)S(1)}, bf16[336,512]{1,0:T(8,128)(2,1)S(1)}, u32[]{:S(2)}, u32[]{:S(2)}) collective-permute-start(bf16[336,512]{1,0:T(8,128)(2,1)S(1)} %slice.105), channel_id=1, source_target_pairs={{0,32},{32,64},{64,96},{96,0},{1,33},{33,65},{65,97},{97,1},{2,34}... | collective-permute-start | bytes 1032200 | tf_op jit(solution)/shard_map/ppermute | solution.py:28
  37.7 12.3 %collective-permute-start.5 = (bf16[336,512]{1,0:T(8,128)(2,1)S(1)}, bf16[336,512]{1,0:T(8,128)(2,1)S(1)}, u32[]{:S(2)}, u32[]{:S(2)}) collective-permute-start(bf16[336,512]{1,0:T(8,128)(2,1)S(1)} %slice.106), channel_id=1, source_target_pairs={{0,96},{32,0},{64,32},{96,64},{1,97},{33,1},{65,33},{97,65},{2,98}... | collective-permute-start | bytes 1032200 | tf_op jit(solution)/shard_map/ppermute | solution.py:28
  40.9 20.6 %collective-permute-start.2 = (bf16[672,512]{1,0:T(8,128)(2,1)}, bf16[672,512]{1,0:T(8,128)(2,1)S(1)}, u32[]{:S(2)}, u32[]{:S(2)}) collective-permute-start(bf16[672,512]{1,0:T(8,128)(2,1)} %collective-permute-done), channel_id=1, source_target_pairs={{0,96},{32,0},{64,32},{96,64},{1,97},{33,1},{65,33},{97,65},{2,98}... | collective-permute-start | bytes 2064392 | tf_op jit(solution)/shard_map/ppermute | solution.py:28
  43.4 17.7 %collective-permute-start.6 = (bf16[672,512]{1,0:T(8,128)(2,1)}, bf16[672,512]{1,0:T(8,128)(2,1)S(1)}, u32[]{:S(2)}, u32[]{:S(2)}) collective-permute-start(bf16[672,512]{1,0:T(8,128)(2,1)} %collective-permute-done), channel_id=1, source_target_pairs={{0,32},{32,64},{64,96},{96,0},{1,33},{33,65},{65,97},{97,1},{2,34}... | collective-permute-start | bytes 2064392 | tf_op jit(solution)/shard_map/ppermute | solution.py:28
  61.1 8.9 %collective-permute-start.7 = (bf16[336,512]{1,0:T(8,128)(2,1)S(1)}, bf16[336,512]{1,0:T(8,128)(2,1)S(1)}, u32[]{:S(2)}, u32[]{:S(2)}) collective-permute-start(bf16[336,512]{1,0:T(8,128)(2,1)S(1)} %slice.107), channel_id=1, source_target_pairs={{0,32},{32,64},{64,96},{96,0},{1,33},{33,65},{65,97},{97,1},{2,34}... | collective-permute-start | bytes 1032200 | tf_op jit(solution)/shard_map/ppermute | solution.py:28
  61.6 8.5 %collective-permute-start.8 = (bf16[336,512]{1,0:T(8,128)(2,1)S(1)}, bf16[336,512]{1,0:T(8,128)(2,1)S(1)}, u32[]{:S(2)}, u32[]{:S(2)}) collective-permute-start(bf16[336,512]{1,0:T(8,128)(2,1)S(1)} %slice.108), channel_id=1, source_target_pairs={{0,96},{32,0},{64,32},{96,64},{1,97},{33,1},{65,33},{97,65},{2,98}... | collective-permute-start | bytes 1032200 | tf_op jit(solution)/shard_map/ppermute | solution.py:28
  95.3 6.0 %copy-start.8 = (f32[128]{0:T(128)S(1)}, f32[128]{0:T(128)}, u32[]{:S(2)}) copy-start(f32[128]{0:T(128)} %param.15) | copy-start | bytes 1540
  96.6 21.1 %collective-permute-start.10 = (bf16[32,5376]{1,0:T(8,128)(2,1)}, bf16[32,5376]{1,0:T(8,128)(2,1)}, u32[]{:S(2)}, u32[]{:S(2)}) collective-permute-start(bf16[32,5376]{1,0:T(8,128)(2,1)} %param.16), channel_id=1, source_target_pairs={{0,16},{16,0},{1,17},{17,1},{2,18},{18,2},{3,19},{19,3},{4,20},{20... | collective-permute-start | bytes 1032200 | tf_op jit(solution)/shard_map/ppermute | solution.py:28
  98.6 14.9 %collective-permute-start.11 = (bf16[32,5376]{1,0:T(8,128)(2,1)}, bf16[32,5376]{1,0:T(8,128)(2,1)}, u32[]{:S(2)}, u32[]{:S(2)}) collective-permute-start(bf16[32,5376]{1,0:T(8,128)(2,1)} %param.16), channel_id=1, source_target_pairs={{0,96},{32,0},{64,32},{96,64},{1,97},{33,1},{65,33},{97,65},{2,98}... | collective-permute-start | bytes 1032200 | tf_op jit(solution)/shard_map/ppermute | solution.py:28
  101.3 11.2 %collective-permute-start.13 = (bf16[32,5376]{1,0:T(8,128)(2,1)}, bf16[32,5376]{1,0:T(8,128)(2,1)}, u32[]{:S(2)}, u32[]{:S(2)}) collective-permute-start(bf16[32,5376]{1,0:T(8,128)(2,1)} %param.16), channel_id=1, source_target_pairs={{0,32},{32,64},{64,96},{96,0},{1,33},{33,65},{65,97},{97,1},{2,34}... | collective-permute-start | bytes 1032200 | tf_op jit(solution)/shard_map/ppermute | solution.py:28
  101.4 9.1 %copy-start.9 = (f32[128]{0:T(128)S(1)}, f32[128]{0:T(128)}, u32[]{:S(2)}) copy-start(f32[128]{0:T(128)} %param.14) | copy-start | bytes 1540
  102.6 5.3 %copy-start.2 = (bf16[1,1024,64]{1,2,0:T(8,128)(2,1)}, bf16[1,1024,64]{1,2,0:T(8,128)(2,1)S(1)}, u32[]{:S(2)}) copy-start(bf16[1,1024,64]{1,2,0:T(8,128)(2,1)S(1)} %get-tuple-element.12) | copy-start | bytes 393220
  103.5 19.8 %collective-permute-start.9 = (bf16[2,1024,128]{1,2,0:T(8,128)(2,1)}, bf16[2,1024,128]{1,2,0:T(8,128)(2,1)}, u32[]{:S(2)}, u32[]{:S(2)}) collective-permute-start(bf16[2,1024,128]{1,2,0:T(8,128)(2,1)} %pad_maximum_fusion), channel_id=1, source_target_pairs={{0,16},{16,32},{32,48},{48,64},{64,80},{80,96},{96,112},{1,17},{17... | collective-permute-start | bytes 1572872 | tf_op jit(solution)/shard_map/ppermute | solution.py:22
  109.4 1.5 copy-start.1
  113.4 9.8 %collective-permute-start.14 = (bf16[16,5376]{1,0:T(8,128)(2,1)S(1)}, bf16[16,5376]{1,0:T(8,128)(2,1)S(1)}, u32[]{:S(2)}, u32[]{:S(2)}) collective-permute-start(bf16[16,5376]{1,0:T(8,128)(2,1)S(1)} %slice.122), channel_id=1, source_target_pairs={{0,32},{32,64},{64,96},{96,0},{1,33},{33,65},{65,97},{97,1},{2,34}... | collective-permute-start | bytes 516104 | tf_op jit(solution)/shard_map/ppermute | solution.py:28
  114.4 8.8 %collective-permute-start.15 = (bf16[16,5376]{1,0:T(8,128)(2,1)S(1)}, bf16[16,5376]{1,0:T(8,128)(2,1)S(1)}, u32[]{:S(2)}, u32[]{:S(2)}) collective-permute-start(bf16[16,5376]{1,0:T(8,128)(2,1)S(1)} %slice.123), channel_id=1, source_target_pairs={{0,96},{32,0},{64,32},{96,64},{1,97},{33,1},{65,33},{97,65},{2,98}... | collective-permute-start | bytes 516104 | tf_op jit(solution)/shard_map/ppermute | solution.py:28
  117.7 17.7 %collective-permute-start.12 = (bf16[32,5376]{1,0:T(8,128)(2,1)}, bf16[32,5376]{1,0:T(8,128)(2,1)S(1)}, u32[]{:S(2)}, u32[]{:S(2)}) collective-permute-start(bf16[32,5376]{1,0:T(8,128)(2,1)} %collective-permute-done.10), channel_id=1, source_target_pairs={{0,96},{32,0},{64,32},{96,64},{1,97},{33,1},{65,33},{97,65},{2,98}... | collective-permute-start | bytes 1032200 | tf_op jit(solution)/shard_map/ppermute | solution.py:28
  118.3 15.9 %collective-permute-start.16 = (bf16[32,5376]{1,0:T(8,128)(2,1)}, bf16[32,5376]{1,0:T(8,128)(2,1)S(1)}, u32[]{:S(2)}, u32[]{:S(2)}) collective-permute-start(bf16[32,5376]{1,0:T(8,128)(2,1)} %collective-permute-done.10), channel_id=1, source_target_pairs={{0,32},{32,64},{64,96},{96,0},{1,33},{33,65},{65,97},{97,1},{2,34}... | collective-permute-start | bytes 1032200 | tf_op jit(solution)/shard_map/ppermute | solution.py:28
  122.9 0.9 copy-start.3
  134.2 6.7 %collective-permute-start.17 = (bf16[16,5376]{1,0:T(8,128)(2,1)S(1)}, bf16[16,5376]{1,0:T(8,128)(2,1)S(1)}, u32[]{:S(2)}, u32[]{:S(2)}) collective-permute-start(bf16[16,5376]{1,0:T(8,128)(2,1)S(1)} %slice.124), channel_id=1, source_target_pairs={{0,32},{32,64},{64,96},{96,0},{1,33},{33,65},{65,97},{97,1},{2,34}... | collective-permute-start | bytes 516104 | tf_op jit(solution)/shard_map/ppermute | solution.py:28
  135.5 5.7 %collective-permute-start.18 = (bf16[16,5376]{1,0:T(8,128)(2,1)S(1)}, bf16[16,5376]{1,0:T(8,128)(2,1)S(1)}, u32[]{:S(2)}, u32[]{:S(2)}) collective-permute-start(bf16[16,5376]{1,0:T(8,128)(2,1)S(1)} %slice.125), channel_id=1, source_target_pairs={{0,96},{32,0},{64,32},{96,64},{1,97},{33,1},{65,33},{97,65},{2,98}... | collective-permute-start | bytes 516104 | tf_op jit(solution)/shard_map/ppermute | solution.py:28
  147.2 84.4 %copy-start = (bf16[64,5376]{1,0:T(8,128)(2,1)S(1)}, bf16[64,5376]{1,0:T(8,128)(2,1)}, u32[]{:S(2)}) copy-start(bf16[64,5376]{1,0:T(8,128)(2,1)} %param.9) | copy-start | bytes 2064388
  147.2 84.4 %copy-start.7 = (f32[5376]{0:T(1024)S(1)}, f32[5376]{0:T(1024)}, u32[]{:S(2)}) copy-start(f32[5376]{0:T(1024)} %param.17) | copy-start | bytes 64516
Sparse Core Ops, SparseCore 0:
  10.3 74.6 all-gather.1
  147.4 82.8 reduce-scatter.1

commit v10 on v8

--- a/solution.py
+++ b/solution.py
@@ -161,11 +161,24 @@
         outputs.append(mixed.astype(jnp.bfloat16).reshape(block_rows, local_heads * HEAD_SIZE))
     attended = jnp.concatenate(outputs, axis=0)
 
-    partial_value = jnp.dot(attended, out_weight, preferred_element_type=jnp.float32).astype(
-        jnp.bfloat16
-    )
+    core = lax.axis_index("core")
+    chips = lax.axis_size("hc")
+    rows = tok_count // (2 * chips)
+    blocks = attended.reshape(chips, 2, rows, attended.shape[-1])
+    by_core = [
+        jnp.dot(
+            blocks[:, c].reshape(chips * rows, attended.shape[-1]), out_weight,
+            preferred_element_type=jnp.float32,
+        ).astype(jnp.bfloat16)
+        for c in range(2)
+    ]
+    give = jnp.where(core == 0, by_core[1], by_core[0])
+    keep = jnp.where(core == 0, by_core[0], by_core[1])
+    pair_sum = (
+        keep.astype(jnp.float32) + rotated(give, "core", 1).astype(jnp.float32)
+    ).astype(jnp.bfloat16)
     summed = lax.psum_scatter(
-        partial_value, HEAD, scatter_dimension=0, tiled=True
+        pair_sum, "hc", scatter_dimension=0, tiled=True
     ).astype(jnp.float32)
     result = own_rows + root_mean_scale(summed, post_gain)
     return result.astype(jnp.bfloat16)

time: 241 us -> 257 us (1.066)
  other arithmetic: 19.8 us -> 30.2 us
  local copies, waits for them, and re-layouts: 24.7 us -> 31 us
  waiting for transfers between devices: 126 us -> 121 us
  matrix products: 22.8 us -> 26.1 us
    reduce_scatter x1, waiting for transfers between devices: 83 us -> 68.2 us  [body(): lax.psum_scatter(pair_sum, 'hc', scatter_dimension=0, tiled=True)]
    ppermute x18 -> x19, waiting for transfers between devices: 30.2 us -> 40.2 us  [rotated(): return lax.ppermute(shard, axis, pairs)]
    convert_element_type x0 -> x1, other arithmetic: none -> 8.56 us  [body(): pair_sum = (keep.astype(jnp.float32) + rotated(give, 'core', 1).astype(jn...]
    reshape x0 -> x2, local copies, waits for them, and re-layouts: none -> 3.66 us  [body(): mixed.astype(jnp.bfloat16).reshape(block_rows, local_heads * HEAD_SIZE)]
    ppermute x18 -> x19, starting transfers between devices: 29.3 us -> 28.6 us  [rotated(): return lax.ppermute(shard, axis, pairs)]
    dot_general x1 -> x2, matrix products: 5.86 us -> 5.76 us  [body(): jnp.dot(blocks[:, c].reshape(chips * rows, attended.shape[-1]), out_weigh...]
  transfers between devices with their start and end apart: 21 -> 22, of which waited for: 10 -> 9; matrix products, arithmetic and copies ran while one was open for 17% -> 20% of each run, Pallas kernels for 0% -> 0%
where the time goes in v10:
time: 257 us; the launch traced here: 255 us
  waiting for transfers between devices  121 us (47%)
  starting transfers between devices  33 us (13%)
  local copies, waits for them, and re-layouts  31 us (12%)
  other arithmetic  30.2 us (12%)
  matrix products  26.1 us (10%)
  between operations  14.1 us (5%)
    reduce_scatter x1, waiting for transfers between devices, body(): lax.psum_scatter(pair_sum, 'hc', scatter_dimension=0, tiled=True)  68.2 us
    ppermute x19, waiting for transfers between devices, rotated(): return lax.ppermute(shard, axis, pairs)  40.2 us
    ppermute x19, starting transfers between devices, rotated(): return lax.ppermute(shard, axis, pairs)  28.6 us
    dynamic_update_slice x20, local copies, waits for them, and re-layouts, placed(): lax.dynamic_update_index_in_dim(stacked, part, (me + i) % count, 0)  15 us
    all_gather x1, waiting for transfers between devices, body(): normed = lax.all_gather(own_normed, HEAD, axis=0, tiled=True)  12.6 us
    dot_general x1, matrix products, body(): projected = jnp.dot(normed, w_in, preferred_element_type=jnp.float32)  10.3 us
    convert_element_type x1, other arithmetic, body(): pair_sum = (keep.astype(jnp.float32) + rotated(give, 'core', 1).astype(jn...  8.56 us
    dot_general x2, matrix products, body(): jnp.einsum('jgqk,kjd->qjgd', probabilities, value_block, preferred_elemen...  6.45 us
  transfers between devices with their start and end apart: 22, of which 9 were waited for; matrix products, arithmetic and copies ran while one was open for 20% of the time, Pallas kernels for 0%

profile of v10, /device:TPU:0, one launch (start us, length us, event | category | flops | bytes accessed | tf_op | source)
XLA Modules:
  0.0 255.5 jit_solution(2485104329630952944)
XLA Ops:
  6.5 1.4 fusion.10
  8.0 2.2 fusion.12
  10.4 3.4 %collective-permute-start = (bf16[672,512]{1,0:T(8,128)(2,1)S(1)}, bf16[672,512]{1,0:T(8,128)(2,1)}, u32[]{:S(2)}, u32[]{:S(2)}) collective-permute-start(bf16[672,512]{1,0:T(8,128)(2,1)S(1)} %constant_dynamic-update-slice_fusion), channel_id=1, source_target_pairs={{0,16},{16,0},{1,17},{17,1},{2,18},{18,2},{3,19},{19,3},{4,20},{20... | collective-permute-start | bytes 2064392 | tf_op jit(solution)/shard_map/ppermute | solution.py:27
  13.8 2.8 %collective-permute-start.1 = (bf16[672,512]{1,0:T(8,128)(2,1)S(1)}, bf16[672,512]{1,0:T(8,128)(2,1)S(1)}, u32[]{:S(2)}, u32[]{:S(2)}) collective-permute-start(bf16[672,512]{1,0:T(8,128)(2,1)S(1)} %constant_dynamic-update-slice_fusion), channel_id=1, source_target_pairs={{0,96},{32,0},{64,32},{96,64},{1,97},{33,1},{65,33},{97,65},{2,98}... | collective-permute-start | bytes 2064392 | tf_op jit(solution)/shard_map/ppermute | solution.py:27
  16.8 1.9 and_and_fusion.1
  18.7 2.9 %multiply_cosine_fusion = (f32[1024,64]{1,0:T(8,128)S(1)}, f32[1024,64]{1,0:T(8,128)}) fusion(f32[64]{0:T(128)S(1)} %multiply_power_fusion, f32[1024]{0:T(1024)S(1)} %get-tuple-element.28), kind=kLoop, calls=%fused_computation.41 | loop fusion | flops 65536 | bytes 528640 | tf_op jit(solution)/shard_map/cos | solution.py:67
  21.6 1.1 and_and_fusion
  22.7 11.6 %collective-permute-done.3 = bf16[672,512]{1,0:T(8,128)(2,1)S(1)} collective-permute-done((bf16[672,512]{1,0:T(8,128)(2,1)S(1)}, bf16[672,512]{1,0:T(8,128)(2,1)S(1)}, u32[]{:S(2)}, u32[]{:S(2)}) %collective-permute-start.3) | collective-permute-done | bytes 688160 | tf_op jit(solution)/shard_map/ppermute | solution.py:27
  34.5 3.3 %collective-permute-start.5 = (bf16[336,512]{1,0:T(8,128)(2,1)S(1)}, bf16[336,512]{1,0:T(8,128)(2,1)S(1)}, u32[]{:S(2)}, u32[]{:S(2)}) collective-permute-start(bf16[336,512]{1,0:T(8,128)(2,1)S(1)} %slice.114), channel_id=1, source_target_pairs={{0,96},{32,0},{64,32},{96,64},{1,97},{33,1},{65,33},{97,65},{2,98}... | collective-permute-start | bytes 1032200 | tf_op jit(solution)/shard_map/ppermute | solution.py:27
  37.8 1.1 collective-permute-start.2
  38.9 0.9 collective-permute-start.6
  40.0 1.2 bitcast_dynamic-update-slice_fusion.4
  41.1 2.9 %broadcast_in_dim.112 = bf16[4,2,672,512]{3,2,1,0:T(8,128)(2,1)} broadcast(bf16[]{:T(256)} %constant.191.clone.1), dimensions={} | broadcast | bytes 5505026 | tf_op jit(solution)/shard_map/broadcast_in_dim | solution.py:31
  44.0 1.2 constant_dynamic-update-slice_fusion.10
  45.3 1.3 collective-permute-done.4
  46.7 12.1 %collective-permute-done.6 = bf16[672,512]{1,0:T(8,128)(2,1)S(1)} collective-permute-done((bf16[672,512]{1,0:T(8,128)(2,1)}, bf16[672,512]{1,0:T(8,128)(2,1)S(1)}, u32[]{:S(2)}, u32[]{:S(2)}) %collective-permute-start.6) | collective-permute-done | bytes 688160 | tf_op jit(solution)/shard_map/ppermute | solution.py:27
  59.0 3.3 %collective-permute-start.8 = (bf16[336,512]{1,0:T(8,128)(2,1)S(1)}, bf16[336,512]{1,0:T(8,128)(2,1)S(1)}, u32[]{:S(2)}, u32[]{:S(2)}) collective-permute-start(bf16[336,512]{1,0:T(8,128)(2,1)S(1)} %slice.116), channel_id=1, source_target_pairs={{0,96},{32,0},{64,32},{96,64},{1,97},{33,1},{65,33},{97,65},{2,98}... | collective-permute-start | bytes 1032200 | tf_op jit(solution)/shard_map/ppermute | solution.py:27
  62.4 1.2 constant_dynamic-update-slice_fusion.9
  63.6 4.2 %collective-permute-done.7 = bf16[336,512]{1,0:T(8,128)(2,1)S(1)} collective-permute-done((bf16[336,512]{1,0:T(8,128)(2,1)S(1)}, bf16[336,512]{1,0:T(8,128)(2,1)S(1)}, u32[]{:S(2)}, u32[]{:S(2)}) %collective-permute-start.7) | collective-permute-done | bytes 344096 | tf_op jit(solution)/shard_map/ppermute | solution.py:27
  67.9 1.2 constant_dynamic-update-slice_fusion.8
  69.1 1.2 constant_dynamic-update-slice_fusion.7
  70.2 12.6 %all-gather.2.cloned.1.call-done = bf16[1024,5376]{1,0:T(8,128)(2,1)} async-done(((bf16[64,5376]{1,0:T(8,128)(2,1)}), bf16[1024,5376]{1,0:T(8,128)(2,1)}) %all-gather.2.cloned.1.call-update) | async-done | bytes 11010064 | tf_op jit(solution)/shard_map/all_gather | solution.py:97
  82.8 10.3 %fusion.45 = f32[1024,512]{0,1:T(8,128)S(1)} fusion(bf16[1024,5376]{1,0:T(8,128)(2,1)} %all-gather.2.cloned.1.call-done, bf16[5376,512]{1,0:T(8,128)(2,1)} %bitcast.8), kind=kOutput, calls=%fused_computation.116 | convolution fusion | flops 5637144576 | bytes 18612224 | tf_op jit(solution)/shard_map/dot_general | solution.py:101
  93.5 1.9 collective-permute-start.10
  95.4 2.8 %collective-permute-start.11 = (bf16[32,5376]{1,0:T(8,128)(2,1)}, bf16[32,5376]{1,0:T(8,128)(2,1)}, u32[]{:S(2)}, u32[]{:S(2)}) collective-permute-start(bf16[32,5376]{1,0:T(8,128)(2,1)} %param.16), channel_id=1, source_target_pairs={{0,96},{32,0},{64,32},{96,64},{1,97},{33,1},{65,33},{97,65},{2,98}... | collective-permute-start | bytes 1032200 | tf_op jit(solution)/shard_map/ppermute | solution.py:27
  98.3 1.2 fusion.39
  99.5 0.9 pad_maximum_fusion
  100.3 4.4 %collective-permute-start.9 = (bf16[2,1024,128]{1,2,0:T(8,128)(2,1)}, bf16[2,1024,128]{1,2,0:T(8,128)(2,1)}, u32[]{:S(2)}, u32[]{:S(2)}) collective-permute-start(bf16[2,1024,128]{1,2,0:T(8,128)(2,1)} %pad_maximum_fusion), channel_id=1, source_target_pairs={{0,16},{16,32},{32,48},{48,64},{64,80},{80,96},{96,112},{1,17},{17... | collective-permute-start | bytes 1572872 | tf_op jit(solution)/shard_map/ppermute | solution.py:21
  105.2 1.1 bitcast_dynamic-update-slice_fusion.11
  106.6 0.5 multiply_subtract_fusion
  107.5 1.8 collective-permute-done.13
  109.3 0.9 slice.131
  110.3 0.9 slice.132
  111.3 3.3 %collective-permute-start.15 = (bf16[16,5376]{1,0:T(8,128)(2,1)S(1)}, bf16[16,5376]{1,0:T(8,128)(2,1)S(1)}, u32[]{:S(2)}, u32[]{:S(2)}) collective-permute-start(bf16[16,5376]{1,0:T(8,128)(2,1)S(1)} %slice.132), channel_id=1, source_target_pairs={{0,96},{32,0},{64,32},{96,64},{1,97},{33,1},{65,33},{97,65},{2,98}... | collective-permute-start | bytes 516104 | tf_op jit(solution)/shard_map/ppermute | solution.py:27
  114.6 1.9 collective-permute-start.16
  116.6 1.0 bitcast_dynamic-update-slice_fusion.10
  117.7 1.0 bitcast_dynamic-update-slice_fusion.9
  118.7 1.0 broadcast_in_dim.126.clone.3
  119.8 1.7 bitcast_dynamic-update-slice_fusion.7
  121.9 0.8 copy-done.5
  122.7 1.1 maximum_maximum_fusion
  123.9 1.3 fusion
  125.2 1.2 fusion.2
  126.4 2.7 %fusion.14 = bf16[128,2,512]{2,0,1:T(8,128)(2,1)} fusion(f32[2,512]{1,0:T(2,128)S(1)} %fusion.2, f32[2,512]{1,0:T(2,128)S(1)} %get-tuple-element.23, f32[1536,512,2]{1,0,2:T(8,128)S(1)} %get-tuple-element.24, pred[512,1536]{0,1:T(8,128)(4,1)S(1)} %copy-done.1, bf16[2,2048,128]{1,2,0:T(8,128)(2,1)S(1)} %maximum_maximum_fusion), kind=kOutput, calls=%fused_computation.31 | convolution fusion | flops 409075712 | bytes 7741440 | tf_op jit(solution)/shard_map/jgqk,kjd->qjgd/dot_general | solution.py:158
  129.1 1.8 copy.20
  130.9 2.3 fusion.1
  133.2 1.3 fusion.3
  134.6 3.8 %fusion.17 = bf16[128,2,512]{2,0,1:T(8,128)(2,1)} fusion(f32[2,512]{1,0:T(2,128)S(1)} %fusion.3, f32[2,512]{1,0:T(2,128)S(1)} %get-tuple-element.21, f32[1536,512,2]{1,0,2:T(8,128)S(1)} %get-tuple-element.22, pred[512,1536]{0,1:T(8,128)(4,1)S(1)} %and_and_fusion, bf16[2,2048,128]{1,2,0:T(8,128)(2,1)} %copy-done.4), kind=kOutput, calls=%fused_computation.32 | convolution fusion | flops 409075712 | bytes 7741440 | tf_op jit(solution)/shard_map/jgqk,kjd->qjgd/dot_general | solution.py:158
  138.3 1.9 copy.21
  140.2 1.1 pad_maximum_fusion.1
  141.4 0.9 slice.133
  142.4 0.9 slice.134
  143.3 3.5 %collective-permute-start.18 = (bf16[16,5376]{1,0:T(8,128)(2,1)S(1)}, bf16[16,5376]{1,0:T(8,128)(2,1)S(1)}, u32[]{:S(2)}, u32[]{:S(2)}) collective-permute-start(bf16[16,5376]{1,0:T(8,128)(2,1)S(1)} %slice.134), channel_id=1, source_target_pairs={{0,96},{32,0},{64,32},{96,64},{1,97},{33,1},{65,33},{97,65},{2,98}... | collective-permute-start | bytes 516104 | tf_op jit(solution)/shard_map/ppermute | solution.py:27
  146.9 1.0 bitcast_dynamic-update-slice_fusion.8
  147.9 1.7 bitcast_dynamic-update-slice_fusion.6
  149.9 1.2 constant_dynamic-update-slice_fusion.3
  151.0 1.6 convolution_convert_fusion.1
  152.7 4.2 %broadcast_select_fusion = (bf16[512,5376]{1,0:T(8,128)(2,1)S(1)}, bf16[512,5376]{1,0:T(8,128)(2,1)}) fusion(bf16[512,5376]{1,0:T(8,128)(2,1)S(1)} %convolution_convert_fusion.1, pred[]{:T(512)S(6)} %eq.29, bf16[512,256]{1,0:T(8,128)(2,1)S(1)} %bitcast.141, bf16[256,5376]{1,0:T(8,128)(2,1)S(1)} %bitcast.138), kind=kOutput, calls=%fused_computation.11 | convolution fusion | flops 1414791168 | bytes 19529728 | tf_op jit(solution)/shard_map/dot_general | solution.py:169
  156.8 9.0 %collective-permute-done.19 = bf16[512,5376]{1,0:T(8,128)(2,1)S(1)} collective-permute-done((bf16[512,5376]{1,0:T(8,128)(2,1)S(1)}, bf16[512,5376]{1,0:T(8,128)(2,1)S(1)}, u32[]{:S(2)}, u32[]{:S(2)}) %collective-permute-start.19) | collective-permute-done | bytes 5505056 | tf_op jit(solution)/shard_map/ppermute | solution.py:27
  165.9 2.4 copy-done.3
  168.2 8.6 %add_convert_fusion = bf16[512,5376]{1,0:T(8,128)(2,1)} fusion(bf16[512,5376]{1,0:T(8,128)(2,1)} %copy-done.3, bf16[512,5376]{1,0:T(8,128)(2,1)} %copy-done, bf16[512,5376]{1,0:T(8,128)(2,1)} %get-tuple-element.26, pred[]{:T(512)S(6)} %eq.29), kind=kLoop, calls=%fused_computation | loop fusion | flops 13762560 | bytes 22020096 | tf_op jit(solution)/shard_map/convert_element_type | solution.py:179
  176.8 68.2 %reduce-scatter.2.cloned.1.call-done = bf16[64,5376]{1,0:T(8,128)(2,1)} async-done(((bf16[512,5376]{1,0:T(8,128)(2,1)}), bf16[64,5376]{1,0:T(8,128)(2,1)}) %reduce-scatter.2.cloned.1.call-update) | async-done | bytes 688144 | tf_op jit(solution)/shard_map/reduce_scatter | solution.py:180
  245.0 1.3 fusion.8
  246.4 2.3 fusion.13
  (116 shorter events, 3.8 us)
Async XLA Ops:
  6.5 3.7 %copy-start.17 = (bf16[672,256]{1,0:T(8,128)(2,1)S(1)}, bf16[672,256]{1,0:T(8,128)(2,1)}, u32[]{:S(2)}) copy-start(bf16[672,256]{1,0:T(8,128)(2,1)} %param.11) | copy-start | bytes 1032196
  6.5 3.7 %copy-start.18 = (bf16[672,128]{1,0:T(8,128)(2,1)S(1)}, bf16[672,128]{1,0:T(8,128)(2,1)}, u32[]{:S(2)}) copy-start(bf16[672,128]{1,0:T(8,128)(2,1)} %param.12) | copy-start | bytes 516100
  6.5 3.8 %copy-start.19 = (bf16[672,128]{1,0:T(8,128)(2,1)S(1)}, bf16[672,128]{1,0:T(8,128)(2,1)}, u32[]{:S(2)}) copy-start(bf16[672,128]{1,0:T(8,128)(2,1)} %param.13) | copy-start | bytes 516100
  6.5 76.3 %all-gather.2.cloned.1.call-start = ((), (), s32[]{:S(2)}) async-start(), calls=%async_computation.1 | async-start | bytes 11698176 | tf_op jit(solution)/shard_map/all_gather | solution.py:97
  10.2 234.8 %reduce-scatter.2.cloned.1.call-start = ((), (), s32[]{:S(2)}) async-start(), calls=%async_computation.2 | async-start | bytes 6193152 | tf_op jit(solution)/shard_map/reduce_scatter | solution.py:180
  10.4 27.4 %collective-permute-start = (bf16[672,512]{1,0:T(8,128)(2,1)S(1)}, bf16[672,512]{1,0:T(8,128)(2,1)}, u32[]{:S(2)}, u32[]{:S(2)}) collective-permute-start(bf16[672,512]{1,0:T(8,128)(2,1)S(1)} %constant_dynamic-update-slice_fusion), channel_id=1, source_target_pairs={{0,16},{16,0},{1,17},{17,1},{2,18},{18,2},{3,19},{19,3},{4,20},{20... | collective-permute-start | bytes 2064392 | tf_op jit(solution)/shard_map/ppermute | solution.py:27
  13.8 20.7 %collective-permute-start.1 = (bf16[672,512]{1,0:T(8,128)(2,1)S(1)}, bf16[672,512]{1,0:T(8,128)(2,1)S(1)}, u32[]{:S(2)}, u32[]{:S(2)}) collective-permute-start(bf16[672,512]{1,0:T(8,128)(2,1)S(1)} %constant_dynamic-update-slice_fusion), channel_id=1, source_target_pairs={{0,96},{32,0},{64,32},{96,64},{1,97},{33,1},{65,33},{97,65},{2,98}... | collective-permute-start | bytes 2064392 | tf_op jit(solution)/shard_map/ppermute | solution.py:27
  16.5 17.8 %collective-permute-start.3 = (bf16[672,512]{1,0:T(8,128)(2,1)S(1)}, bf16[672,512]{1,0:T(8,128)(2,1)S(1)}, u32[]{:S(2)}, u32[]{:S(2)}) collective-permute-start(bf16[672,512]{1,0:T(8,128)(2,1)S(1)} %constant_dynamic-update-slice_fusion), channel_id=1, source_target_pairs={{0,32},{32,64},{64,96},{96,0},{1,33},{33,65},{65,97},{97,1},{2,34}... | collective-permute-start | bytes 2064392 | tf_op jit(solution)/shard_map/ppermute | solution.py:27
  34.4 12.2 %collective-permute-start.4 = (bf16[336,512]{1,0:T(8,128)(2,1)S(1)}, bf16[336,512]{1,0:T(8,128)(2,1)S(1)}, u32[]{:S(2)}, u32[]{:S(2)}) collective-permute-start(bf16[336,512]{1,0:T(8,128)(2,1)S(1)} %slice.113), channel_id=1, source_target_pairs={{0,32},{32,64},{64,96},{96,0},{1,33},{33,65},{65,97},{97,1},{2,34}... | collective-permute-start | bytes 1032200 | tf_op jit(solution)/shard_map/ppermute | solution.py:27
  34.5 12.1 %collective-permute-start.5 = (bf16[336,512]{1,0:T(8,128)(2,1)S(1)}, bf16[336,512]{1,0:T(8,128)(2,1)S(1)}, u32[]{:S(2)}, u32[]{:S(2)}) collective-permute-start(bf16[336,512]{1,0:T(8,128)(2,1)S(1)} %slice.114), channel_id=1, source_target_pairs={{0,96},{32,0},{64,32},{96,64},{1,97},{33,1},{65,33},{97,65},{2,98}... | collective-permute-start | bytes 1032200 | tf_op jit(solution)/shard_map/ppermute | solution.py:27
  37.8 21.2 %collective-permute-start.2 = (bf16[672,512]{1,0:T(8,128)(2,1)}, bf16[672,512]{1,0:T(8,128)(2,1)S(1)}, u32[]{:S(2)}, u32[]{:S(2)}) collective-permute-start(bf16[672,512]{1,0:T(8,128)(2,1)} %collective-permute-done), channel_id=1, source_target_pairs={{0,96},{32,0},{64,32},{96,64},{1,97},{33,1},{65,33},{97,65},{2,98}... | collective-permute-start | bytes 2064392 | tf_op jit(solution)/shard_map/ppermute | solution.py:27
  38.9 20.0 %collective-permute-start.6 = (bf16[672,512]{1,0:T(8,128)(2,1)}, bf16[672,512]{1,0:T(8,128)(2,1)S(1)}, u32[]{:S(2)}, u32[]{:S(2)}) collective-permute-start(bf16[672,512]{1,0:T(8,128)(2,1)} %collective-permute-done), channel_id=1, source_target_pairs={{0,32},{32,64},{64,96},{96,0},{1,33},{33,65},{65,97},{97,1},{2,34}... | collective-permute-start | bytes 2064392 | tf_op jit(solution)/shard_map/ppermute | solution.py:27
  58.9 8.9 %collective-permute-start.7 = (bf16[336,512]{1,0:T(8,128)(2,1)S(1)}, bf16[336,512]{1,0:T(8,128)(2,1)S(1)}, u32[]{:S(2)}, u32[]{:S(2)}) collective-permute-start(bf16[336,512]{1,0:T(8,128)(2,1)S(1)} %slice.115), channel_id=1, source_target_pairs={{0,32},{32,64},{64,96},{96,0},{1,33},{33,65},{65,97},{97,1},{2,34}... | collective-permute-start | bytes 1032200 | tf_op jit(solution)/shard_map/ppermute | solution.py:27
  59.0 8.8 %collective-permute-start.8 = (bf16[336,512]{1,0:T(8,128)(2,1)S(1)}, bf16[336,512]{1,0:T(8,128)(2,1)S(1)}, u32[]{:S(2)}, u32[]{:S(2)}) collective-permute-start(bf16[336,512]{1,0:T(8,128)(2,1)S(1)} %slice.116), channel_id=1, source_target_pairs={{0,96},{32,0},{64,32},{96,64},{1,97},{33,1},{65,33},{97,65},{2,98}... | collective-permute-start | bytes 1032200 | tf_op jit(solution)/shard_map/ppermute | solution.py:27
  93.2 5.0 %copy-start.21 = (f32[128]{0:T(128)S(1)}, f32[128]{0:T(128)}, u32[]{:S(2)}) copy-start(f32[128]{0:T(128)} %param.15) | copy-start | bytes 1540
  93.3 7.1 %copy-start.9 = (bf16[1,1024,128]{1,2,0:T(8,128)(2,1)}, bf16[1,1024,128]{1,2,0:T(8,128)(2,1)S(1)}, u32[]{:S(2)}) copy-start(bf16[1,1024,128]{1,2,0:T(8,128)(2,1)S(1)} %fusion.35) | copy-start | bytes 786436
  93.5 21.1 %collective-permute-start.10 = (bf16[32,5376]{1,0:T(8,128)(2,1)}, bf16[32,5376]{1,0:T(8,128)(2,1)}, u32[]{:S(2)}, u32[]{:S(2)}) collective-permute-start(bf16[32,5376]{1,0:T(8,128)(2,1)} %param.16), channel_id=1, source_target_pairs={{0,16},{16,0},{1,17},{17,1},{2,18},{18,2},{3,19},{19,3},{4,20},{20... | collective-permute-start | bytes 1032200 | tf_op jit(solution)/shard_map/ppermute | solution.py:27
  95.4 14.9 %collective-permute-start.11 = (bf16[32,5376]{1,0:T(8,128)(2,1)}, bf16[32,5376]{1,0:T(8,128)(2,1)}, u32[]{:S(2)}, u32[]{:S(2)}) collective-permute-start(bf16[32,5376]{1,0:T(8,128)(2,1)} %param.16), channel_id=1, source_target_pairs={{0,96},{32,0},{64,32},{96,64},{1,97},{33,1},{65,33},{97,65},{2,98}... | collective-permute-start | bytes 1032200 | tf_op jit(solution)/shard_map/ppermute | solution.py:27
  98.1 11.2 %collective-permute-start.13 = (bf16[32,5376]{1,0:T(8,128)(2,1)}, bf16[32,5376]{1,0:T(8,128)(2,1)}, u32[]{:S(2)}, u32[]{:S(2)}) collective-permute-start(bf16[32,5376]{1,0:T(8,128)(2,1)} %param.16), channel_id=1, source_target_pairs={{0,32},{32,64},{64,96},{96,0},{1,33},{33,65},{65,97},{97,1},{2,34}... | collective-permute-start | bytes 1032200 | tf_op jit(solution)/shard_map/ppermute | solution.py:27
  98.3 8.0 %copy-start.22 = (f32[128]{0:T(128)S(1)}, f32[128]{0:T(128)}, u32[]{:S(2)}) copy-start(f32[128]{0:T(128)} %param.14) | copy-start | bytes 1540
  99.4 5.3 %copy-start.13 = (bf16[1,1024,64]{1,2,0:T(8,128)(2,1)}, bf16[1,1024,64]{1,2,0:T(8,128)(2,1)S(1)}, u32[]{:S(2)}) copy-start(bf16[1,1024,64]{1,2,0:T(8,128)(2,1)S(1)} %get-tuple-element.11) | copy-start | bytes 393220
  99.4 5.3 %copy-start.15 = (bf16[1,1024,64]{1,2,0:T(8,128)(2,1)}, bf16[1,1024,64]{1,2,0:T(8,128)(2,1)S(1)}, u32[]{:S(2)}) copy-start(bf16[1,1024,64]{1,2,0:T(8,128)(2,1)S(1)} %get-tuple-element.12) | copy-start | bytes 393220
  100.3 22.4 %collective-permute-start.9 = (bf16[2,1024,128]{1,2,0:T(8,128)(2,1)}, bf16[2,1024,128]{1,2,0:T(8,128)(2,1)}, u32[]{:S(2)}, u32[]{:S(2)}) collective-permute-start(bf16[2,1024,128]{1,2,0:T(8,128)(2,1)} %pad_maximum_fusion), channel_id=1, source_target_pairs={{0,16},{16,32},{32,48},{48,64},{64,80},{80,96},{96,112},{1,17},{17... | collective-permute-start | bytes 1572872 | tf_op jit(solution)/shard_map/ppermute | solution.py:21
  105.1 1.5 copy-start.12
  107.4 16.4 %copy-start.11 = (bf16[1024,2,128]{2,0,1:T(8,128)(2,1)}, bf16[1024,2,128]{2,0,1:T(8,128)(2,1)S(1)}, u32[]{:S(2)}) copy-start(bf16[1024,2,128]{2,0,1:T(8,128)(2,1)S(1)} %fusion.20) | copy-start | bytes 1572868
  110.2 11.5 %collective-permute-start.14 = (bf16[16,5376]{1,0:T(8,128)(2,1)S(1)}, bf16[16,5376]{1,0:T(8,128)(2,1)S(1)}, u32[]{:S(2)}, u32[]{:S(2)}) collective-permute-start(bf16[16,5376]{1,0:T(8,128)(2,1)S(1)} %slice.131), channel_id=1, source_target_pairs={{0,32},{32,64},{64,96},{96,0},{1,33},{33,65},{65,97},{97,1},{2,34}... | collective-permute-start | bytes 516104 | tf_op jit(solution)/shard_map/ppermute | solution.py:27
  111.3 10.5 %collective-permute-start.15 = (bf16[16,5376]{1,0:T(8,128)(2,1)S(1)}, bf16[16,5376]{1,0:T(8,128)(2,1)S(1)}, u32[]{:S(2)}, u32[]{:S(2)}) collective-permute-start(bf16[16,5376]{1,0:T(8,128)(2,1)S(1)} %slice.132), channel_id=1, source_target_pairs={{0,96},{32,0},{64,32},{96,64},{1,97},{33,1},{65,33},{97,65},{2,98}... | collective-permute-start | bytes 516104 | tf_op jit(solution)/shard_map/ppermute | solution.py:27
  114.5 27.8 %collective-permute-start.12 = (bf16[32,5376]{1,0:T(8,128)(2,1)}, bf16[32,5376]{1,0:T(8,128)(2,1)}, u32[]{:S(2)}, u32[]{:S(2)}) collective-permute-start(bf16[32,5376]{1,0:T(8,128)(2,1)} %collective-permute-done.10), channel_id=1, source_target_pairs={{0,96},{32,0},{64,32},{96,64},{1,97},{33,1},{65,33},{97,65},{2,98}... | collective-permute-start | bytes 1032200 | tf_op jit(solution)/shard_map/ppermute | solution.py:27
  114.6 26.7 %collective-permute-start.16 = (bf16[32,5376]{1,0:T(8,128)(2,1)}, bf16[32,5376]{1,0:T(8,128)(2,1)}, u32[]{:S(2)}, u32[]{:S(2)}) collective-permute-start(bf16[32,5376]{1,0:T(8,128)(2,1)} %collective-permute-done.10), channel_id=1, source_target_pairs={{0,32},{32,64},{64,96},{96,0},{1,33},{33,65},{65,97},{97,1},{2,34}... | collective-permute-start | bytes 1032200 | tf_op jit(solution)/shard_map/ppermute | solution.py:27
  118.7 1.1 copy-start.7
  121.5 1.2 copy-start.10
  121.5 1.2 copy-start.14
  121.5 1.2 copy-start.16
  121.7 2.2 copy-start.1
  121.9 0.9 copy-start.5
  123.9 2.5 copy-start.4
  138.3 8.6 %copy-start.8 = (bf16[1,2,32,5376]{3,2,1,0:T(8,128)(2,1)S(1)}, bf16[1,2,32,5376]{3,2,1,0:T(8,128)(2,1)}, u32[]{:S(2)}) copy-start(bf16[1,2,32,5376]{3,2,1,0:T(8,128)(2,1)} %copy-done.7) | copy-start | bytes 2064388
  140.2 9.6 %copy-start.6 = (bf16[1,2,32,5376]{3,2,1,0:T(8,128)(2,1)S(1)}, bf16[1,2,32,5376]{3,2,1,0:T(8,128)(2,1)}, u32[]{:S(2)}) copy-start(bf16[1,2,32,5376]{3,2,1,0:T(8,128)(2,1)} %copy-done.5) | copy-start | bytes 2064388
  142.3 7.4 %collective-permute-start.17 = (bf16[16,5376]{1,0:T(8,128)(2,1)S(1)}, bf16[16,5376]{1,0:T(8,128)(2,1)S(1)}, u32[]{:S(2)}, u32[]{:S(2)}) collective-permute-start(bf16[16,5376]{1,0:T(8,128)(2,1)S(1)} %slice.133), channel_id=1, source_target_pairs={{0,32},{32,64},{64,96},{96,0},{1,33},{33,65},{65,97},{97,1},{2,34}... | collective-permute-start | bytes 516104 | tf_op jit(solution)/shard_map/ppermute | solution.py:27
  143.3 6.5 %collective-permute-start.18 = (bf16[16,5376]{1,0:T(8,128)(2,1)S(1)}, bf16[16,5376]{1,0:T(8,128)(2,1)S(1)}, u32[]{:S(2)}, u32[]{:S(2)}) collective-permute-start(bf16[16,5376]{1,0:T(8,128)(2,1)S(1)} %slice.134), channel_id=1, source_target_pairs={{0,96},{32,0},{64,32},{96,64},{1,97},{33,1},{65,33},{97,65},{2,98}... | collective-permute-start | bytes 516104 | tf_op jit(solution)/shard_map/ppermute | solution.py:27
  152.6 4.2 %copy-start = (bf16[512,5376]{1,0:T(8,128)(2,1)}, bf16[512,5376]{1,0:T(8,128)(2,1)S(1)}, u32[]{:S(2)}) copy-start(bf16[512,5376]{1,0:T(8,128)(2,1)S(1)} %convolution_convert_fusion.1) | copy-start | bytes 16515076
  156.8 9.0 %collective-permute-start.19 = (bf16[512,5376]{1,0:T(8,128)(2,1)S(1)}, bf16[512,5376]{1,0:T(8,128)(2,1)S(1)}, u32[]{:S(2)}, u32[]{:S(2)}) collective-permute-start(bf16[512,5376]{1,0:T(8,128)(2,1)S(1)} %get-tuple-element.25), channel_id=1, source_target_pairs={{0,1},{1,0},{2,3},{3,2},{4,5},{5,4},{6,7},{7,6},{8,9},{9,8},{10,11... | collective-permute-start | bytes 16515080 | tf_op jit(solution)/shard_map/ppermute | solution.py:27
  165.9 2.4 copy-start.3
  176.8 69.5 %copy-start.2 = (bf16[64,5376]{1,0:T(8,128)(2,1)S(1)}, bf16[64,5376]{1,0:T(8,128)(2,1)}, u32[]{:S(2)}) copy-start(bf16[64,5376]{1,0:T(8,128)(2,1)} %param.9) | copy-start | bytes 2064388
  176.8 69.6 %copy-start.20 = (f32[5376]{0:T(1024)S(1)}, f32[5376]{0:T(1024)}, u32[]{:S(2)}) copy-start(f32[5376]{0:T(1024)} %param.17) | copy-start | bytes 64516
Sparse Core Ops, SparseCore 0:
  10.3 72.4 all-gather.1
  176.9 67.9 reduce-scatter.1

commit v11 on v8

--- a/solution.py
+++ b/solution.py
@@ -51,6 +51,14 @@
     partner = ring_over_cx(rotated(piece, "cy", 1))
     pairs = [placed([a, b], cy, 2) for a, b in zip(own, partner)]
     ring = placed(pairs, cx, 4)
+    return ring.reshape((8 * piece.shape[0],) + piece.shape[1:])
+
+
+def gathered_pair_first(piece):
+    cy = lax.axis_index("cy")
+    cx = lax.axis_index("cx")
+    pair = placed([piece, rotated(piece, "cy", 1)], cy, 2)
+    ring = placed(ring_over_cx(pair), cx, 4)
     return ring.reshape((8 * piece.shape[0],) + piece.shape[1:])
 
 
@@ -96,7 +104,7 @@
     own_normed = root_mean_scale(own_rows, pre_gain).astype(jnp.bfloat16)
     normed = lax.all_gather(own_normed, HEAD, axis=0, tiled=True)
     normed, w_output = lax.optimization_barrier((normed, w_output))
-    out_weight = gathered_over_ctx(w_output)
+    out_weight = gathered_pair_first(w_output)
     tok_count = normed.shape[0]
     projected = jnp.dot(normed, w_in, preferred_element_type=jnp.float32)
     query_raw = projected[:, :q_cols]

time: 241 us -> 254 us (1.054)
  waiting for transfers between devices: 126 us -> 146 us
  local copies, waits for them, and re-layouts: 24.7 us -> 19.1 us
    ppermute x18 -> x14, waiting for transfers between devices: 30.2 us -> 52.9 us  [rotated(): return lax.ppermute(shard, axis, pairs)]
    dynamic_update_slice x20 -> x15, local copies, waits for them, and re-layouts: 12.8 us -> 9.65 us  [placed(): lax.dynamic_update_index_in_dim(stacked, part, (me + i) % count, 0)]
    ppermute x18 -> x14, starting transfers between devices: 29.3 us -> 27 us  [rotated(): return lax.ppermute(shard, axis, pairs)]
  transfers between devices with their start and end apart: 21 -> 17, of which waited for: 10 -> 10; matrix products, arithmetic and copies ran while one was open for 17% -> 14% of each run, Pallas kernels for 0% -> 0%
where the time goes in v11:
time: 254 us; the launch traced here: 253 us
  waiting for transfers between devices  146 us (57%)
  starting transfers between devices  31.6 us (12%)
  matrix products  22.8 us (9%)
  other arithmetic  19.8 us (8%)
  local copies, waits for them, and re-layouts  19.1 us (8%)
  between operations  13.9 us (5%)
    reduce_scatter x1, waiting for transfers between devices, body(): lax.psum_scatter(partial_value, HEAD, scatter_dimension=0, tiled=True)  80.7 us
    ppermute x14, waiting for transfers between devices, rotated(): return lax.ppermute(shard, axis, pairs)  52.9 us
    ppermute x14, starting transfers between devices, rotated(): return lax.ppermute(shard, axis, pairs)  27 us
    all_gather x1, waiting for transfers between devices, body(): normed = lax.all_gather(own_normed, HEAD, axis=0, tiled=True)  12.5 us
    dot_general x1, matrix products, body(): projected = jnp.dot(normed, w_in, preferred_element_type=jnp.float32)  10.3 us
    dynamic_update_slice x15, local copies, waits for them, and re-layouts, placed(): lax.dynamic_update_index_in_dim(stacked, part, (me + i) % count, 0)  9.65 us
    dot_general x1, matrix products, body(): jnp.dot(attended, out_weight, preferred_element_type=jnp.float32)  5.89 us
  transfers between devices with their start and end apart: 17, of which 10 were waited for; matrix products, arithmetic and copies ran while one was open for 14% of the time, Pallas kernels for 0%

profile of v11, /device:TPU:0, one launch (start us, length us, event | category | flops | bytes accessed | tf_op | source)
XLA Modules:
  0.0 253.2 jit_solution(428646395345652590)
XLA Ops:
  6.5 1.4 fusion.10
  8.0 2.2 fusion.12
  10.2 0.8 constant_dynamic-update-slice_fusion.2
  11.0 0.7 constant_dynamic-update-slice_fusion.1
  11.7 0.7 constant_dynamic-update-slice_fusion
  12.4 3.3 %collective-permute-start = (bf16[672,512]{1,0:T(8,128)(2,1)}, bf16[672,512]{1,0:T(8,128)(2,1)}, u32[]{:S(2)}, u32[]{:S(2)}) collective-permute-start(bf16[672,512]{1,0:T(8,128)(2,1)} %constant_dynamic-update-slice_fusion), channel_id=1, source_target_pairs={{0,16},{16,0},{1,17},{17,1},{2,18},{18,2},{3,19},{19,3},{4,20},{20... | collective-permute-start | bytes 2064392 | tf_op jit(solution)/shard_map/ppermute | solution.py:27
  15.8 2.8 %collective-permute-start.1 = (bf16[672,512]{1,0:T(8,128)(2,1)}, bf16[672,512]{1,0:T(8,128)(2,1)}, u32[]{:S(2)}, u32[]{:S(2)}) collective-permute-start(bf16[672,512]{1,0:T(8,128)(2,1)} %constant_dynamic-update-slice_fusion), channel_id=1, source_target_pairs={{0,96},{32,0},{64,32},{96,64},{1,97},{33,1},{65,33},{97,65},{2,98}... | collective-permute-start | bytes 2064392 | tf_op jit(solution)/shard_map/ppermute | solution.py:27
  18.6 0.1 broadcast_in_dim.104.clone
  18.7 1.2 bitcast_dynamic-update-slice_fusion.8
  19.8 1.1 and_and_fusion.1
  21.0 3.0 %multiply_cosine_fusion = (f32[1024,64]{1,0:T(8,128)S(1)}, f32[1024,64]{1,0:T(8,128)}) fusion(f32[64]{0:T(128)S(1)} %multiply_power_fusion, f32[1024]{0:T(1024)S(1)} %get-tuple-element.24), kind=kLoop, calls=%fused_computation.38 | loop fusion | flops 65536 | bytes 528640 | tf_op jit(solution)/shard_map/cos | solution.py:75
  23.9 1.1 and_and_fusion
  25.1 11.5 %collective-permute-done.3 = bf16[672,512]{1,0:T(8,128)(2,1)S(1)} collective-permute-done((bf16[672,512]{1,0:T(8,128)(2,1)}, bf16[672,512]{1,0:T(8,128)(2,1)S(1)}, u32[]{:S(2)}, u32[]{:S(2)}) %collective-permute-start.3) | collective-permute-done | bytes 688160 | tf_op jit(solution)/shard_map/ppermute | solution.py:27
  36.6 0.1 collective-permute-start.4
  36.7 1.0 slice.98
  37.7 3.3 %collective-permute-start.5 = (bf16[336,512]{1,0:T(8,128)(2,1)S(1)}, bf16[336,512]{1,0:T(8,128)(2,1)S(1)}, u32[]{:S(2)}, u32[]{:S(2)}) collective-permute-start(bf16[336,512]{1,0:T(8,128)(2,1)S(1)} %slice.98), channel_id=1, source_target_pairs={{0,96},{32,0},{64,32},{96,64},{1,97},{33,1},{65,33},{97,65},{2,98}... | collective-permute-start | bytes 1032200 | tf_op jit(solution)/shard_map/ppermute | solution.py:27
  41.0 2.5 collective-permute-start.2
  43.4 0.1 broadcast_in_dim.104.clone.1
  43.5 1.2 bitcast_dynamic-update-slice_fusion.6
  44.7 1.2 bitcast_dynamic-update-slice_fusion.7
  45.8 2.8 %broadcast_in_dim.103 = bf16[4,2,672,512]{3,2,1,0:T(8,128)(2,1)} broadcast(bf16[]{:T(256)} %constant.154.clone.1), dimensions={} | broadcast | bytes 5505026 | tf_op jit(solution)/shard_map/broadcast_in_dim | solution.py:31
  48.7 1.2 constant_dynamic-update-slice_fusion.6
  49.9 0.1 broadcast_in_dim.104.clone.3
  50.0 0.1 broadcast_in_dim.104.clone.2
  50.2 10.9 %collective-permute-done.6 = bf16[672,512]{1,0:T(8,128)(2,1)S(1)} collective-permute-done((bf16[672,512]{1,0:T(8,128)(2,1)}, bf16[672,512]{1,0:T(8,128)(2,1)S(1)}, u32[]{:S(2)}, u32[]{:S(2)}) %collective-permute-start.6) | collective-permute-done | bytes 688160 | tf_op jit(solution)/shard_map/ppermute | solution.py:27
  61.1 0.1 collective-permute-start.7
  61.2 0.3 collective-permute-done.2
  61.6 3.7 %collective-permute-start.8 = (bf16[336,512]{1,0:T(8,128)(2,1)S(1)}, bf16[336,512]{1,0:T(8,128)(2,1)S(1)}, u32[]{:S(2)}, u32[]{:S(2)}) collective-permute-start(bf16[336,512]{1,0:T(8,128)(2,1)S(1)} %slice.100), channel_id=1, source_target_pairs={{0,96},{32,0},{64,32},{96,64},{1,97},{33,1},{65,33},{97,65},{2,98}... | collective-permute-start | bytes 1032200 | tf_op jit(solution)/shard_map/ppermute | solution.py:27
  65.3 1.2 constant_dynamic-update-slice_fusion.5
  66.6 3.5 %collective-permute-done.7 = bf16[336,512]{1,0:T(8,128)(2,1)S(1)} collective-permute-done((bf16[336,512]{1,0:T(8,128)(2,1)S(1)}, bf16[336,512]{1,0:T(8,128)(2,1)S(1)}, u32[]{:S(2)}, u32[]{:S(2)}) %collective-permute-start.7) | collective-permute-done | bytes 344096 | tf_op jit(solution)/shard_map/ppermute | solution.py:27
  70.0 0.1 collective-permute-done.8
  70.2 1.2 constant_dynamic-update-slice_fusion.4
  71.4 1.2 constant_dynamic-update-slice_fusion.3
  72.6 12.5 %all-gather.2.cloned.1.call-done = bf16[1024,5376]{1,0:T(8,128)(2,1)} async-done(((bf16[64,5376]{1,0:T(8,128)(2,1)}), bf16[1024,5376]{1,0:T(8,128)(2,1)}) %all-gather.2.cloned.1.call-update) | async-done | bytes 11010064 | tf_op jit(solution)/shard_map/all_gather | solution.py:105
  85.0 10.3 %fusion.47 = f32[1024,512]{0,1:T(8,128)S(1)} fusion(bf16[1024,5376]{1,0:T(8,128)(2,1)} %all-gather.2.cloned.1.call-done, bf16[5376,512]{1,0:T(8,128)(2,1)} %bitcast.8), kind=kOutput, calls=%fused_computation.108 | convolution fusion | flops 5637144576 | bytes 18612224 | tf_op jit(solution)/shard_map/dot_general | solution.py:109
  95.5 1.1 slice.107
  96.5 0.1 multiply_reduce_fusion
  96.7 0.1 multiply_bitcast_fusion
  96.8 1.2 fusion.41
  98.0 0.8 pad_maximum_fusion
  98.8 4.6 %collective-permute-start.9 = (bf16[2,1024,128]{1,2,0:T(8,128)(2,1)}, bf16[2,1024,128]{1,2,0:T(8,128)(2,1)}, u32[]{:S(2)}, u32[]{:S(2)}) collective-permute-start(bf16[2,1024,128]{1,2,0:T(8,128)(2,1)} %pad_maximum_fusion), channel_id=1, source_target_pairs={{0,16},{16,32},{32,48},{48,64},{64,80},{80,96},{96,112},{1,17},{17... | collective-permute-start | bytes 1572872 | tf_op jit(solution)/shard_map/ppermute | solution.py:21
  103.4 1.5 copy.10
  104.9 2.1 collective-permute-start.10
  107.1 1.0 bitcast_dynamic-update-slice_fusion.10
  108.1 0.3 multiply_multiply_fusion
  108.5 0.5 multiply_subtract_fusion
  109.0 0.3 fusion.20
  109.3 12.5 %collective-permute-done.10 = bf16[32,5376]{1,0:T(8,128)(2,1)S(1)} collective-permute-done((bf16[32,5376]{1,0:T(8,128)(2,1)}, bf16[32,5376]{1,0:T(8,128)(2,1)S(1)}, u32[]{:S(2)}, u32[]{:S(2)}) %collective-permute-start.10) | collective-permute-done | bytes 344096 | tf_op jit(solution)/shard_map/ppermute | solution.py:27
  121.8 5.8 %collective-permute-start.11 = (bf16[2,32,5376]{2,1,0:T(8,128)(2,1)S(1)}, bf16[2,32,5376]{2,1,0:T(8,128)(2,1)S(1)}, u32[]{:S(2)}, u32[]{:S(2)}) collective-permute-start(bf16[2,32,5376]{2,1,0:T(8,128)(2,1)S(1)} %bitcast_dynamic-update-slice_fusion.9), channel_id=1, source_target_pairs={{0,96},{32,0},{64,32},{96,64},{1,97},{33,1},{65,33},{97,65},{2,98}... | collective-permute-start | bytes 2064392 | tf_op jit(solution)/shard_map/ppermute | solution.py:27
  127.6 0.2 broadcast_in_dim.116
  127.9 1.1 maximum_maximum_fusion
  129.0 1.3 fusion
  130.3 1.3 fusion.2
  131.6 2.0 fusion.14
  133.6 1.3 fusion.1
  134.9 1.3 fusion.3
  136.2 2.0 fusion.17
  138.2 7.7 %collective-permute-done.12 = bf16[2,32,5376]{2,1,0:T(8,128)(2,1)S(1)} collective-permute-done((bf16[2,32,5376]{2,1,0:T(8,128)(2,1)S(1)}, bf16[2,32,5376]{2,1,0:T(8,128)(2,1)S(1)}, u32[]{:S(2)}, u32[]{:S(2)}) %collective-permute-start.12) | collective-permute-done | bytes 688160 | tf_op jit(solution)/shard_map/ppermute | solution.py:27
  146.0 3.5 %collective-permute-start.14 = (bf16[1,32,5376]{2,1,0:T(8,128)(2,1)S(1)}, bf16[1,32,5376]{2,1,0:T(8,128)(2,1)S(1)}, u32[]{:S(2)}, u32[]{:S(2)}) collective-permute-start(bf16[1,32,5376]{2,1,0:T(8,128)(2,1)S(1)} %slice.115), channel_id=1, source_target_pairs={{0,96},{32,0},{64,32},{96,64},{1,97},{33,1},{65,33},{97,65},{2,98}... | collective-permute-start | bytes 1032200 | tf_op jit(solution)/shard_map/ppermute | solution.py:27
  149.6 6.4 %collective-permute-done.13 = bf16[1,32,5376]{2,1,0:T(8,128)(2,1)S(1)} collective-permute-done((bf16[1,32,5376]{2,1,0:T(8,128)(2,1)S(1)}, bf16[1,32,5376]{2,1,0:T(8,128)(2,1)S(1)}, u32[]{:S(2)}, u32[]{:S(2)}) %collective-permute-start.13) | collective-permute-done | bytes 344096 | tf_op jit(solution)/shard_map/ppermute | solution.py:27
  156.1 5.9 %convolution_convert_fusion = bf16[1024,5376]{1,0:T(8,128)(2,1)} fusion(bf16[256,5376]{1,0:T(8,128)(2,1)S(1)} %bitcast.125, bf16[512,256]{0,1:T(8,128)(2,1)S(1)} %bitcast.128, bf16[512,256]{0,1:T(8,128)(2,1)S(1)} %bitcast.127), kind=kOutput, calls=%fused_computation | convolution fusion | flops 2825125888 | bytes 14286848 | tf_op jit(solution)/shard_map/dot_general | solution.py:172
  162.1 80.7 %reduce-scatter.2.cloned.1.call-done = bf16[64,5376]{1,0:T(8,128)(2,1)} async-done(((bf16[1024,5376]{1,0:T(8,128)(2,1)}), bf16[64,5376]{1,0:T(8,128)(2,1)}) %reduce-scatter.2.cloned.1.call-update) | async-done | bytes 688144 | tf_op jit(solution)/shard_map/reduce_scatter | solution.py:175
  242.8 1.3 fusion.8
  244.1 2.3 fusion.13
  (63 shorter events, 1.0 us)
Async XLA Ops:
  6.5 3.7 %copy-start.4 = (bf16[672,256]{1,0:T(8,128)(2,1)S(1)}, bf16[672,256]{1,0:T(8,128)(2,1)}, u32[]{:S(2)}) copy-start(bf16[672,256]{1,0:T(8,128)(2,1)} %param.11) | copy-start | bytes 1032196
  6.5 4.5 %copy-start.5 = (bf16[672,128]{1,0:T(8,128)(2,1)S(1)}, bf16[672,128]{1,0:T(8,128)(2,1)}, u32[]{:S(2)}) copy-start(bf16[672,128]{1,0:T(8,128)(2,1)} %param.12) | copy-start | bytes 516100
  6.5 5.2 %copy-start.6 = (bf16[672,128]{1,0:T(8,128)(2,1)S(1)}, bf16[672,128]{1,0:T(8,128)(2,1)}, u32[]{:S(2)}) copy-start(bf16[672,128]{1,0:T(8,128)(2,1)} %param.13) | copy-start | bytes 516100
  6.5 78.5 %all-gather.2.cloned.1.call-start = ((), (), s32[]{:S(2)}) async-start(), calls=%async_computation.1 | async-start | bytes 11698176 | tf_op jit(solution)/shard_map/all_gather | solution.py:105
  10.2 232.6 %reduce-scatter.2.cloned.1.call-start = ((), (), s32[]{:S(2)}) async-start(), calls=%async_computation.2 | async-start | bytes 11698176 | tf_op jit(solution)/shard_map/reduce_scatter | solution.py:175
  12.4 28.5 %collective-permute-start = (bf16[672,512]{1,0:T(8,128)(2,1)}, bf16[672,512]{1,0:T(8,128)(2,1)}, u32[]{:S(2)}, u32[]{:S(2)}) collective-permute-start(bf16[672,512]{1,0:T(8,128)(2,1)} %constant_dynamic-update-slice_fusion), channel_id=1, source_target_pairs={{0,16},{16,0},{1,17},{17,1},{2,18},{18,2},{3,19},{19,3},{4,20},{20... | collective-permute-start | bytes 2064392 | tf_op jit(solution)/shard_map/ppermute | solution.py:27
  15.8 20.9 %collective-permute-start.1 = (bf16[672,512]{1,0:T(8,128)(2,1)}, bf16[672,512]{1,0:T(8,128)(2,1)}, u32[]{:S(2)}, u32[]{:S(2)}) collective-permute-start(bf16[672,512]{1,0:T(8,128)(2,1)} %constant_dynamic-update-slice_fusion), channel_id=1, source_target_pairs={{0,96},{32,0},{64,32},{96,64},{1,97},{33,1},{65,33},{97,65},{2,98}... | collective-permute-start | bytes 2064392 | tf_op jit(solution)/shard_map/ppermute | solution.py:27
  18.5 18.0 %collective-permute-start.3 = (bf16[672,512]{1,0:T(8,128)(2,1)}, bf16[672,512]{1,0:T(8,128)(2,1)S(1)}, u32[]{:S(2)}, u32[]{:S(2)}) collective-permute-start(bf16[672,512]{1,0:T(8,128)(2,1)} %constant_dynamic-update-slice_fusion), channel_id=1, source_target_pairs={{0,32},{32,64},{64,96},{96,0},{1,33},{33,65},{65,97},{97,1},{2,34}... | collective-permute-start | bytes 2064392 | tf_op jit(solution)/shard_map/ppermute | solution.py:27
  36.6 13.4 %collective-permute-start.4 = (bf16[336,512]{1,0:T(8,128)(2,1)S(1)}, bf16[336,512]{1,0:T(8,128)(2,1)S(1)}, u32[]{:S(2)}, u32[]{:S(2)}) collective-permute-start(bf16[336,512]{1,0:T(8,128)(2,1)S(1)} %slice.97), channel_id=1, source_target_pairs={{0,32},{32,64},{64,96},{96,0},{1,33},{33,65},{65,97},{97,1},{2,34}... | collective-permute-start | bytes 1032200 | tf_op jit(solution)/shard_map/ppermute | solution.py:27
  37.7 12.4 %collective-permute-start.5 = (bf16[336,512]{1,0:T(8,128)(2,1)S(1)}, bf16[336,512]{1,0:T(8,128)(2,1)S(1)}, u32[]{:S(2)}, u32[]{:S(2)}) collective-permute-start(bf16[336,512]{1,0:T(8,128)(2,1)S(1)} %slice.98), channel_id=1, source_target_pairs={{0,96},{32,0},{64,32},{96,64},{1,97},{33,1},{65,33},{97,65},{2,98}... | collective-permute-start | bytes 1032200 | tf_op jit(solution)/shard_map/ppermute | solution.py:27
  41.0 20.6 %collective-permute-start.2 = (bf16[672,512]{1,0:T(8,128)(2,1)}, bf16[672,512]{1,0:T(8,128)(2,1)S(1)}, u32[]{:S(2)}, u32[]{:S(2)}) collective-permute-start(bf16[672,512]{1,0:T(8,128)(2,1)} %collective-permute-done), channel_id=1, source_target_pairs={{0,96},{32,0},{64,32},{96,64},{1,97},{33,1},{65,33},{97,65},{2,98}... | collective-permute-start | bytes 2064392 | tf_op jit(solution)/shard_map/ppermute | solution.py:27
  43.4 17.7 %collective-permute-start.6 = (bf16[672,512]{1,0:T(8,128)(2,1)}, bf16[672,512]{1,0:T(8,128)(2,1)S(1)}, u32[]{:S(2)}, u32[]{:S(2)}) collective-permute-start(bf16[672,512]{1,0:T(8,128)(2,1)} %collective-permute-done), channel_id=1, source_target_pairs={{0,32},{32,64},{64,96},{96,0},{1,33},{33,65},{65,97},{97,1},{2,34}... | collective-permute-start | bytes 2064392 | tf_op jit(solution)/shard_map/ppermute | solution.py:27
  61.1 8.9 %collective-permute-start.7 = (bf16[336,512]{1,0:T(8,128)(2,1)S(1)}, bf16[336,512]{1,0:T(8,128)(2,1)S(1)}, u32[]{:S(2)}, u32[]{:S(2)}) collective-permute-start(bf16[336,512]{1,0:T(8,128)(2,1)S(1)} %slice.99), channel_id=1, source_target_pairs={{0,32},{32,64},{64,96},{96,0},{1,33},{33,65},{65,97},{97,1},{2,34}... | collective-permute-start | bytes 1032200 | tf_op jit(solution)/shard_map/ppermute | solution.py:27
  61.6 8.5 %collective-permute-start.8 = (bf16[336,512]{1,0:T(8,128)(2,1)S(1)}, bf16[336,512]{1,0:T(8,128)(2,1)S(1)}, u32[]{:S(2)}, u32[]{:S(2)}) collective-permute-start(bf16[336,512]{1,0:T(8,128)(2,1)S(1)} %slice.100), channel_id=1, source_target_pairs={{0,96},{32,0},{64,32},{96,64},{1,97},{33,1},{65,33},{97,65},{2,98}... | collective-permute-start | bytes 1032200 | tf_op jit(solution)/shard_map/ppermute | solution.py:27
  95.4 1.3 copy-start.8
  96.8 11.3 %copy-start.9 = (f32[128]{0:T(128)S(1)}, f32[128]{0:T(128)}, u32[]{:S(2)}) copy-start(f32[128]{0:T(128)} %param.14) | copy-start | bytes 1540
  98.0 5.4 %copy-start.2 = (bf16[1,1024,64]{1,2,0:T(8,128)(2,1)}, bf16[1,1024,64]{1,2,0:T(8,128)(2,1)S(1)}, u32[]{:S(2)}) copy-start(bf16[1,1024,64]{1,2,0:T(8,128)(2,1)S(1)} %get-tuple-element.12) | copy-start | bytes 393220
  98.8 29.0 %collective-permute-start.9 = (bf16[2,1024,128]{1,2,0:T(8,128)(2,1)}, bf16[2,1024,128]{1,2,0:T(8,128)(2,1)}, u32[]{:S(2)}, u32[]{:S(2)}) collective-permute-start(bf16[2,1024,128]{1,2,0:T(8,128)(2,1)} %pad_maximum_fusion), channel_id=1, source_target_pairs={{0,16},{16,32},{32,48},{48,64},{64,80},{80,96},{96,112},{1,17},{17... | collective-permute-start | bytes 1572872 | tf_op jit(solution)/shard_map/ppermute | solution.py:21
  104.9 3.5 %copy-start.1 = (f32[1024,64]{1,0:T(8,128)S(1)}, f32[1024,64]{1,0:T(8,128)}, u32[]{:S(2)}) copy-start(f32[1024,64]{1,0:T(8,128)} %get-tuple-element.14) | copy-start | bytes 786436
  104.9 16.8 %collective-permute-start.10 = (bf16[32,5376]{1,0:T(8,128)(2,1)}, bf16[32,5376]{1,0:T(8,128)(2,1)S(1)}, u32[]{:S(2)}, u32[]{:S(2)}) collective-permute-start(bf16[32,5376]{1,0:T(8,128)(2,1)} %param.16), channel_id=1, source_target_pairs={{0,16},{16,0},{1,17},{17,1},{2,18},{18,2},{3,19},{19,3},{4,20},{20... | collective-permute-start | bytes 1032200 | tf_op jit(solution)/shard_map/ppermute | solution.py:27
  109.3 18.5 %copy-start.3 = (bf16[1,1024,64]{1,2,0:T(8,128)(2,1)S(1)}, bf16[1,1024,64]{1,2,0:T(8,128)(2,1)}, u32[]{:S(2)}) copy-start(bf16[1,1024,64]{1,2,0:T(8,128)(2,1)} %copy-done.2) | copy-start | bytes 393220
  121.8 24.2 %collective-permute-start.11 = (bf16[2,32,5376]{2,1,0:T(8,128)(2,1)S(1)}, bf16[2,32,5376]{2,1,0:T(8,128)(2,1)S(1)}, u32[]{:S(2)}, u32[]{:S(2)}) collective-permute-start(bf16[2,32,5376]{2,1,0:T(8,128)(2,1)S(1)} %bitcast_dynamic-update-slice_fusion.9), channel_id=1, source_target_pairs={{0,96},{32,0},{64,32},{96,64},{1,97},{33,1},{65,33},{97,65},{2,98}... | collective-permute-start | bytes 2064392 | tf_op jit(solution)/shard_map/ppermute | solution.py:27
  127.6 18.3 %collective-permute-start.12 = (bf16[2,32,5376]{2,1,0:T(8,128)(2,1)S(1)}, bf16[2,32,5376]{2,1,0:T(8,128)(2,1)S(1)}, u32[]{:S(2)}, u32[]{:S(2)}) collective-permute-start(bf16[2,32,5376]{2,1,0:T(8,128)(2,1)S(1)} %bitcast_dynamic-update-slice_fusion.9), channel_id=1, source_target_pairs={{0,32},{32,64},{64,96},{96,0},{1,33},{33,65},{65,97},{97,1},{2,34}... | collective-permute-start | bytes 2064392 | tf_op jit(solution)/shard_map/ppermute | solution.py:27
  145.9 10.1 %collective-permute-start.13 = (bf16[1,32,5376]{2,1,0:T(8,128)(2,1)S(1)}, bf16[1,32,5376]{2,1,0:T(8,128)(2,1)S(1)}, u32[]{:S(2)}, u32[]{:S(2)}) collective-permute-start(bf16[1,32,5376]{2,1,0:T(8,128)(2,1)S(1)} %slice.114), channel_id=1, source_target_pairs={{0,32},{32,64},{64,96},{96,0},{1,33},{33,65},{65,97},{97,1},{2,34}... | collective-permute-start | bytes 1032200 | tf_op jit(solution)/shard_map/ppermute | solution.py:27
  146.0 10.0 %collective-permute-start.14 = (bf16[1,32,5376]{2,1,0:T(8,128)(2,1)S(1)}, bf16[1,32,5376]{2,1,0:T(8,128)(2,1)S(1)}, u32[]{:S(2)}, u32[]{:S(2)}) collective-permute-start(bf16[1,32,5376]{2,1,0:T(8,128)(2,1)S(1)} %slice.115), channel_id=1, source_target_pairs={{0,96},{32,0},{64,32},{96,64},{1,97},{33,1},{65,33},{97,65},{2,98}... | collective-permute-start | bytes 1032200 | tf_op jit(solution)/shard_map/ppermute | solution.py:27
  162.0 82.1 %copy-start = (bf16[64,5376]{1,0:T(8,128)(2,1)S(1)}, bf16[64,5376]{1,0:T(8,128)(2,1)}, u32[]{:S(2)}) copy-start(bf16[64,5376]{1,0:T(8,128)(2,1)} %param.9) | copy-start | bytes 2064388
  162.0 82.1 %copy-start.7 = (f32[5376]{0:T(1024)S(1)}, f32[5376]{0:T(1024)}, u32[]{:S(2)}) copy-start(f32[5376]{0:T(1024)} %param.17) | copy-start | bytes 64516
Sparse Core Ops, SparseCore 0:
  10.3 74.6 all-gather.1
  162.2 80.5 reduce-scatter.1

commit v12 on v11

--- a/solution.py
+++ b/solution.py
@@ -54,11 +54,13 @@
     return ring.reshape((8 * piece.shape[0],) + piece.shape[1:])
 
 
-def gathered_pair_first(piece):
+def gathered_with_partner(piece, crossed):
     cy = lax.axis_index("cy")
     cx = lax.axis_index("cx")
-    pair = placed([piece, rotated(piece, "cy", 1)], cy, 2)
-    ring = placed(ring_over_cx(pair), cx, 4)
+    own = ring_over_cx(piece)
+    partner = ring_over_cx(crossed)
+    pairs = [placed([a, b], cy, 2) for a, b in zip(own, partner)]
+    ring = placed(pairs, cx, 4)
     return ring.reshape((8 * piece.shape[0],) + piece.shape[1:])
 
 
@@ -103,8 +105,9 @@
 
     own_normed = root_mean_scale(own_rows, pre_gain).astype(jnp.bfloat16)
     normed = lax.all_gather(own_normed, HEAD, axis=0, tiled=True)
-    normed, w_output = lax.optimization_barrier((normed, w_output))
-    out_weight = gathered_pair_first(w_output)
+    crossed = rotated(w_output, "cy", 1)
+    normed, w_output, crossed = lax.optimization_barrier((normed, w_output, crossed))
+    out_weight = gathered_with_partner(w_output, crossed)
     tok_count = normed.shape[0]
     projected = jnp.dot(normed, w_in, preferred_element_type=jnp.float32)
     query_raw = projected[:, :q_cols]

time: 254 us -> 250 us (0.984)
  waiting for transfers between devices: 146 us -> 129 us
  local copies, waits for them, and re-layouts: 19.1 us -> 29 us
    ppermute x14 -> x18, waiting for transfers between devices: 52.9 us -> 25.8 us  [rotated(): return lax.ppermute(shard, axis, pairs)]
    all_gather x1, waiting for transfers between devices: 12.5 us -> 19.9 us  [body(): normed = lax.all_gather(own_normed, HEAD, axis=0, tiled=True)]
    dynamic_update_slice x15 -> x20, local copies, waits for them, and re-layouts: 9.65 us -> 14.7 us  [placed(): lax.dynamic_update_index_in_dim(stacked, part, (me + i) % count, 0)]
    reduce_scatter x1, waiting for transfers between devices: 80.7 us -> 83.8 us  [body(): lax.psum_scatter(partial_value, HEAD, scatter_dimension=0, tiled=True)]
    ppermute x14 -> x18, starting transfers between devices: 27 us -> 29.2 us  [rotated(): return lax.ppermute(shard, axis, pairs)]
  transfers between devices with their start and end apart: 17 -> 21, of which waited for: 10 -> 8; matrix products, arithmetic and copies ran while one was open for 14% -> 14% of each run, Pallas kernels for 0% -> 0%
where the time goes in v12:
time: 250 us; the launch traced here: 249 us
  waiting for transfers between devices  129 us (52%)
  starting transfers between devices  33.8 us (14%)
  local copies, waits for them, and re-layouts  29 us (12%)
  matrix products  22.8 us (9%)
  other arithmetic  19.8 us (8%)
  between operations  14 us (6%)
    reduce_scatter x1, waiting for transfers between devices, body(): lax.psum_scatter(partial_value, HEAD, scatter_dimension=0, tiled=True)  83.8 us
    ppermute x18, starting transfers between devices, rotated(): return lax.ppermute(shard, axis, pairs)  29.2 us
    ppermute x18, waiting for transfers between devices, rotated(): return lax.ppermute(shard, axis, pairs)  25.8 us
    all_gather x1, waiting for transfers between devices, body(): normed = lax.all_gather(own_normed, HEAD, axis=0, tiled=True)  19.9 us
    dynamic_update_slice x20, local copies, waits for them, and re-layouts, placed(): lax.dynamic_update_index_in_dim(stacked, part, (me + i) % count, 0)  14.7 us
    dot_general x1, matrix products, body(): projected = jnp.dot(normed, w_in, preferred_element_type=jnp.float32)  10.3 us
    dot_general x1, matrix products, body(): jnp.dot(attended, out_weight, preferred_element_type=jnp.float32)  5.86 us
  transfers between devices with their start and end apart: 21, of which 8 were waited for; matrix products, arithmetic and copies ran while one was open for 14% of the time, Pallas kernels for 0%

profile of v12, /device:TPU:0, one launch (start us, length us, event | category | flops | bytes accessed | tf_op | source)
XLA Modules:
  0.0 248.7 jit_solution(10108746350810854791)
XLA Ops:
  6.5 1.4 fusion.10
  8.0 2.2 fusion.12
  10.2 0.8 constant_dynamic-update-slice_fusion.2
  11.0 0.7 constant_dynamic-update-slice_fusion.1
  11.7 0.7 constant_dynamic-update-slice_fusion
  12.4 3.3 %collective-permute-start.1 = (bf16[672,512]{1,0:T(8,128)(2,1)}, bf16[672,512]{1,0:T(8,128)(2,1)}, u32[]{:S(2)}, u32[]{:S(2)}) collective-permute-start(bf16[672,512]{1,0:T(8,128)(2,1)} %constant_dynamic-update-slice_fusion), channel_id=1, source_target_pairs={{0,16},{16,0},{1,17},{17,1},{2,18},{18,2},{3,19},{19,3},{4,20},{20... | collective-permute-start | bytes 2064392 | tf_op jit(solution)/shard_map/ppermute | solution.py:27
  15.7 2.8 %collective-permute-start.2 = (bf16[672,512]{1,0:T(8,128)(2,1)}, bf16[672,512]{1,0:T(8,128)(2,1)}, u32[]{:S(2)}, u32[]{:S(2)}) collective-permute-start(bf16[672,512]{1,0:T(8,128)(2,1)} %constant_dynamic-update-slice_fusion), channel_id=1, source_target_pairs={{0,96},{32,0},{64,32},{96,64},{1,97},{33,1},{65,33},{97,65},{2,98}... | collective-permute-start | bytes 2064392 | tf_op jit(solution)/shard_map/ppermute | solution.py:27
  19.0 1.2 bitcast_dynamic-update-slice_fusion.5
  20.2 1.1 and_and_fusion.1
  21.3 2.9 %multiply_cosine_fusion = (f32[1024,64]{1,0:T(8,128)S(1)}, f32[1024,64]{1,0:T(8,128)}) fusion(f32[64]{0:T(128)S(1)} %multiply_power_fusion, f32[1024]{0:T(1024)S(1)} %get-tuple-element.26), kind=kLoop, calls=%fused_computation.38 | loop fusion | flops 65536 | bytes 528640 | tf_op jit(solution)/shard_map/cos | solution.py:77
  24.2 1.1 and_and_fusion
  25.4 11.2 %collective-permute-done.4 = bf16[672,512]{1,0:T(8,128)(2,1)S(1)} collective-permute-done((bf16[672,512]{1,0:T(8,128)(2,1)}, bf16[672,512]{1,0:T(8,128)(2,1)S(1)}, u32[]{:S(2)}, u32[]{:S(2)}) %collective-permute-start.4) | collective-permute-done | bytes 688160 | tf_op jit(solution)/shard_map/ppermute | solution.py:27
  36.6 1.0 slice.106
  37.7 3.3 %collective-permute-start.6 = (bf16[336,512]{1,0:T(8,128)(2,1)S(1)}, bf16[336,512]{1,0:T(8,128)(2,1)S(1)}, u32[]{:S(2)}, u32[]{:S(2)}) collective-permute-start(bf16[336,512]{1,0:T(8,128)(2,1)S(1)} %slice.106), channel_id=1, source_target_pairs={{0,96},{32,0},{64,32},{96,64},{1,97},{33,1},{65,33},{97,65},{2,98}... | collective-permute-start | bytes 1032200 | tf_op jit(solution)/shard_map/ppermute | solution.py:27
  40.9 0.9 collective-permute-done.1
  41.8 2.7 %collective-permute-start.3 = (bf16[672,512]{1,0:T(8,128)(2,1)}, bf16[672,512]{1,0:T(8,128)(2,1)S(1)}, u32[]{:S(2)}, u32[]{:S(2)}) collective-permute-start(bf16[672,512]{1,0:T(8,128)(2,1)} %collective-permute-done.1), channel_id=1, source_target_pairs={{0,96},{32,0},{64,32},{96,64},{1,97},{33,1},{65,33},{97,65},{2,98}... | collective-permute-start | bytes 2064392 | tf_op jit(solution)/shard_map/ppermute | solution.py:27
  44.6 1.2 bitcast_dynamic-update-slice_fusion.3
  45.8 1.2 bitcast_dynamic-update-slice_fusion.4
  46.9 2.8 %broadcast_in_dim.112 = bf16[4,2,672,512]{3,2,1,0:T(8,128)(2,1)} broadcast(bf16[]{:T(256)} %constant.186.clone.1), dimensions={} | broadcast | bytes 5505026 | tf_op jit(solution)/shard_map/broadcast_in_dim | solution.py:31
  49.8 1.2 constant_dynamic-update-slice_fusion.10
  51.3 9.8 %collective-permute-done.7 = bf16[672,512]{1,0:T(8,128)(2,1)S(1)} collective-permute-done((bf16[672,512]{1,0:T(8,128)(2,1)}, bf16[672,512]{1,0:T(8,128)(2,1)S(1)}, u32[]{:S(2)}, u32[]{:S(2)}) %collective-permute-start.7) | collective-permute-done | bytes 688160 | tf_op jit(solution)/shard_map/ppermute | solution.py:27
  61.2 0.3 collective-permute-done.3
  61.6 3.7 %collective-permute-start.9 = (bf16[336,512]{1,0:T(8,128)(2,1)S(1)}, bf16[336,512]{1,0:T(8,128)(2,1)S(1)}, u32[]{:S(2)}, u32[]{:S(2)}) collective-permute-start(bf16[336,512]{1,0:T(8,128)(2,1)S(1)} %slice.108), channel_id=1, source_target_pairs={{0,96},{32,0},{64,32},{96,64},{1,97},{33,1},{65,33},{97,65},{2,98}... | collective-permute-start | bytes 1032200 | tf_op jit(solution)/shard_map/ppermute | solution.py:27
  65.3 1.3 constant_dynamic-update-slice_fusion.9
  66.6 3.1 %collective-permute-done.8 = bf16[336,512]{1,0:T(8,128)(2,1)S(1)} collective-permute-done((bf16[336,512]{1,0:T(8,128)(2,1)S(1)}, bf16[336,512]{1,0:T(8,128)(2,1)S(1)}, u32[]{:S(2)}, u32[]{:S(2)}) %collective-permute-start.8) | collective-permute-done | bytes 344096 | tf_op jit(solution)/shard_map/ppermute | solution.py:27
  69.6 0.5 collective-permute-done.9
  70.1 1.2 constant_dynamic-update-slice_fusion.8
  71.3 1.2 constant_dynamic-update-slice_fusion.7
  72.5 19.9 %all-gather.2.cloned.1.call-done = bf16[1024,5376]{1,0:T(8,128)(2,1)} async-done(((bf16[64,5376]{1,0:T(8,128)(2,1)}), bf16[1024,5376]{1,0:T(8,128)(2,1)}) %all-gather.2.cloned.1.call-update) | async-done | bytes 11010064 | tf_op jit(solution)/shard_map/all_gather | solution.py:107
  92.4 10.3 %fusion.48 = f32[1024,512]{0,1:T(8,128)S(1)} fusion(bf16[1024,5376]{1,0:T(8,128)(2,1)} %all-gather.2.cloned.1.call-done, bf16[5376,512]{1,0:T(8,128)(2,1)} %bitcast.8), kind=kOutput, calls=%fused_computation.115 | convolution fusion | flops 5637144576 | bytes 18612224 | tf_op jit(solution)/shard_map/dot_general | solution.py:112
  102.8 1.1 slice.115
  104.0 2.8 %collective-permute-start.11 = (bf16[32,5376]{1,0:T(8,128)(2,1)}, bf16[32,5376]{1,0:T(8,128)(2,1)}, u32[]{:S(2)}, u32[]{:S(2)}) collective-permute-start(bf16[32,5376]{1,0:T(8,128)(2,1)} %param.16), channel_id=1, source_target_pairs={{0,96},{32,0},{64,32},{96,64},{1,97},{33,1},{65,33},{97,65},{2,98}... | collective-permute-start | bytes 1032200 | tf_op jit(solution)/shard_map/ppermute | solution.py:27
  106.8 3.2 %collective-permute-start.12 = (bf16[32,5376]{1,0:T(8,128)(2,1)}, bf16[32,5376]{1,0:T(8,128)(2,1)}, u32[]{:S(2)}, u32[]{:S(2)}) collective-permute-start(bf16[32,5376]{1,0:T(8,128)(2,1)} %collective-permute-done), channel_id=1, source_target_pairs={{0,96},{32,0},{64,32},{96,64},{1,97},{33,1},{65,33},{97,65},{2,98}... | collective-permute-start | bytes 1032200 | tf_op jit(solution)/shard_map/ppermute | solution.py:27
  110.2 1.2 fusion.42
  111.4 0.8 pad_maximum_fusion
  112.2 4.6 %collective-permute-start.10 = (bf16[2,1024,128]{1,2,0:T(8,128)(2,1)}, bf16[2,1024,128]{1,2,0:T(8,128)(2,1)}, u32[]{:S(2)}, u32[]{:S(2)}) collective-permute-start(bf16[2,1024,128]{1,2,0:T(8,128)(2,1)} %pad_maximum_fusion), channel_id=1, source_target_pairs={{0,16},{16,32},{32,48},{48,64},{64,80},{80,96},{96,112},{1,17},{17... | collective-permute-start | bytes 1572872 | tf_op jit(solution)/shard_map/ppermute | solution.py:21
  116.8 1.5 copy.10
  118.4 1.0 bitcast_dynamic-update-slice_fusion.11
  119.4 1.0 bitcast_dynamic-update-slice_fusion.10
  121.0 0.4 copy-done.1
  121.5 0.5 multiply_subtract_fusion
  122.0 0.3 fusion.20
  122.3 0.9 slice.122
  123.4 0.9 slice.123
  124.3 3.3 %collective-permute-start.15 = (bf16[16,5376]{1,0:T(8,128)(2,1)S(1)}, bf16[16,5376]{1,0:T(8,128)(2,1)S(1)}, u32[]{:S(2)}, u32[]{:S(2)}) collective-permute-start(bf16[16,5376]{1,0:T(8,128)(2,1)S(1)} %slice.123), channel_id=1, source_target_pairs={{0,96},{32,0},{64,32},{96,64},{1,97},{33,1},{65,33},{97,65},{2,98}... | collective-permute-start | bytes 516104 | tf_op jit(solution)/shard_map/ppermute | solution.py:27
  127.6 0.9 slice.124
  128.6 0.9 slice.125
  129.6 3.5 %collective-permute-start.18 = (bf16[16,5376]{1,0:T(8,128)(2,1)S(1)}, bf16[16,5376]{1,0:T(8,128)(2,1)S(1)}, u32[]{:S(2)}, u32[]{:S(2)}) collective-permute-start(bf16[16,5376]{1,0:T(8,128)(2,1)S(1)} %slice.125), channel_id=1, source_target_pairs={{0,96},{32,0},{64,32},{96,64},{1,97},{33,1},{65,33},{97,65},{2,98}... | collective-permute-start | bytes 516104 | tf_op jit(solution)/shard_map/ppermute | solution.py:27
  133.1 1.0 bitcast_dynamic-update-slice_fusion.9
  134.1 1.0 bitcast_dynamic-update-slice_fusion.8
  135.2 1.0 bitcast_dynamic-update-slice_fusion.7
  136.2 1.0 bitcast_dynamic-update-slice_fusion.6
  137.6 0.6 copy-done.3
  138.2 1.1 maximum_maximum_fusion
  139.3 1.3 fusion
  140.6 1.3 fusion.2
  141.9 2.0 fusion.14
  143.9 1.3 fusion.1
  145.2 1.3 fusion.3
  146.5 2.0 fusion.17
  148.5 5.9 %convolution_convert_fusion = bf16[1024,5376]{1,0:T(8,128)(2,1)} fusion(bf16[256,5376]{1,0:T(8,128)(2,1)S(1)} %bitcast.131, bf16[512,256]{0,1:T(8,128)(2,1)S(1)} %bitcast.134, bf16[512,256]{0,1:T(8,128)(2,1)S(1)} %bitcast.133), kind=kOutput, calls=%fused_computation | convolution fusion | flops 2825125888 | bytes 14286848 | tf_op jit(solution)/shard_map/dot_general | solution.py:175
  154.4 83.8 %reduce-scatter.2.cloned.1.call-done = bf16[64,5376]{1,0:T(8,128)(2,1)} async-done(((bf16[1024,5376]{1,0:T(8,128)(2,1)}), bf16[64,5376]{1,0:T(8,128)(2,1)}) %reduce-scatter.2.cloned.1.call-update) | async-done | bytes 688144 | tf_op jit(solution)/shard_map/reduce_scatter | solution.py:178
  238.2 1.3 fusion.8
  239.6 2.3 fusion.13
  (82 shorter events, 2.8 us)
Async XLA Ops:
  6.5 3.7 %copy-start.4 = (bf16[672,256]{1,0:T(8,128)(2,1)S(1)}, bf16[672,256]{1,0:T(8,128)(2,1)}, u32[]{:S(2)}) copy-start(bf16[672,256]{1,0:T(8,128)(2,1)} %param.11) | copy-start | bytes 1032196
  6.5 4.5 %copy-start.5 = (bf16[672,128]{1,0:T(8,128)(2,1)S(1)}, bf16[672,128]{1,0:T(8,128)(2,1)}, u32[]{:S(2)}) copy-start(bf16[672,128]{1,0:T(8,128)(2,1)} %param.12) | copy-start | bytes 516100
  6.5 5.2 %copy-start.6 = (bf16[672,128]{1,0:T(8,128)(2,1)S(1)}, bf16[672,128]{1,0:T(8,128)(2,1)}, u32[]{:S(2)}) copy-start(bf16[672,128]{1,0:T(8,128)(2,1)} %param.13) | copy-start | bytes 516100
  6.5 85.8 %all-gather.2.cloned.1.call-start = ((), (), s32[]{:S(2)}) async-start(), calls=%async_computation.1 | async-start | bytes 11698176 | tf_op jit(solution)/shard_map/all_gather | solution.py:107
  10.2 228.0 %reduce-scatter.2.cloned.1.call-start = ((), (), s32[]{:S(2)}) async-start(), calls=%async_computation.2 | async-start | bytes 11698176 | tf_op jit(solution)/shard_map/reduce_scatter | solution.py:178
  12.4 29.4 %collective-permute-start.1 = (bf16[672,512]{1,0:T(8,128)(2,1)}, bf16[672,512]{1,0:T(8,128)(2,1)}, u32[]{:S(2)}, u32[]{:S(2)}) collective-permute-start(bf16[672,512]{1,0:T(8,128)(2,1)} %constant_dynamic-update-slice_fusion), channel_id=1, source_target_pairs={{0,16},{16,0},{1,17},{17,1},{2,18},{18,2},{3,19},{19,3},{4,20},{20... | collective-permute-start | bytes 2064392 | tf_op jit(solution)/shard_map/ppermute | solution.py:27
  15.7 20.9 %collective-permute-start.2 = (bf16[672,512]{1,0:T(8,128)(2,1)}, bf16[672,512]{1,0:T(8,128)(2,1)}, u32[]{:S(2)}, u32[]{:S(2)}) collective-permute-start(bf16[672,512]{1,0:T(8,128)(2,1)} %constant_dynamic-update-slice_fusion), channel_id=1, source_target_pairs={{0,96},{32,0},{64,32},{96,64},{1,97},{33,1},{65,33},{97,65},{2,98}... | collective-permute-start | bytes 2064392 | tf_op jit(solution)/shard_map/ppermute | solution.py:27
  18.5 18.0 %collective-permute-start.4 = (bf16[672,512]{1,0:T(8,128)(2,1)}, bf16[672,512]{1,0:T(8,128)(2,1)S(1)}, u32[]{:S(2)}, u32[]{:S(2)}) collective-permute-start(bf16[672,512]{1,0:T(8,128)(2,1)} %constant_dynamic-update-slice_fusion), channel_id=1, source_target_pairs={{0,32},{32,64},{64,96},{96,0},{1,33},{33,65},{65,97},{97,1},{2,34}... | collective-permute-start | bytes 2064392 | tf_op jit(solution)/shard_map/ppermute | solution.py:27
  18.5 54.0 %collective-permute-start = (bf16[32,5376]{1,0:T(8,128)(2,1)}, bf16[32,5376]{1,0:T(8,128)(2,1)}, u32[]{:S(2)}, u32[]{:S(2)}) collective-permute-start(bf16[32,5376]{1,0:T(8,128)(2,1)} %param.16), channel_id=1, source_target_pairs={{0,16},{16,0},{1,17},{17,1},{2,18},{18,2},{3,19},{19,3},{4,20},{20... | collective-permute-start | bytes 1032200 | tf_op jit(solution)/shard_map/ppermute | solution.py:27
  36.6 14.5 %collective-permute-start.5 = (bf16[336,512]{1,0:T(8,128)(2,1)S(1)}, bf16[336,512]{1,0:T(8,128)(2,1)S(1)}, u32[]{:S(2)}, u32[]{:S(2)}) collective-permute-start(bf16[336,512]{1,0:T(8,128)(2,1)S(1)} %slice.105), channel_id=1, source_target_pairs={{0,32},{32,64},{64,96},{96,0},{1,33},{33,65},{65,97},{97,1},{2,34}... | collective-permute-start | bytes 1032200 | tf_op jit(solution)/shard_map/ppermute | solution.py:27
  37.7 13.4 %collective-permute-start.6 = (bf16[336,512]{1,0:T(8,128)(2,1)S(1)}, bf16[336,512]{1,0:T(8,128)(2,1)S(1)}, u32[]{:S(2)}, u32[]{:S(2)}) collective-permute-start(bf16[336,512]{1,0:T(8,128)(2,1)S(1)} %slice.106), channel_id=1, source_target_pairs={{0,96},{32,0},{64,32},{96,64},{1,97},{33,1},{65,33},{97,65},{2,98}... | collective-permute-start | bytes 1032200 | tf_op jit(solution)/shard_map/ppermute | solution.py:27
  41.8 19.7 %collective-permute-start.3 = (bf16[672,512]{1,0:T(8,128)(2,1)}, bf16[672,512]{1,0:T(8,128)(2,1)S(1)}, u32[]{:S(2)}, u32[]{:S(2)}) collective-permute-start(bf16[672,512]{1,0:T(8,128)(2,1)} %collective-permute-done.1), channel_id=1, source_target_pairs={{0,96},{32,0},{64,32},{96,64},{1,97},{33,1},{65,33},{97,65},{2,98}... | collective-permute-start | bytes 2064392 | tf_op jit(solution)/shard_map/ppermute | solution.py:27
  44.5 16.5 %collective-permute-start.7 = (bf16[672,512]{1,0:T(8,128)(2,1)}, bf16[672,512]{1,0:T(8,128)(2,1)S(1)}, u32[]{:S(2)}, u32[]{:S(2)}) collective-permute-start(bf16[672,512]{1,0:T(8,128)(2,1)} %collective-permute-done.1), channel_id=1, source_target_pairs={{0,32},{32,64},{64,96},{96,0},{1,33},{33,65},{65,97},{97,1},{2,34}... | collective-permute-start | bytes 2064392 | tf_op jit(solution)/shard_map/ppermute | solution.py:27
  61.1 8.5 %collective-permute-start.8 = (bf16[336,512]{1,0:T(8,128)(2,1)S(1)}, bf16[336,512]{1,0:T(8,128)(2,1)S(1)}, u32[]{:S(2)}, u32[]{:S(2)}) collective-permute-start(bf16[336,512]{1,0:T(8,128)(2,1)S(1)} %slice.107), channel_id=1, source_target_pairs={{0,32},{32,64},{64,96},{96,0},{1,33},{33,65},{65,97},{97,1},{2,34}... | collective-permute-start | bytes 1032200 | tf_op jit(solution)/shard_map/ppermute | solution.py:27
  61.6 8.5 %collective-permute-start.9 = (bf16[336,512]{1,0:T(8,128)(2,1)S(1)}, bf16[336,512]{1,0:T(8,128)(2,1)S(1)}, u32[]{:S(2)}, u32[]{:S(2)}) collective-permute-start(bf16[336,512]{1,0:T(8,128)(2,1)S(1)} %slice.108), channel_id=1, source_target_pairs={{0,96},{32,0},{64,32},{96,64},{1,97},{33,1},{65,33},{97,65},{2,98}... | collective-permute-start | bytes 1032200 | tf_op jit(solution)/shard_map/ppermute | solution.py:27
  102.7 7.4 %copy-start.8 = (f32[128]{0:T(128)S(1)}, f32[128]{0:T(128)}, u32[]{:S(2)}) copy-start(f32[128]{0:T(128)} %param.15) | copy-start | bytes 1540
  104.0 19.4 %collective-permute-start.11 = (bf16[32,5376]{1,0:T(8,128)(2,1)}, bf16[32,5376]{1,0:T(8,128)(2,1)}, u32[]{:S(2)}, u32[]{:S(2)}) collective-permute-start(bf16[32,5376]{1,0:T(8,128)(2,1)} %param.16), channel_id=1, source_target_pairs={{0,96},{32,0},{64,32},{96,64},{1,97},{33,1},{65,33},{97,65},{2,98}... | collective-permute-start | bytes 1032200 | tf_op jit(solution)/shard_map/ppermute | solution.py:27
  106.8 15.5 %collective-permute-start.13 = (bf16[32,5376]{1,0:T(8,128)(2,1)}, bf16[32,5376]{1,0:T(8,128)(2,1)}, u32[]{:S(2)}, u32[]{:S(2)}) collective-permute-start(bf16[32,5376]{1,0:T(8,128)(2,1)} %param.16), channel_id=1, source_target_pairs={{0,32},{32,64},{64,96},{96,0},{1,33},{33,65},{65,97},{97,1},{2,34}... | collective-permute-start | bytes 1032200 | tf_op jit(solution)/shard_map/ppermute | solution.py:27
  106.8 21.8 %collective-permute-start.12 = (bf16[32,5376]{1,0:T(8,128)(2,1)}, bf16[32,5376]{1,0:T(8,128)(2,1)}, u32[]{:S(2)}, u32[]{:S(2)}) collective-permute-start(bf16[32,5376]{1,0:T(8,128)(2,1)} %collective-permute-done), channel_id=1, source_target_pairs={{0,96},{32,0},{64,32},{96,64},{1,97},{33,1},{65,33},{97,65},{2,98}... | collective-permute-start | bytes 1032200 | tf_op jit(solution)/shard_map/ppermute | solution.py:27
  110.1 17.5 %collective-permute-start.16 = (bf16[32,5376]{1,0:T(8,128)(2,1)}, bf16[32,5376]{1,0:T(8,128)(2,1)}, u32[]{:S(2)}, u32[]{:S(2)}) collective-permute-start(bf16[32,5376]{1,0:T(8,128)(2,1)} %collective-permute-done), channel_id=1, source_target_pairs={{0,32},{32,64},{64,96},{96,0},{1,33},{33,65},{65,97},{97,1},{2,34}... | collective-permute-start | bytes 1032200 | tf_op jit(solution)/shard_map/ppermute | solution.py:27
  111.4 5.4 %copy-start.2 = (bf16[1,1024,64]{1,2,0:T(8,128)(2,1)}, bf16[1,1024,64]{1,2,0:T(8,128)(2,1)S(1)}, u32[]{:S(2)}) copy-start(bf16[1,1024,64]{1,2,0:T(8,128)(2,1)S(1)} %get-tuple-element.14) | copy-start | bytes 393220
  112.2 25.4 %collective-permute-start.10 = (bf16[2,1024,128]{1,2,0:T(8,128)(2,1)}, bf16[2,1024,128]{1,2,0:T(8,128)(2,1)}, u32[]{:S(2)}, u32[]{:S(2)}) collective-permute-start(bf16[2,1024,128]{1,2,0:T(8,128)(2,1)} %pad_maximum_fusion), channel_id=1, source_target_pairs={{0,16},{16,32},{32,48},{48,64},{64,80},{80,96},{96,112},{1,17},{17... | collective-permute-start | bytes 1572872 | tf_op jit(solution)/shard_map/ppermute | solution.py:21
  118.4 2.3 copy-start.9
  120.4 1.0 copy-start.1
  123.3 14.0 %collective-permute-start.14 = (bf16[16,5376]{1,0:T(8,128)(2,1)S(1)}, bf16[16,5376]{1,0:T(8,128)(2,1)S(1)}, u32[]{:S(2)}, u32[]{:S(2)}) collective-permute-start(bf16[16,5376]{1,0:T(8,128)(2,1)S(1)} %slice.122), channel_id=1, source_target_pairs={{0,32},{32,64},{64,96},{96,0},{1,33},{33,65},{65,97},{97,1},{2,34}... | collective-permute-start | bytes 516104 | tf_op jit(solution)/shard_map/ppermute | solution.py:27
  124.3 13.0 %collective-permute-start.15 = (bf16[16,5376]{1,0:T(8,128)(2,1)S(1)}, bf16[16,5376]{1,0:T(8,128)(2,1)S(1)}, u32[]{:S(2)}, u32[]{:S(2)}) collective-permute-start(bf16[16,5376]{1,0:T(8,128)(2,1)S(1)} %slice.123), channel_id=1, source_target_pairs={{0,96},{32,0},{64,32},{96,64},{1,97},{33,1},{65,33},{97,65},{2,98}... | collective-permute-start | bytes 516104 | tf_op jit(solution)/shard_map/ppermute | solution.py:27
  128.5 8.9 %collective-permute-start.17 = (bf16[16,5376]{1,0:T(8,128)(2,1)S(1)}, bf16[16,5376]{1,0:T(8,128)(2,1)S(1)}, u32[]{:S(2)}, u32[]{:S(2)}) collective-permute-start(bf16[16,5376]{1,0:T(8,128)(2,1)S(1)} %slice.124), channel_id=1, source_target_pairs={{0,32},{32,64},{64,96},{96,0},{1,33},{33,65},{65,97},{97,1},{2,34}... | collective-permute-start | bytes 516104 | tf_op jit(solution)/shard_map/ppermute | solution.py:27
  129.6 7.9 %collective-permute-start.18 = (bf16[16,5376]{1,0:T(8,128)(2,1)S(1)}, bf16[16,5376]{1,0:T(8,128)(2,1)S(1)}, u32[]{:S(2)}, u32[]{:S(2)}) collective-permute-start(bf16[16,5376]{1,0:T(8,128)(2,1)S(1)} %slice.125), channel_id=1, source_target_pairs={{0,96},{32,0},{64,32},{96,64},{1,97},{33,1},{65,33},{97,65},{2,98}... | collective-permute-start | bytes 516104 | tf_op jit(solution)/shard_map/ppermute | solution.py:27
  137.3 0.9 copy-start.3
  154.4 85.1 %copy-start = (bf16[64,5376]{1,0:T(8,128)(2,1)S(1)}, bf16[64,5376]{1,0:T(8,128)(2,1)}, u32[]{:S(2)}) copy-start(bf16[64,5376]{1,0:T(8,128)(2,1)} %param.9) | copy-start | bytes 2064388
  154.4 85.2 %copy-start.7 = (f32[5376]{0:T(1024)S(1)}, f32[5376]{0:T(1024)}, u32[]{:S(2)}) copy-start(f32[5376]{0:T(1024)} %param.17) | copy-start | bytes 64516
Sparse Core Ops, SparseCore 0:
  10.3 82.0 all-gather.1
  154.5 83.5 reduce-scatter.1
